TPU v7x, 512 devices: a whole 4x8x8 slice. The times are simulated.
512 devices in a mesh: lat: 16 (over y, core), lon: 32 (over z, x).
Axes of the slice: x: 4, y: 8, z: 8, core: 2. Of those that a mesh axis runs over, the one named last changes fastest.
Arguments:
- tracers: bfloat16 [1, 512, 1440, 128], P(None, 'lat', 'lon'), may hold values from -6 to 6
- courant: float32 [512, 2, 1440, 128], P('lat', None, 'lon'), may hold values from -0.5 to 0.5
- row_mask: int32 [512], P('lat'), may hold values from 0 to 1, as said below
- damped_modes: int32 [512], P('lat'), may hold values from 180 to 720
- damping: float32 [512, 721], P('lat'), may hold values from 0.05 to 0.8
Outputs:
- advected: bfloat16 [1, 512, 1440, 128], P(None, 'lat', 'lon')
Inputs may be any that keep to these rules, and one draw needn't show every extreme that they name: row_mask is 0 outside the first 128 and the last 128 latitude rows.
All inputs are finite; a program needn't handle non-finite values.
Results may differ from a plain program's by a relative error of at most 0.0052.
Values may be sent and summed in bfloat16 or wider, within the bound.
No kernel may reach another device: no remote copies, remote signals or barrier semaphores. Data moves between devices by JAX's collectives and lax.ppermute only.
A program may use at most 64 MiB of HBM per device.

v0:
```python
import math

import jax
import jax.numpy as jnp
from jax import lax
from jax.sharding import PartitionSpec as P


def padded(value, sides, width, wrap):
    for axis, dim in sides:
        size, length = (lax.axis_size(axis), value.shape[dim])
        up = [(i, (i + 1) % size) for i in range(size if wrap else size - 1)]
        down = [(j, i) for i, j in up]
        last = lax.slice_in_dim(value, length - width, length, axis=dim)
        leading = lax.slice_in_dim(value, 0, width, axis=dim)
        before = lax.ppermute(last, axis, up)
        after = lax.ppermute(leading, axis, down)
        value = jnp.concatenate([before, value, after], axis=dim)
    return value


def take_slice(values, low_end, high_end, along_axis):
    return lax.slice_in_dim(values, low_end, high_end, axis=along_axis)


def ppm_change(extended, courant_faces, along_axis, count_cells):
    edge_values = 7.0 / 12.0 * (
        take_slice(extended, 1, count_cells + 4, along_axis)
        + take_slice(extended, 2, count_cells + 5, along_axis)
    ) - 1.0 / 12.0 * (
        take_slice(extended, 0, count_cells + 3, along_axis)
        + take_slice(extended, 3, count_cells + 6, along_axis)
    )
    left_edge = take_slice(edge_values, 0, count_cells + 2, along_axis)
    right_edge = take_slice(edge_values, 1, count_cells + 3, along_axis)
    centre = take_slice(extended, 2, count_cells + 4, along_axis)
    slope_edge = right_edge - left_edge
    curvature = 6.0 * (centre - 0.5 * (left_edge + right_edge))
    upwind_plus = courant_faces * (
        take_slice(right_edge, 0, count_cells + 1, along_axis)
        - 0.5
        * courant_faces
        * (
            take_slice(slope_edge, 0, count_cells + 1, along_axis)
            - (1.0 - courant_faces * (2.0 / 3.0))
            * take_slice(curvature, 0, count_cells + 1, along_axis)
        )
    )
    upwind_minus = courant_faces * (
        take_slice(left_edge, 1, count_cells + 2, along_axis)
        - 0.5
        * courant_faces
        * (
            take_slice(slope_edge, 1, count_cells + 2, along_axis)
            + (1.0 + courant_faces * (2.0 / 3.0))
            * take_slice(curvature, 1, count_cells + 2, along_axis)
        )
    )
    face_flux = jnp.where(courant_faces > 0, upwind_plus, upwind_minus)
    return take_slice(face_flux, 0, count_cells, along_axis) - take_slice(
        face_flux, 1, count_cells + 1, along_axis
    )


def spectral_basis(blocks, block_len, span, mode_count):
    total_lon = blocks * block_len
    scale = 2.0 * math.pi / total_lon
    mode_index = jnp.arange(mode_count, dtype=jnp.int32)[None, :]
    coarse = jnp.arange(blocks, dtype=jnp.int32)[:, None]
    fine = jnp.arange(span, dtype=jnp.int32)[:, None]
    coarse_angle = ((block_len * coarse * mode_index) % total_lon).astype(jnp.float32) * scale
    fine_angle = ((fine * mode_index) % total_lon).astype(jnp.float32) * scale
    cc, sc = jnp.cos(coarse_angle)[:, None, :], jnp.sin(coarse_angle)[:, None, :]
    cf, sf = jnp.cos(fine_angle)[None], jnp.sin(fine_angle)[None]
    cosine = cc * cf - sc * sf
    sine = sc * cf + cc * sf
    table = jnp.concatenate([cosine, -sine], axis=2)
    mode_weight = (
        jnp.where((mode_index[0] == 0) | (2 * mode_index[0] == total_lon), 1.0, 2.0) / total_lon
    )
    return table, jnp.concatenate([mode_weight, mode_weight], axis=0)


def filter_correction(courant, row_factor):
    row_count, _, lon_local, levels = courant.shape
    blocks = lax.axis_size("lon")
    mode_count = row_factor.shape[1]
    table, mode_weight = spectral_basis(blocks, lon_local, lon_local + 1, mode_count)
    forward_table = table[:, :lon_local].reshape(blocks * lon_local, 2 * mode_count).astype(jnp.bfloat16)
    inverse_table = table.astype(jnp.bfloat16)
    flattened = courant.reshape(2 * row_count, lon_local, levels).astype(jnp.bfloat16)
    pair_factor = jnp.repeat(1.0 - row_factor, 2, axis=0)
    removal = jnp.concatenate([pair_factor, pair_factor], axis=1) * mode_weight[None, :]
    per_device = 2 * row_count // blocks
    level_block = lax.all_to_all(flattened, "lon", split_axis=0, concat_axis=1, tiled=True)
    first_row = lax.axis_index("lon") * per_device
    local_removal = lax.dynamic_slice_in_dim(removal, first_row, per_device, 0)
    spectrum = jnp.einsum(
        "cnl,nm->cml", level_block, forward_table, preferred_element_type=jnp.float32
    )
    weighted = (spectrum * local_removal[:, :, None]).astype(jnp.bfloat16)
    correction = jnp.einsum(
        "cml,djm->dcjl", weighted, inverse_table, preferred_element_type=jnp.float32
    ).astype(jnp.bfloat16)
    returned = lax.all_to_all(correction, "lon", split_axis=0, concat_axis=0, tiled=True)
    return returned.reshape(row_count, 2, lon_local + 1, levels)


def local(tracers, courant, row_mask, damped_modes, damping):
    rows_local = courant.shape[0]
    lon_local = courant.shape[2]
    mode_count = damping.shape[1]
    tracer_count = tracers.shape[0]
    lon_size = lax.axis_size("lon")
    mode_index = jnp.arange(mode_count, dtype=jnp.int32)
    damped = (row_mask[:, None] == 1) & (mode_index[None, :] >= mode_count - damped_modes[:, None])
    factor = jnp.where(damped, damping, 1.0)
    tracer_wide = padded(tracers, (("lon", 2),), 3, True).astype(jnp.float32)
    east_column = lax.ppermute(
        courant[:, 0, 0:1], "lon", [(i, (i - 1) % lon_size) for i in range(lon_size)]
    )
    correction = filter_correction(courant, factor).astype(jnp.float32)
    zonal_courant = jnp.concatenate([courant[:, 0], east_column], axis=1)
    zonal_faces = (zonal_courant - correction[:, 0]).astype(jnp.bfloat16)
    meridional_filtered = (courant[:, 1] - correction[:, 1, :lon_local]).astype(jnp.bfloat16)
    middle = (
        tracers.astype(jnp.float32)
        + ppm_change(tracer_wide, zonal_faces.astype(jnp.float32)[None], 2, lon_local)
    ).astype(jnp.bfloat16)
    meridional_stack = jnp.concatenate([middle, meridional_filtered[None]], axis=0)
    meridional_band = padded(meridional_stack, (("lat", 1),), 3, False)
    middle_wide = meridional_band[:tracer_count].astype(jnp.float32)
    meridional_faces = meridional_band[tracer_count, 3 : rows_local + 4].astype(jnp.float32)
    face_rows = lax.axis_index("lat") * rows_local + jnp.arange(rows_local + 1, dtype=jnp.int32)
    meridional_faces = jnp.where(face_rows[:, None, None] > 0, meridional_faces, 0.0)
    return (
        middle.astype(jnp.float32) + ppm_change(middle_wide, meridional_faces[None], 1, rows_local)
    ).astype(jnp.bfloat16)


def solution(mesh):
    placed = (
        P(None, "lat", "lon", None),
        P("lat", None, "lon", None),
        P("lat"),
        P("lat"),
        P("lat", None),
    )
    return jax.shard_map(
        local, mesh=mesh, in_specs=placed, out_specs=P(None, "lat", "lon", None), check_vma=False
    )
```

profile of v0, /device:TPU:32, one launch (start us, length us, event | category | flops | bytes accessed | tf_op | source)
XLA Modules:
  0.0 87.5 jit_solution(14624698446690196999)
XLA Ops:
  0.0 0.0 copy-start.5
  0.0 0.0 copy-start.6
  0.0 0.0 copy-start.4
  0.0 1.9 %convert_element_type.150 = bf16[32,2,45,128]{3,1,2,0:T(2,128)(2,1)S(1)} convert(f32[32,2,45,128]{3,1,2,0:T(2,128)} %param.6) | non-fusion elementwise | flops 368640 | bytes 2211840 | tf_op jit(solution)/shard_map/convert_element_type | solution.py:91
  1.9 0.8 copy.38
  2.7 1.4 %copy.39 = bf16[64,45,128]{2,1,0:T(8,128)(2,1)} copy(bf16[64,45,128]{2,0,1:T(8,128)(2,1)S(1)} %bitcast.59) | data formatting | bytes 1474560 | tf_op jit(solution)/shard_map/convert_element_type | solution.py:91
  4.1 13.2 %all-to-all-start = ((bf16[64,45,128]{2,1,0:T(8,128)(2,1)}), bf16[64,45,128]{2,1,0:T(8,128)(2,1)S(1)}, u32[]{:S(2)}, u32[]{:S(2)}) async-start(bf16[64,45,128]{2,1,0:T(8,128)(2,1)} %copy.39), calls=%async_computation | async-start | bytes 1572864 | tf_op jit(solution)/shard_map/all_to_all | solution.py:95
  17.3 0.6 fusion.57
  17.9 0.0 copy-done.5
  17.9 0.0 copy-done.6
  18.0 0.1 pad_maximum_fusion.7
  18.0 0.0 copy-done.4
  18.0 0.1 select_subtract_fusion
  18.2 0.1 broadcast_in_dim.20
  18.2 0.1 reshape.291
  18.4 0.5 fusion.65
  18.9 1.6 %multiply_subtract_fusion = (bf16[32,46,721]{2,1,0:T(8,128)(2,1)S(1)}, bf16[32,46,721]{2,1,0:T(8,128)(2,1)S(1)}) fusion(f32[46,721]{1,0:T(8,128)S(1)} %get-tuple-element.19, f32[32,721]{1,0:T(8,128)S(1)} %get-tuple-element.18, f32[46,721]{1,0:T(8,128)S(1)} %get-tuple-element.20, f32[32,721]{1,0:T(8,128)S(1)} %get-tuple-element.17), kind=kLoop, calls=%fused_computation.6 | loop fusion | flops 9551808 | bytes 4695152 | tf_op jit(solution)/shard_map/sub | solution.py:75
  20.5 3.9 %maximum_convert_fusion = bf16[32,46,1442]{2,1,0:T(8,128)(2,1)} fusion(bf16[32,46,721]{2,1,0:T(8,128)(2,1)S(1)} %get-tuple-element.14, bf16[32,46,721]{2,1,0:T(8,128)(2,1)S(1)} %get-tuple-element.13), kind=kLoop, calls=%fused_computation | loop fusion | flops 8490496 | bytes 8490496 | tf_op jit(solution)/shard_map/convert_element_type | solution.py:90
  24.4 0.1 fusion.69
  24.4 15.7 %all-to-all-done = bf16[64,45,128]{2,1,0:T(8,128)(2,1)S(1)} async-done(((bf16[64,45,128]{2,1,0:T(8,128)(2,1)}), bf16[64,45,128]{2,1,0:T(8,128)(2,1)S(1)}, u32[]{:S(2)}, u32[]{:S(2)}) %all-to-all-start) | async-done | bytes 737312 | tf_op jit(solution)/shard_map/all_to_all | solution.py:95
  40.2 0.0 copy-start.1
  40.2 4.2 %fusion.6 = bf16[2,1442,128,1]{2,1,0,3:T(8,128)(2,1)S(1)} fusion(bf16[32,46,1442]{2,1,0:T(8,128)(2,1)} %maximum_convert_fusion, bf16[32,2,45,128]{3,2,1,0:T(8,128)(2,1)S(1)} %bitcast.60, f32[2,1442]{1,0:T(2,128)S(1)} %fusion.69), kind=kOutput, calls=%fused_computation.10 | convolution fusion | flops 1063896064 | bytes 5732368 | tf_op jit(solution)/shard_map/cnl,nm->cml/dot_general | solution.py:98
  44.3 0.0 copy-done.1
  44.4 0.0 copy-start.3
  44.4 0.0 copy-start
  44.4 1.4 %fusion.10 = bf16[32,2,46,128]{3,2,1,0:T(8,128)(2,1)S(1)} fusion(bf16[2,1442,128,1]{2,1,0,3:T(8,128)(2,1)S(1)} %fusion.6, bf16[32,46,1442]{2,1,0:T(8,128)(2,1)S(1)} %copy-done.1), kind=kOutput, calls=%fused_computation.17 | convolution fusion | flops 1087160320 | bytes 5737216 | tf_op jit(solution)/shard_map/cml,djm->dcjl/dot_general | solution.py:102
  45.8 1.4 %copy.42 = bf16[32,2,46,128]{3,1,2,0:T(2,128)(2,1)} copy(bf16[32,2,46,128]{3,2,1,0:T(8,128)(2,1)S(1)} %fusion.10) | data formatting | bytes 1507328 | tf_op jit(solution)/shard_map/convert_element_type | solution.py:104
  47.3 5.1 %all-to-all-start.1 = ((bf16[32,2,46,128]{3,1,2,0:T(2,128)(2,1)}), bf16[32,2,46,128]{3,1,2,0:T(2,128)(2,1)S(1)}, u32[]{:S(2)}, u32[]{:S(2)}) async-start(bf16[32,2,46,128]{3,1,2,0:T(2,128)(2,1)} %copy.42), calls=%async_computation.1 | async-start | bytes 1507328 | tf_op jit(solution)/shard_map/all_to_all | solution.py:105
  52.4 0.0 copy-done.3
  52.4 3.7 %collective-permute-start.1 = (bf16[1,32,3,128]{3,1,2,0:T(8,128)(2,1)S(1)}, bf16[1,32,3,128]{3,1,2,0:T(8,128)(2,1)S(1)}, u32[]{:S(2)}, u32[]{:S(2)}) collective-permute-start(bf16[1,32,3,128]{3,1,2,0:T(8,128)(2,1)S(1)} %get-tuple-element.15), channel_id=1, source_target_pairs={{0,1},{1,2},{2,3},{3,4},{4,5},{5,6},{6,7},{7,8},{8,9},{9,10},{10,1... | collective-permute-start | bytes 73736 | tf_op jit(solution)/shard_map/ppermute | solution.py:16
  56.1 5.5 %collective-permute-start.2 = (bf16[1,32,3,128]{3,1,2,0:T(8,128)(2,1)S(1)}, bf16[1,32,3,128]{3,1,2,0:T(8,128)(2,1)S(1)}, u32[]{:S(2)}, u32[]{:S(2)}) collective-permute-start(bf16[1,32,3,128]{3,1,2,0:T(8,128)(2,1)S(1)} %get-tuple-element.16), channel_id=1, source_target_pairs={{1,0},{2,1},{3,2},{4,3},{5,4},{6,5},{7,6},{8,7},{9,8},{10,9},{11,1... | collective-permute-start | bytes 73736 | tf_op jit(solution)/shard_map/ppermute | solution.py:17
  61.6 0.0 copy-done
  61.7 4.0 %collective-permute-start = (f32[32,1,128]{2,0,1:T(8,128)S(1)}, f32[32,1,128]{2,0,1:T(8,128)S(1)}, u32[]{:S(2)}, u32[]{:S(2)}) collective-permute-start(f32[32,1,128]{2,0,1:T(8,128)S(1)} %bitcast.62), channel_id=1, source_target_pairs={{0,31},{1,0},{2,1},{3,2},{4,3},{5,4},{6,5},{7,6},{8,7},{9,8},{10,9... | collective-permute-start | bytes 49160 | tf_op jit(solution)/shard_map/ppermute | solution.py:119
  65.6 2.0 %fusion.72 = (f32[32,1,45,128]{3,1,2,0:T(1,128)S(1)}, f32[32,1,45,128]{3,1,2,0:T(1,128)}) fusion(f32[32,2,45,128]{3,1,2,0:T(2,128)S(1)} %copy-done), kind=kLoop, calls=%fused_computation.118 | loop fusion | bytes 2949120 | tf_op jit(solution)/shard_map/slice | solution.py:123
  67.7 1.0 %copy.61 = f32[32,1,45,128]{3,0,2,1:T(8,128)} copy(f32[32,1,45,128]{3,1,2,0:T(1,128)S(1)} %get-tuple-element.5) | data formatting | bytes 1474560
  68.6 3.2 %collective-permute-done.1 = bf16[1,32,3,128]{3,1,2,0:T(8,128)(2,1)S(1)} collective-permute-done((bf16[1,32,3,128]{3,1,2,0:T(8,128)(2,1)S(1)}, bf16[1,32,3,128]{3,1,2,0:T(8,128)(2,1)S(1)}, u32[]{:S(2)}, u32[]{:S(2)}) %collective-permute-start.1) | collective-permute-done | bytes 24608 | tf_op jit(solution)/shard_map/ppermute | solution.py:16
  71.9 0.0 collective-permute-done.2
  71.9 0.1 maximum_convert_fusion.1
  71.9 0.1 fusion.32
  72.1 0.2 slice_subtract_fusion.6
  72.3 1.3 %all-to-all-done.1 = bf16[32,2,46,128]{3,1,2,0:T(2,128)(2,1)S(1)} async-done(((bf16[32,2,46,128]{3,1,2,0:T(2,128)(2,1)}), bf16[32,2,46,128]{3,1,2,0:T(2,128)(2,1)S(1)}, u32[]{:S(2)}, u32[]{:S(2)}) %all-to-all-start.1) | async-done | bytes 753696 | tf_op jit(solution)/shard_map/all_to_all | solution.py:105
  73.6 0.0 copy-start.2
  73.6 0.2 copy_convert_fusion
  73.8 0.0 collective-permute-done
  73.8 1.6 %fusion.43 = f32[1,32,46,128]{3,1,2,0:T(8,128)S(1)} fusion(f32[1,32,47,128]{3,1,2,0:T(8,128)S(1)} %get-tuple-element.10, f32[1,32,47,128]{3,1,2,0:T(8,128)S(1)} %get-tuple-element.9, f32[1,32,48,128]{3,1,2,0:T(8,128)S(1)} %fusion.32, f32[32,2,46,128]{3,0,2,1:T(8,128)S(1)} %copy_convert_fusion, f32[1,32,1,128]{3,1,2,0:T(8,128)S(1)} %bitcast.61, ...), kind=kLoop, calls=%fused_computation.58 | loop fusion | flops 3768320 | bytes 6029312 | tf_op jit(solution)/shard_map/jit(_where)/select_n | solution.py:59
  75.4 0.1 fusion.50
  75.6 0.0 copy-done.2
  75.6 0.1 fusion.52
  75.7 0.1 pad_maximum_fusion.5
  75.8 1.9 %collective-permute-start.3 = (bf16[2,3,45,128]{3,1,2,0:T(4,128)(2,1)S(1)}, bf16[2,3,45,128]{3,1,2,0:T(4,128)(2,1)S(1)}, u32[]{:S(2)}, u32[]{:S(2)}) collective-permute-start(bf16[2,3,45,128]{3,1,2,0:T(4,128)(2,1)S(1)} %get-tuple-element.12), channel_id=1, source_target_pairs={{32,0},{64,32},{96,64},{128,96},{160,128},{192,160},{224,192},{256... | collective-permute-start | bytes 207368 | tf_op jit(solution)/shard_map/ppermute | solution.py:17
  77.7 2.4 %collective-permute-start.4 = (bf16[2,3,45,128]{3,1,2,0:T(4,128)(2,1)S(1)}, bf16[2,3,45,128]{3,1,2,0:T(4,128)(2,1)S(1)}, u32[]{:S(2)}, u32[]{:S(2)}) collective-permute-start(bf16[2,3,45,128]{3,1,2,0:T(4,128)(2,1)S(1)} %get-tuple-element.11), channel_id=1, source_target_pairs={{0,32},{32,64},{64,96},{96,128},{128,160},{160,192},{192,224},{224... | collective-permute-start | bytes 207368 | tf_op jit(solution)/shard_map/ppermute | solution.py:16
  80.2 0.0 collective-permute-done.3
  80.2 4.6 %collective-permute-done.4 = bf16[2,3,45,128]{3,1,2,0:T(4,128)(2,1)S(1)} collective-permute-done((bf16[2,3,45,128]{3,1,2,0:T(4,128)(2,1)S(1)}, bf16[2,3,45,128]{3,1,2,0:T(4,128)(2,1)S(1)}, u32[]{:S(2)}, u32[]{:S(2)}) %collective-permute-start.4) | collective-permute-done | bytes 69152 | tf_op jit(solution)/shard_map/ppermute | solution.py:16
  84.8 0.2 fusion.51
  85.0 0.3 fusion.24
  85.3 0.3 slice_subtract_fusion.1
  85.7 0.9 fusion.17
  86.5 0.9 %fusion.47 = bf16[1,32,45,128]{3,1,2,0:T(8,128)(2,1)} fusion(f32[1,33,45,128]{3,1,2,0:T(8,128)S(1)} %fusion.17, bf16[1,32,45,128]{3,1,2,0:T(8,128)(2,1)S(1)} %fusion.50), kind=kLoop, calls=%fused_computation.65 | loop fusion | flops 737280 | bytes 2211840 | tf_op jit(solution)/shard_map/convert_element_type | solution.py:138
  (7 shorter events, 0.0 us)
Async XLA Ops:
  0.0 17.9 %copy-start.5 = (s32[32]{0:T(128)S(1)}, s32[32]{0:T(128)}, u32[]{:S(2)}) copy-start(s32[32]{0:T(128)} %param.7) | copy-start | bytes 388
  0.0 17.9 %copy-start.6 = (s32[32]{0:T(128)S(1)}, s32[32]{0:T(128)}, u32[]{:S(2)}) copy-start(s32[32]{0:T(128)} %param.8) | copy-start | bytes 388
  0.0 18.0 %copy-start.4 = (f32[32,721]{1,0:T(8,128)S(1)}, f32[32,721]{1,0:T(8,128)}, u32[]{:S(2)}) copy-start(f32[32,721]{1,0:T(8,128)} %param.9) | copy-start | bytes 276868
  4.1 36.1 %all-to-all-start = ((bf16[64,45,128]{2,1,0:T(8,128)(2,1)}), bf16[64,45,128]{2,1,0:T(8,128)(2,1)S(1)}, u32[]{:S(2)}, u32[]{:S(2)}) async-start(bf16[64,45,128]{2,1,0:T(8,128)(2,1)} %copy.39), calls=%async_computation | async-start | bytes 1572864 | tf_op jit(solution)/shard_map/all_to_all | solution.py:95
  40.2 4.2 %copy-start.1 = (bf16[32,46,1442]{2,1,0:T(8,128)(2,1)S(1)}, bf16[32,46,1442]{2,1,0:T(8,128)(2,1)}, u32[]{:S(2)}) copy-start(bf16[32,46,1442]{2,1,0:T(8,128)(2,1)} %maximum_convert_fusion) | copy-start | bytes 12735748
  44.4 8.1 %copy-start.3 = (bf16[1,32,45,128]{3,1,2,0:T(8,128)(2,1)S(1)}, bf16[1,32,45,128]{3,1,2,0:T(8,128)(2,1)}, u32[]{:S(2)}) copy-start(bf16[1,32,45,128]{3,1,2,0:T(8,128)(2,1)} %param.5) | copy-start | bytes 1105924
  44.4 17.3 %copy-start = (f32[32,2,45,128]{3,1,2,0:T(2,128)S(1)}, f32[32,2,45,128]{3,1,2,0:T(2,128)}, u32[]{:S(2)}) copy-start(f32[32,2,45,128]{3,1,2,0:T(2,128)} %param.6) | copy-start | bytes 4423684
  47.3 26.3 %all-to-all-start.1 = ((bf16[32,2,46,128]{3,1,2,0:T(2,128)(2,1)}), bf16[32,2,46,128]{3,1,2,0:T(2,128)(2,1)S(1)}, u32[]{:S(2)}, u32[]{:S(2)}) async-start(bf16[32,2,46,128]{3,1,2,0:T(2,128)(2,1)} %copy.42), calls=%async_computation.1 | async-start | bytes 1507328 | tf_op jit(solution)/shard_map/all_to_all | solution.py:105
  52.4 19.4 %collective-permute-start.1 = (bf16[1,32,3,128]{3,1,2,0:T(8,128)(2,1)S(1)}, bf16[1,32,3,128]{3,1,2,0:T(8,128)(2,1)S(1)}, u32[]{:S(2)}, u32[]{:S(2)}) collective-permute-start(bf16[1,32,3,128]{3,1,2,0:T(8,128)(2,1)S(1)} %get-tuple-element.15), channel_id=1, source_target_pairs={{0,1},{1,2},{2,3},{3,4},{4,5},{5,6},{6,7},{7,8},{8,9},{9,10},{10,1... | collective-permute-start | bytes 73736 | tf_op jit(solution)/shard_map/ppermute | solution.py:16
  56.1 15.7 %collective-permute-start.2 = (bf16[1,32,3,128]{3,1,2,0:T(8,128)(2,1)S(1)}, bf16[1,32,3,128]{3,1,2,0:T(8,128)(2,1)S(1)}, u32[]{:S(2)}, u32[]{:S(2)}) collective-permute-start(bf16[1,32,3,128]{3,1,2,0:T(8,128)(2,1)S(1)} %get-tuple-element.16), channel_id=1, source_target_pairs={{1,0},{2,1},{3,2},{4,3},{5,4},{6,5},{7,6},{8,7},{9,8},{10,9},{11,1... | collective-permute-start | bytes 73736 | tf_op jit(solution)/shard_map/ppermute | solution.py:17
  61.7 12.2 %collective-permute-start = (f32[32,1,128]{2,0,1:T(8,128)S(1)}, f32[32,1,128]{2,0,1:T(8,128)S(1)}, u32[]{:S(2)}, u32[]{:S(2)}) collective-permute-start(f32[32,1,128]{2,0,1:T(8,128)S(1)} %bitcast.62), channel_id=1, source_target_pairs={{0,31},{1,0},{2,1},{3,2},{4,3},{5,4},{6,5},{7,6},{8,7},{9,8},{10,9... | collective-permute-start | bytes 49160 | tf_op jit(solution)/shard_map/ppermute | solution.py:119
  73.6 2.0 %copy-start.2 = (f32[32,1,45,128]{3,1,2,0:T(1,128)S(1)}, f32[32,1,45,128]{3,1,2,0:T(1,128)}, u32[]{:S(2)}) copy-start(f32[32,1,45,128]{3,1,2,0:T(1,128)} %get-tuple-element.6) | copy-start | bytes 2211844
  75.8 4.4 %collective-permute-start.3 = (bf16[2,3,45,128]{3,1,2,0:T(4,128)(2,1)S(1)}, bf16[2,3,45,128]{3,1,2,0:T(4,128)(2,1)S(1)}, u32[]{:S(2)}, u32[]{:S(2)}) collective-permute-start(bf16[2,3,45,128]{3,1,2,0:T(4,128)(2,1)S(1)} %get-tuple-element.12), channel_id=1, source_target_pairs={{32,0},{64,32},{96,64},{128,96},{160,128},{192,160},{224,192},{256... | collective-permute-start | bytes 207368 | tf_op jit(solution)/shard_map/ppermute | solution.py:17
  77.7 7.1 %collective-permute-start.4 = (bf16[2,3,45,128]{3,1,2,0:T(4,128)(2,1)S(1)}, bf16[2,3,45,128]{3,1,2,0:T(4,128)(2,1)S(1)}, u32[]{:S(2)}, u32[]{:S(2)}) collective-permute-start(bf16[2,3,45,128]{3,1,2,0:T(4,128)(2,1)S(1)} %get-tuple-element.11), channel_id=1, source_target_pairs={{0,32},{32,64},{64,96},{96,128},{128,160},{160,192},{192,224},{224... | collective-permute-start | bytes 207368 | tf_op jit(solution)/shard_map/ppermute | solution.py:16
where the time goes:
time: 87.9 us; the launch traced here: 87.5 us
  starting transfers between devices  35.8 us (41%)
  waiting for transfers between devices  24.9 us (28%)
  other arithmetic  14 us (16%)
  local copies, waits for them, and re-layouts  6.87 us (8%)
  matrix products  5.61 us (6%)
    all_to_all x1, waiting for transfers between devices, filter_correction(): lax.all_to_all(flattened, 'lon', split_axis=0, concat_axis=1, tiled=True)  15.7 us
    all_to_all x1, starting transfers between devices, filter_correction(): lax.all_to_all(flattened, 'lon', split_axis=0, concat_axis=1, tiled=True)  13.2 us
    ppermute x2, waiting for transfers between devices, padded(): before = lax.ppermute(last, axis, up)  7.87 us
    ppermute x2, starting transfers between devices, padded(): after = lax.ppermute(leading, axis, down)  7.39 us
    ppermute x2, starting transfers between devices, padded(): before = lax.ppermute(last, axis, up)  6.1 us
    all_to_all x1, starting transfers between devices, filter_correction(): lax.all_to_all(correction, 'lon', split_axis=0, concat_axis=0, tiled=True)  5.13 us
    dot_general x1, matrix products, filter_correction(): jnp.einsum('cnl,nm->cml', level_block, forward_table, preferred_element_t...  4.17 us
    ppermute x1, starting transfers between devices, local(): lax.ppermute(courant[:, 0, 0:1], 'lon', [(i, (i - 1) % lon_size) for i in...  3.97 us
  transfers between devices with their start and end apart: 7, of which 4 were waited for; matrix products, arithmetic and copies ran while one was open for 12% of the time, Pallas kernels for 0%

commit v1 on v0

--- a/solution.py
+++ b/solution.py
@@ -85,25 +85,31 @@
     row_count, _, lon_local, levels = courant.shape
     blocks = lax.axis_size("lon")
     mode_count = row_factor.shape[1]
+    per_device = 2 * row_count // blocks
     table, mode_weight = spectral_basis(blocks, lon_local, lon_local + 1, mode_count)
-    forward_table = table[:, :lon_local].reshape(blocks * lon_local, 2 * mode_count).astype(jnp.bfloat16)
+    forward_table = table[:, :lon_local].astype(jnp.bfloat16)
     inverse_table = table.astype(jnp.bfloat16)
-    flattened = courant.reshape(2 * row_count, lon_local, levels).astype(jnp.bfloat16)
+    outgoing = courant.transpose(0, 2, 1, 3).astype(jnp.bfloat16)
+    outgoing = outgoing.reshape(blocks, (2 * row_count // blocks) * lon_local, levels)
     pair_factor = jnp.repeat(1.0 - row_factor, 2, axis=0)
     removal = jnp.concatenate([pair_factor, pair_factor], axis=1) * mode_weight[None, :]
-    per_device = 2 * row_count // blocks
-    level_block = lax.all_to_all(flattened, "lon", split_axis=0, concat_axis=1, tiled=True)
+    arrived = lax.all_to_all(outgoing, "lon", split_axis=0, concat_axis=0, tiled=True)
+    level_block = arrived.reshape(blocks, per_device // 2, lon_local, 2, levels)
     first_row = lax.axis_index("lon") * per_device
     local_removal = lax.dynamic_slice_in_dim(removal, first_row, per_device, 0)
     spectrum = jnp.einsum(
-        "cnl,nm->cml", level_block, forward_table, preferred_element_type=jnp.float32
-    )
+        "drjcl,djm->rcml", level_block, forward_table, preferred_element_type=jnp.float32
+    ).reshape(per_device, 2 * mode_count, levels)
     weighted = (spectrum * local_removal[:, :, None]).astype(jnp.bfloat16)
     correction = jnp.einsum(
-        "cml,djm->dcjl", weighted, inverse_table, preferred_element_type=jnp.float32
+        "rcml,djm->drjcl",
+        weighted.reshape(per_device // 2, 2, 2 * mode_count, levels),
+        inverse_table,
+        preferred_element_type=jnp.float32,
     ).astype(jnp.bfloat16)
+    correction = correction.reshape(blocks, per_device * (lon_local + 1), levels)
     returned = lax.all_to_all(correction, "lon", split_axis=0, concat_axis=0, tiled=True)
-    return returned.reshape(row_count, 2, lon_local + 1, levels)
+    return returned.reshape(row_count, lon_local + 1, 2, levels)
 
 
 def local(tracers, courant, row_mask, damped_modes, damping):
@@ -121,8 +127,8 @@
     )
     correction = filter_correction(courant, factor).astype(jnp.float32)
     zonal_courant = jnp.concatenate([courant[:, 0], east_column], axis=1)
-    zonal_faces = (zonal_courant - correction[:, 0]).astype(jnp.bfloat16)
-    meridional_filtered = (courant[:, 1] - correction[:, 1, :lon_local]).astype(jnp.bfloat16)
+    zonal_faces = (zonal_courant - correction[:, :, 0]).astype(jnp.bfloat16)
+    meridional_filtered = (courant[:, 1] - correction[:, :lon_local, 1]).astype(jnp.bfloat16)
     middle = (
         tracers.astype(jnp.float32)
         + ppm_change(tracer_wide, zonal_faces.astype(jnp.float32)[None], 2, lon_local)

time: 87.9 us -> 88.1 us (level)
  other arithmetic: 14 us -> 12 us
  local copies, waits for them, and re-layouts: 6.87 us -> 8.14 us
    convert_element_type x3 -> x1, local copies, waits for them, and re-layouts: 3.62 us -> 0.29 us  [filter_correction(): correction = jnp.einsum('rcml,djm->drjcl', weighted.reshape(per_device //...]
    reshape x0 -> x2, local copies, waits for them, and re-layouts: none -> 2.39 us  [the longest x1 1.21 us: filter_correction(): outgoing.reshape(blocks, 2 * row_count // blocks * lon_local, levels)]
    convert_element_type x2 -> x1, other arithmetic: 2.05 us -> 0.13 us  [local(): (courant[:, 1] - correction[:, :lon_local, 1]).astype(jnp.bfloat16)]
    unnamed x15 -> x18, local copies, waits for them, and re-layouts: 1 us -> 2.6 us
  transfers between devices with their start and end apart: 7 -> 7, of which waited for: 4 -> 4; matrix products, arithmetic and copies ran while one was open for 12% -> 13% of each run, Pallas kernels for 0% -> 0%
where the time goes in v1:
time: 88.1 us; the launch traced here: 87.7 us
  starting transfers between devices  35.8 us (41%)
  waiting for transfers between devices  25.5 us (29%)
  other arithmetic  12 us (14%)
  local copies, waits for them, and re-layouts  8.14 us (9%)
  matrix products  5.84 us (7%)
    all_to_all x1, waiting for transfers between devices, filter_correction(): lax.all_to_all(outgoing, 'lon', split_axis=0, concat_axis=0, tiled=True)  15.7 us
    all_to_all x1, starting transfers between devices, filter_correction(): lax.all_to_all(outgoing, 'lon', split_axis=0, concat_axis=0, tiled=True)  13.2 us
    ppermute x2, waiting for transfers between devices, padded(): before = lax.ppermute(last, axis, up)  8.59 us
    ppermute x2, starting transfers between devices, padded(): after = lax.ppermute(leading, axis, down)  7.39 us
    ppermute x2, starting transfers between devices, padded(): before = lax.ppermute(last, axis, up)  6.1 us
    all_to_all x1, starting transfers between devices, filter_correction(): lax.all_to_all(correction, 'lon', split_axis=0, concat_axis=0, tiled=True)  5.13 us
    dot_general x1, matrix products, filter_correction(): jnp.einsum('drjcl,djm->rcml', level_block, forward_table, preferred_eleme...  4.39 us
    ppermute x1, starting transfers between devices, local(): lax.ppermute(courant[:, 0, 0:1], 'lon', [(i, (i - 1) % lon_size) for i in...  3.97 us
  transfers between devices with their start and end apart: 7, of which 4 were waited for; matrix products, arithmetic and copies ran while one was open for 13% of the time, Pallas kernels for 0%

profile of v1, /device:TPU:32, one launch (start us, length us, event | category | flops | bytes accessed | tf_op | source)
XLA Modules:
  0.0 87.7 jit_solution(12664591957132486584)
XLA Ops:
  0.0 0.0 copy-start.4
  0.0 0.0 copy-start.5
  0.0 0.0 copy-start.3
  0.0 1.6 %copy.40 = bf16[32,2,45,128]{3,0,1,2:T(8,128)(2,1)S(1)} copy(f32[32,2,45,128]{3,1,2,0:T(2,128)} %param.6) | data formatting | bytes 2211840 | tf_op args[1]
  1.6 1.2 %copy.19 = bf16[32,90,128]{2,1,0:T(8,128)(2,1)} copy(bf16[32,90,128]{2,0,1:T(8,128)(2,1)S(1)} %bitcast.73) | data formatting | bytes 1474560 | tf_op jit(solution)/shard_map/reshape | solution.py:93
  2.8 13.2 %all-to-all-start = ((bf16[32,90,128]{2,1,0:T(8,128)(2,1)}), bf16[32,90,128]{2,1,0:T(8,128)(2,1)S(1)}, u32[]{:S(2)}, u32[]{:S(2)}) async-start(bf16[32,90,128]{2,1,0:T(8,128)(2,1)} %copy.19), calls=%async_computation | async-start | bytes 1572864 | tf_op jit(solution)/shard_map/all_to_all | solution.py:96
  16.0 0.6 fusion.53
  16.6 0.0 copy-done.4
  16.7 0.0 copy-done.5
  16.7 0.1 pad_maximum_fusion.7
  16.8 0.0 copy-done.3
  16.8 0.1 select_subtract_fusion
  16.9 0.1 broadcast_in_dim.20
  17.0 0.1 reshape.311
  17.1 0.5 fusion.61
  17.6 1.6 %multiply_subtract_fusion = (bf16[32,46,721]{2,1,0:T(8,128)(2,1)S(1)}, bf16[32,46,721]{2,1,0:T(8,128)(2,1)S(1)}) fusion(f32[46,721]{1,0:T(8,128)S(1)} %get-tuple-element.19, f32[32,721]{1,0:T(8,128)S(1)} %get-tuple-element.18, f32[46,721]{1,0:T(8,128)S(1)} %get-tuple-element.20, f32[32,721]{1,0:T(8,128)S(1)} %get-tuple-element.17), kind=kLoop, calls=%fused_computation.6 | loop fusion | flops 9551808 | bytes 4695152 | tf_op jit(solution)/shard_map/sub | solution.py:75
  19.2 3.9 %maximum_convert_fusion = bf16[32,46,1442]{2,1,0:T(8,128)(2,1)} fusion(bf16[32,46,721]{2,1,0:T(8,128)(2,1)S(1)} %get-tuple-element.14, bf16[32,46,721]{2,1,0:T(8,128)(2,1)S(1)} %get-tuple-element.13), kind=kLoop, calls=%fused_computation | loop fusion | flops 8490496 | bytes 8490496 | tf_op jit(solution)/shard_map/convert_element_type | solution.py:91
  23.1 0.1 fusion.65
  23.2 15.7 %all-to-all-done = bf16[32,90,128]{2,1,0:T(8,128)(2,1)S(1)} async-done(((bf16[32,90,128]{2,1,0:T(8,128)(2,1)}), bf16[32,90,128]{2,1,0:T(8,128)(2,1)S(1)}, u32[]{:S(2)}, u32[]{:S(2)}) %all-to-all-start) | async-done | bytes 737312 | tf_op jit(solution)/shard_map/all_to_all | solution.py:96
  38.9 0.0 slice-start
  38.9 0.3 copy.20
  39.2 0.0 slice-start.1
  39.2 4.4 %fusion.6 = bf16[2,1442,128,1]{2,1,0,3:T(8,128)(2,1)S(1)} fusion(bf16[32,46,1442]{2,1,0:T(8,128)(2,1)} %maximum_convert_fusion, bf16[32,45,2,128]{3,0,2,1:T(8,128)(2,1)S(1)} %bitcast.74, f32[2,1442]{1,0:T(2,128)S(1)} %fusion.65), kind=kOutput, calls=%fused_computation.10 | convolution fusion | flops 1063896064 | bytes 5732368 | tf_op jit(solution)/shard_map/drjcl,djm->rcml/dot_general | solution.py:100
  43.6 0.0 slice-done
  43.6 0.0 slice-done.1
  43.6 0.0 copy-start.2
  43.6 1.4 %fusion.7 = bf16[32,46,2,128]{3,1,2,0:T(8,128)(2,1)S(1)} fusion(bf16[2,1442,128,1]{2,1,0,3:T(8,128)(2,1)S(1)} %fusion.6, bf16[32,46,1442]{2,1,0:T(8,128)(2,1)S(1)} %bitcast.69), kind=kOutput, calls=%fused_computation.17 | convolution fusion | flops 1087160320 | bytes 5737216 | tf_op jit(solution)/shard_map/rcml,djm->drjcl/dot_general | solution.py:104
  45.1 0.0 copy-start
  45.1 0.3 copy.22
  45.4 1.2 %copy.23 = bf16[32,92,128]{2,1,0:T(8,128)(2,1)} copy(bf16[32,92,128]{2,0,1:T(8,128)(2,1)S(1)} %bitcast.70) | data formatting | bytes 1507328 | tf_op jit(solution)/shard_map/reshape | solution.py:110
  46.6 5.1 %all-to-all-start.1 = ((bf16[32,92,128]{2,1,0:T(8,128)(2,1)}), bf16[32,92,128]{2,1,0:T(8,128)(2,1)S(1)}, u32[]{:S(2)}, u32[]{:S(2)}) async-start(bf16[32,92,128]{2,1,0:T(8,128)(2,1)} %copy.23), calls=%async_computation.1 | async-start | bytes 1572864 | tf_op jit(solution)/shard_map/all_to_all | solution.py:111
  51.7 0.0 copy-done.2
  51.7 3.7 %collective-permute-start.1 = (bf16[1,32,3,128]{3,1,2,0:T(8,128)(2,1)S(1)}, bf16[1,32,3,128]{3,1,2,0:T(8,128)(2,1)S(1)}, u32[]{:S(2)}, u32[]{:S(2)}) collective-permute-start(bf16[1,32,3,128]{3,1,2,0:T(8,128)(2,1)S(1)} %get-tuple-element.15), channel_id=1, source_target_pairs={{0,1},{1,2},{2,3},{3,4},{4,5},{5,6},{6,7},{7,8},{8,9},{9,10},{10,1... | collective-permute-start | bytes 73736 | tf_op jit(solution)/shard_map/ppermute | solution.py:16
  55.5 5.5 %collective-permute-start.2 = (bf16[1,32,3,128]{3,1,2,0:T(8,128)(2,1)S(1)}, bf16[1,32,3,128]{3,1,2,0:T(8,128)(2,1)S(1)}, u32[]{:S(2)}, u32[]{:S(2)}) collective-permute-start(bf16[1,32,3,128]{3,1,2,0:T(8,128)(2,1)S(1)} %get-tuple-element.16), channel_id=1, source_target_pairs={{1,0},{2,1},{3,2},{4,3},{5,4},{6,5},{7,6},{8,7},{9,8},{10,9},{11,1... | collective-permute-start | bytes 73736 | tf_op jit(solution)/shard_map/ppermute | solution.py:17
  60.9 0.0 copy-done
  61.0 4.0 %collective-permute-start = (f32[32,1,128]{2,0,1:T(8,128)S(1)}, f32[32,1,128]{2,0,1:T(8,128)S(1)}, u32[]{:S(2)}, u32[]{:S(2)}) collective-permute-start(f32[32,1,128]{2,0,1:T(8,128)S(1)} %bitcast.76), channel_id=1, source_target_pairs={{0,31},{1,0},{2,1},{3,2},{4,3},{5,4},{6,5},{7,6},{8,7},{9,8},{10,9... | collective-permute-start | bytes 49160 | tf_op jit(solution)/shard_map/ppermute | solution.py:125
  64.9 2.0 %fusion.68 = (f32[32,1,45,128]{3,1,2,0:T(1,128)S(1)}, f32[32,1,45,128]{3,1,2,0:T(1,128)}) fusion(f32[32,2,45,128]{3,1,2,0:T(2,128)S(1)} %copy-done), kind=kLoop, calls=%fused_computation.117 | loop fusion | bytes 2949120 | tf_op jit(solution)/shard_map/slice | solution.py:129
  67.0 1.0 %copy.41 = f32[32,1,45,128]{3,0,2,1:T(8,128)} copy(f32[32,1,45,128]{3,1,2,0:T(1,128)S(1)} %get-tuple-element.5) | data formatting | bytes 1474560
  67.9 3.9 %collective-permute-done.1 = bf16[1,32,3,128]{3,1,2,0:T(8,128)(2,1)S(1)} collective-permute-done((bf16[1,32,3,128]{3,1,2,0:T(8,128)(2,1)S(1)}, bf16[1,32,3,128]{3,1,2,0:T(8,128)(2,1)S(1)}, u32[]{:S(2)}, u32[]{:S(2)}) %collective-permute-start.1) | collective-permute-done | bytes 24608 | tf_op jit(solution)/shard_map/ppermute | solution.py:16
  71.9 0.0 collective-permute-done.2
  71.9 0.1 maximum_convert_fusion.1
  72.0 0.1 fusion.29
  72.1 0.2 slice_subtract_fusion.5
  72.3 1.2 %all-to-all-done.1 = bf16[32,92,128]{2,1,0:T(8,128)(2,1)S(1)} async-done(((bf16[32,92,128]{2,1,0:T(8,128)(2,1)}), bf16[32,92,128]{2,1,0:T(8,128)(2,1)S(1)}, u32[]{:S(2)}, u32[]{:S(2)}) %all-to-all-start.1) | async-done | bytes 753696 | tf_op jit(solution)/shard_map/all_to_all | solution.py:111
  73.5 0.3 copy.24
  73.8 0.0 copy-start.1
  73.8 0.2 convert.2
  74.0 0.0 collective-permute-done
  74.1 1.6 %fusion.39 = f32[1,32,46,128]{3,1,2,0:T(8,128)S(1)} fusion(f32[1,32,47,128]{3,1,2,0:T(8,128)S(1)} %get-tuple-element.10, f32[1,32,47,128]{3,1,2,0:T(8,128)S(1)} %get-tuple-element.9, f32[1,32,48,128]{3,1,2,0:T(8,128)S(1)} %fusion.29, f32[32,46,2,128]{3,0,2,1:T(8,128)S(1)} %convert.2, f32[1,32,1,128]{3,1,2,0:T(8,128)S(1)} %bitcast.75, ...), kind=kLoop, calls=%fused_computation.57 | loop fusion | flops 3768320 | bytes 6029312 | tf_op jit(solution)/shard_map/jit(_where)/select_n | solution.py:59
  75.6 0.1 fusion.47
  75.8 0.0 copy-done.1
  75.8 0.1 fusion.45
  75.9 0.1 pad_maximum_fusion.5
  76.0 1.9 %collective-permute-start.3 = (bf16[2,3,45,128]{3,1,2,0:T(4,128)(2,1)S(1)}, bf16[2,3,45,128]{3,1,2,0:T(4,128)(2,1)S(1)}, u32[]{:S(2)}, u32[]{:S(2)}) collective-permute-start(bf16[2,3,45,128]{3,1,2,0:T(4,128)(2,1)S(1)} %get-tuple-element.12), channel_id=1, source_target_pairs={{32,0},{64,32},{96,64},{128,96},{160,128},{192,160},{224,192},{256... | collective-permute-start | bytes 207368 | tf_op jit(solution)/shard_map/ppermute | solution.py:17
  77.9 2.4 %collective-permute-start.4 = (bf16[2,3,45,128]{3,1,2,0:T(4,128)(2,1)S(1)}, bf16[2,3,45,128]{3,1,2,0:T(4,128)(2,1)S(1)}, u32[]{:S(2)}, u32[]{:S(2)}) collective-permute-start(bf16[2,3,45,128]{3,1,2,0:T(4,128)(2,1)S(1)} %get-tuple-element.11), channel_id=1, source_target_pairs={{0,32},{32,64},{64,96},{96,128},{128,160},{160,192},{192,224},{224... | collective-permute-start | bytes 207368 | tf_op jit(solution)/shard_map/ppermute | solution.py:16
  80.4 0.0 collective-permute-done.3
  80.4 4.6 %collective-permute-done.4 = bf16[2,3,45,128]{3,1,2,0:T(4,128)(2,1)S(1)} collective-permute-done((bf16[2,3,45,128]{3,1,2,0:T(4,128)(2,1)S(1)}, bf16[2,3,45,128]{3,1,2,0:T(4,128)(2,1)S(1)}, u32[]{:S(2)}, u32[]{:S(2)}) %collective-permute-start.4) | collective-permute-done | bytes 69152 | tf_op jit(solution)/shard_map/ppermute | solution.py:16
  85.0 0.2 fusion.48
  85.2 0.3 fusion.21
  85.5 0.3 slice_subtract_fusion.1
  85.9 0.9 fusion.14
  86.7 0.9 %fusion.43 = bf16[1,32,45,128]{3,1,2,0:T(8,128)(2,1)} fusion(f32[1,33,45,128]{3,1,2,0:T(8,128)S(1)} %fusion.14, bf16[1,32,45,128]{3,1,2,0:T(8,128)(2,1)S(1)} %fusion.47), kind=kLoop, calls=%fused_computation.63 | loop fusion | flops 737280 | bytes 2211840 | tf_op jit(solution)/shard_map/convert_element_type | solution.py:144
  (8 shorter events, 0.0 us)
Async XLA Ops:
  0.0 16.7 %copy-start.4 = (s32[32]{0:T(128)S(1)}, s32[32]{0:T(128)}, u32[]{:S(2)}) copy-start(s32[32]{0:T(128)} %param.7) | copy-start | bytes 388
  0.0 16.7 %copy-start.5 = (s32[32]{0:T(128)S(1)}, s32[32]{0:T(128)}, u32[]{:S(2)}) copy-start(s32[32]{0:T(128)} %param.8) | copy-start | bytes 388
  0.0 16.8 %copy-start.3 = (f32[32,721]{1,0:T(8,128)S(1)}, f32[32,721]{1,0:T(8,128)}, u32[]{:S(2)}) copy-start(f32[32,721]{1,0:T(8,128)} %param.9) | copy-start | bytes 276868
  2.8 36.1 %all-to-all-start = ((bf16[32,90,128]{2,1,0:T(8,128)(2,1)}), bf16[32,90,128]{2,1,0:T(8,128)(2,1)S(1)}, u32[]{:S(2)}, u32[]{:S(2)}) async-start(bf16[32,90,128]{2,1,0:T(8,128)(2,1)} %copy.19), calls=%async_computation | async-start | bytes 1572864 | tf_op jit(solution)/shard_map/all_to_all | solution.py:96
  38.9 4.7 %slice-start = ((s8[4718592]{0:T(1024)(128)(4,1)}), s8[4194304]{0:T(1024)(128)(4,1)S(1)}, s32[]{:S(2)}) async-start(s8[4718592]{0:T(1024)(128)(4,1)} %bitcast.68), calls=%async_computation.2 | async-start | bytes 8388608
  39.2 4.4 %slice-start.1 = ((s8[4718592]{0:T(1024)(128)(4,1)}), s8[524288]{0:T(1024)(128)(4,1)S(1)}, s32[]{:S(2)}) async-start(s8[4718592]{0:T(1024)(128)(4,1)} %bitcast.68), calls=%async_computation.3 | async-start | bytes 1048576
  43.6 8.1 %copy-start.2 = (bf16[1,32,45,128]{3,1,2,0:T(8,128)(2,1)S(1)}, bf16[1,32,45,128]{3,1,2,0:T(8,128)(2,1)}, u32[]{:S(2)}) copy-start(bf16[1,32,45,128]{3,1,2,0:T(8,128)(2,1)} %param.5) | copy-start | bytes 1105924
  45.1 15.8 %copy-start = (f32[32,2,45,128]{3,1,2,0:T(2,128)S(1)}, f32[32,2,45,128]{3,1,2,0:T(2,128)}, u32[]{:S(2)}) copy-start(f32[32,2,45,128]{3,1,2,0:T(2,128)} %param.6) | copy-start | bytes 4423684
  46.6 27.0 %all-to-all-start.1 = ((bf16[32,92,128]{2,1,0:T(8,128)(2,1)}), bf16[32,92,128]{2,1,0:T(8,128)(2,1)S(1)}, u32[]{:S(2)}, u32[]{:S(2)}) async-start(bf16[32,92,128]{2,1,0:T(8,128)(2,1)} %copy.23), calls=%async_computation.1 | async-start | bytes 1572864 | tf_op jit(solution)/shard_map/all_to_all | solution.py:111
  51.7 20.1 %collective-permute-start.1 = (bf16[1,32,3,128]{3,1,2,0:T(8,128)(2,1)S(1)}, bf16[1,32,3,128]{3,1,2,0:T(8,128)(2,1)S(1)}, u32[]{:S(2)}, u32[]{:S(2)}) collective-permute-start(bf16[1,32,3,128]{3,1,2,0:T(8,128)(2,1)S(1)} %get-tuple-element.15), channel_id=1, source_target_pairs={{0,1},{1,2},{2,3},{3,4},{4,5},{5,6},{6,7},{7,8},{8,9},{9,10},{10,1... | collective-permute-start | bytes 73736 | tf_op jit(solution)/shard_map/ppermute | solution.py:16
  55.5 16.4 %collective-permute-start.2 = (bf16[1,32,3,128]{3,1,2,0:T(8,128)(2,1)S(1)}, bf16[1,32,3,128]{3,1,2,0:T(8,128)(2,1)S(1)}, u32[]{:S(2)}, u32[]{:S(2)}) collective-permute-start(bf16[1,32,3,128]{3,1,2,0:T(8,128)(2,1)S(1)} %get-tuple-element.16), channel_id=1, source_target_pairs={{1,0},{2,1},{3,2},{4,3},{5,4},{6,5},{7,6},{8,7},{9,8},{10,9},{11,1... | collective-permute-start | bytes 73736 | tf_op jit(solution)/shard_map/ppermute | solution.py:17
  61.0 13.1 %collective-permute-start = (f32[32,1,128]{2,0,1:T(8,128)S(1)}, f32[32,1,128]{2,0,1:T(8,128)S(1)}, u32[]{:S(2)}, u32[]{:S(2)}) collective-permute-start(f32[32,1,128]{2,0,1:T(8,128)S(1)} %bitcast.76), channel_id=1, source_target_pairs={{0,31},{1,0},{2,1},{3,2},{4,3},{5,4},{6,5},{7,6},{8,7},{9,8},{10,9... | collective-permute-start | bytes 49160 | tf_op jit(solution)/shard_map/ppermute | solution.py:125
  73.8 1.9 %copy-start.1 = (f32[32,1,45,128]{3,1,2,0:T(1,128)S(1)}, f32[32,1,45,128]{3,1,2,0:T(1,128)}, u32[]{:S(2)}) copy-start(f32[32,1,45,128]{3,1,2,0:T(1,128)} %get-tuple-element.6) | copy-start | bytes 2211844
  76.0 4.4 %collective-permute-start.3 = (bf16[2,3,45,128]{3,1,2,0:T(4,128)(2,1)S(1)}, bf16[2,3,45,128]{3,1,2,0:T(4,128)(2,1)S(1)}, u32[]{:S(2)}, u32[]{:S(2)}) collective-permute-start(bf16[2,3,45,128]{3,1,2,0:T(4,128)(2,1)S(1)} %get-tuple-element.12), channel_id=1, source_target_pairs={{32,0},{64,32},{96,64},{128,96},{160,128},{192,160},{224,192},{256... | collective-permute-start | bytes 207368 | tf_op jit(solution)/shard_map/ppermute | solution.py:17
  77.9 7.1 %collective-permute-start.4 = (bf16[2,3,45,128]{3,1,2,0:T(4,128)(2,1)S(1)}, bf16[2,3,45,128]{3,1,2,0:T(4,128)(2,1)S(1)}, u32[]{:S(2)}, u32[]{:S(2)}) collective-permute-start(bf16[2,3,45,128]{3,1,2,0:T(4,128)(2,1)S(1)} %get-tuple-element.11), channel_id=1, source_target_pairs={{0,32},{32,64},{64,96},{96,128},{128,160},{160,192},{192,224},{224... | collective-permute-start | bytes 207368 | tf_op jit(solution)/shard_map/ppermute | solution.py:16

commit v2 on v1

--- a/solution.py
+++ b/solution.py
@@ -86,28 +86,34 @@
     blocks = lax.axis_size("lon")
     mode_count = row_factor.shape[1]
     per_device = 2 * row_count // blocks
+    rows_here = per_device // 2
     table, mode_weight = spectral_basis(blocks, lon_local, lon_local + 1, mode_count)
-    forward_table = table[:, :lon_local].astype(jnp.bfloat16)
-    inverse_table = table.astype(jnp.bfloat16)
-    outgoing = courant.transpose(0, 2, 1, 3).astype(jnp.bfloat16)
-    outgoing = outgoing.reshape(blocks, (2 * row_count // blocks) * lon_local, levels)
+    forward_table = table[:, :lon_local].reshape(blocks * lon_local, 2 * mode_count)
+    inverse_table = table.reshape(blocks * (lon_local + 1), 2 * mode_count).astype(jnp.bfloat16)
+    outgoing = courant.transpose(0, 2, 1, 3).reshape(row_count, lon_local, 2 * levels)
+    outgoing = outgoing.astype(jnp.bfloat16).reshape(blocks, rows_here * lon_local, 2 * levels)
     pair_factor = jnp.repeat(1.0 - row_factor, 2, axis=0)
     removal = jnp.concatenate([pair_factor, pair_factor], axis=1) * mode_weight[None, :]
     arrived = lax.all_to_all(outgoing, "lon", split_axis=0, concat_axis=0, tiled=True)
-    level_block = arrived.reshape(blocks, per_device // 2, lon_local, 2, levels)
     first_row = lax.axis_index("lon") * per_device
     local_removal = lax.dynamic_slice_in_dim(removal, first_row, per_device, 0)
+    local_removal = local_removal.reshape(rows_here, 2, 2 * mode_count).transpose(0, 2, 1)
+    gathered = arrived.reshape(blocks, rows_here, lon_local, 2 * levels)
     spectrum = jnp.einsum(
-        "drjcl,djm->rcml", level_block, forward_table, preferred_element_type=jnp.float32
-    ).reshape(per_device, 2 * mode_count, levels)
-    weighted = (spectrum * local_removal[:, :, None]).astype(jnp.bfloat16)
+        "drjk,djm->rmk",
+        gathered,
+        forward_table.astype(jnp.bfloat16).reshape(blocks, lon_local, 2 * mode_count),
+        preferred_element_type=jnp.float32,
+    ).reshape(rows_here, 2 * mode_count, 2, levels)
+    weighted = (spectrum * local_removal[:, :, :, None]).astype(jnp.bfloat16)
     correction = jnp.einsum(
-        "rcml,djm->drjcl",
-        weighted.reshape(per_device // 2, 2, 2 * mode_count, levels),
+        "rmk,pm->prk",
+        weighted.reshape(rows_here, 2 * mode_count, 2 * levels),
         inverse_table,
         preferred_element_type=jnp.float32,
     ).astype(jnp.bfloat16)
-    correction = correction.reshape(blocks, per_device * (lon_local + 1), levels)
+    correction = correction.reshape(blocks, lon_local + 1, rows_here, 2 * levels)
+    correction = correction.transpose(0, 2, 1, 3).reshape(blocks, rows_here * (lon_local + 1), 2 * levels)
     returned = lax.all_to_all(correction, "lon", split_axis=0, concat_axis=0, tiled=True)
     return returned.reshape(row_count, lon_local + 1, 2, levels)
 

time: 88.1 us -> 101 us (1.15)
  local copies, waits for them, and re-layouts: 8.14 us -> 25.7 us
  waiting for transfers between devices: 25.5 us -> 21.3 us
    convert_element_type x1 -> x3, local copies, waits for them, and re-layouts: 0.29 us -> 9.68 us  [the longest x1 5.36 us: filter_correction(): weighted = (spectrum * local_removal[:, :, :, None]).astype(jnp.bfloat16)]
    neg x0 -> x1, local copies, waits for them, and re-layouts: none -> 4.28 us  [spectral_basis(): table = jnp.concatenate([cosine, -sine], axis=2)]
    all_to_all x1, waiting for transfers between devices: 15.7 us -> 11.5 us  [filter_correction(): lax.all_to_all(outgoing, 'lon', split_axis=0, concat_axis=0, tiled=True)]
    another operation x0 -> x1, other arithmetic: none -> 3.02 us
    reshape x2 -> x0, local copies, waits for them, and re-layouts: 2.39 us -> none  [the longest x1 1.21 us: filter_correction(): outgoing.reshape(blocks, 2 * row_count // blocks * lon_local, levels)]
    sub x0 -> x1, local copies, waits for them, and re-layouts: none -> 2.39 us  [spectral_basis(): cosine = cc * cf - sc * sf]
    slice x0 -> x3, local copies, waits for them, and re-layouts: none -> 2.22 us  [the longest x1 2.22 us: local(): correction[:, :lon_local, 1]]
    convert_element_type x1, other arithmetic: 3.86 us -> 1.92 us  [filter_correction(): outgoing.astype(jnp.bfloat16)]
  transfers between devices with their start and end apart: 7 -> 7, of which waited for: 4 -> 4; matrix products, arithmetic and copies ran while one was open for 13% -> 21% of each run, Pallas kernels for 0% -> 0%
where the time goes in v2:
time: 101 us
  starting transfers between devices  35.8 us (35%)
  local copies, waits for them, and re-layouts  25.7 us (25%)
  waiting for transfers between devices  21.3 us (21%)
  other arithmetic  11.5 us (11%)
  matrix products  5.87 us (6%)
    all_to_all x1, starting transfers between devices, filter_correction(): lax.all_to_all(outgoing, 'lon', split_axis=0, concat_axis=0, tiled=True)  13.2 us
    all_to_all x1, waiting for transfers between devices, filter_correction(): lax.all_to_all(outgoing, 'lon', split_axis=0, concat_axis=0, tiled=True)  11.5 us
    ppermute x2, waiting for transfers between devices, padded(): before = lax.ppermute(last, axis, up)  8.6 us
    ppermute x2, starting transfers between devices, padded(): after = lax.ppermute(leading, axis, down)  7.39 us
    ppermute x2, starting transfers between devices, padded(): before = lax.ppermute(last, axis, up)  6.1 us
    convert_element_type x1, local copies, waits for them, and re-layouts, filter_correction(): weighted = (spectrum * local_removal[:, :, :, None]).astype(jnp.bfloat16)  5.36 us
    all_to_all x1, starting transfers between devices, filter_correction(): lax.all_to_all(correction, 'lon', split_axis=0, concat_axis=0, tiled=True)  5.13 us
    dot_general x1, matrix products, filter_correction(): jnp.einsum('drjk,djm->rmk', gathered, forward_table.astype(jnp.bfloat16)....  4.39 us
  transfers between devices with their start and end apart: 7, of which 4 were waited for; matrix products, arithmetic and copies ran while one was open for 21% of the time, Pallas kernels for 0%

profile of v2, /device:TPU:32, one launch (start us, length us, event | category | flops | bytes accessed | tf_op | source)
XLA Modules:
  0.0 100.6 jit_solution(15781048308352977201)
XLA Ops:
  0.0 1.9 %convert_bitcast_fusion = bf16[32,45,2,128]{3,2,1,0:T(2,128)(2,1)S(1)} fusion(f32[32,2,45,128]{3,1,2,0:T(2,128)} %param.6), kind=kLoop, calls=%fused_computation.72 | loop fusion | flops 368640 | bytes 2211840 | tf_op jit(solution)/shard_map/convert_element_type | solution.py:94
  1.9 1.3 %reshape.341 = bf16[32,45,256]{2,1,0:T(8,128)(2,1)} reshape(bf16[32,45,2,128]{3,2,1,0:T(2,128)(2,1)S(1)} %convert_bitcast_fusion) | data formatting | bytes 1474560 | tf_op jit(solution)/shard_map/convert_element_type | solution.py:94
  3.3 13.2 %all-to-all-start = ((bf16[32,45,256]{2,1,0:T(8,128)(2,1)}), bf16[32,45,256]{2,1,0:T(8,128)(2,1)S(1)}, u32[]{:S(2)}, u32[]{:S(2)}) async-start(bf16[32,45,256]{2,1,0:T(8,128)(2,1)} %reshape.341), calls=%async_computation | async-start | bytes 1572864 | tf_op jit(solution)/shard_map/all_to_all | solution.py:97
  16.5 0.0 copy-done.7
  16.5 0.0 copy-done.8
  16.5 0.0 copy-done.6
  16.5 0.1 select_subtract_fusion
  16.6 0.1 broadcast_in_dim.20
  16.7 0.1 reshape.335
  16.8 0.6 fusion.62
  17.5 0.5 fusion.70
  18.0 3.0 %subtract_convert_fusion = (bf16[32,46,721]{2,1,0:T(8,128)(2,1)S(1)}, bf16[32,46,721]{2,1,0:T(8,128)(2,1)}) fusion(f32[46,721]{1,0:T(8,128)S(1)} %get-tuple-element.19, f32[32,721]{1,0:T(8,128)S(1)} %get-tuple-element.18, f32[46,721]{1,0:T(8,128)S(1)} %get-tuple-element.20, f32[32,721]{1,0:T(8,128)S(1)} %get-tuple-element.17), kind=kLoop, calls=%fused_computation.5 | loop fusion | flops 9551808 | bytes 4695152 | tf_op jit(solution)/shard_map/convert.7
  21.0 4.3 %neg.10 = bf16[1472,721]{1,0:T(8,128)(2,1)} reshape(bf16[32,46,721]{2,1,0:T(8,128)(2,1)} %get-tuple-element.14) | data formatting | bytes 4245248 | tf_op jit(solution)/shard_map/neg | solution.py:77
  25.3 2.4 %sub.117 = bf16[1472,721]{1,0:T(8,128)(2,1)} reshape(bf16[32,46,721]{2,1,0:T(8,128)(2,1)S(1)} %get-tuple-element.13) | data formatting | bytes 4245248 | tf_op jit(solution)/shard_map/sub | solution.py:75
  27.7 0.1 pad_maximum_fusion.8
  27.7 0.1 multiply_bitcast_fusion
  27.8 11.5 %all-to-all-done = bf16[32,45,256]{2,1,0:T(8,128)(2,1)S(1)} async-done(((bf16[32,45,256]{2,1,0:T(8,128)(2,1)}), bf16[32,45,256]{2,1,0:T(8,128)(2,1)S(1)}, u32[]{:S(2)}, u32[]{:S(2)}) %all-to-all-start) | async-done | bytes 737312 | tf_op jit(solution)/shard_map/all_to_all | solution.py:97
  39.3 1.1 %reshape.342 = bf16[2,128,32,45]{1,0,3,2:T(2,128)(2,1)} reshape(bf16[256,32,45]{0,2,1:T(8,128)(2,1)S(1)} %bitcast.51) | data formatting | bytes 1474560 | tf_op jit(solution)/shard_map/drjk,djm->rmk/dot_general | solution.py:102
  40.5 4.4 %fusion.17 = bf16[1442,2,128]{2,0,1:T(8,128)(2,1)S(1)} fusion(bf16[32,46,721]{2,1,0:T(8,128)(2,1)} %get-tuple-element.14, bf16[32,46,721]{2,1,0:T(8,128)(2,1)S(1)} %get-tuple-element.13, bf16[2,128,32,45]{1,0,3,2:T(2,128)(2,1)} %reshape.342, f32[1442,2]{0,1:T(2,128)S(1)} %multiply_bitcast_fusion), kind=kOutput, calls=%fused_computation.13 | convolution fusion | flops 1072201984 | bytes 5732368 | tf_op jit(solution)/shard_map/drjk,djm->rmk/dot_general | solution.py:102
  44.9 0.0 copy-start.3
  44.9 5.4 %copy.43 = bf16[1442,2,128]{2,1,0:T(2,128)(2,1)S(1)} copy(bf16[1442,2,128]{2,0,1:T(8,128)(2,1)S(1)} %fusion.17) | data formatting | bytes 1476608 | tf_op jit(solution)/shard_map/convert_element_type | solution.py:108
  50.3 0.6 pad.35
  50.9 0.1 copy.55
  51.0 0.0 copy-done.4
  51.0 0.0 copy-done.3
  51.0 1.5 %fusion.14 = bf16[1472,256]{1,0:T(8,128)(2,1)S(1)} fusion(bf16[1442,256]{1,0:T(8,128)(2,1)S(1)} %bitcast.55, bf16[1472,721]{1,0:T(8,128)(2,1)S(1)} %copy-done.3, bf16[1472,721]{1,0:T(8,128)(2,1)S(1)} %copy-done.4), kind=kOutput, calls=%fused_computation.12 | convolution fusion | flops 1095650816 | bytes 5737216 | tf_op jit(solution)/shard_map/rmk,pm->prk/dot_general | solution.py:109
  52.5 0.0 copy-start.5
  52.5 0.0 copy-start
  52.5 1.1 %reshape_transpose_reshape.3 = bf16[32,46,256]{2,1,0:T(8,128)(2,1)} reshape(bf16[1472,256]{1,0:T(8,128)(2,1)S(1)} %fusion.14) | data formatting | bytes 1507328 | tf_op jit(solution)/shard_map/reshape;transpose;reshape | solution.py:116
  53.6 5.1 %all-to-all-start.1 = ((bf16[32,46,256]{2,1,0:T(8,128)(2,1)}), bf16[32,46,256]{2,1,0:T(8,128)(2,1)S(1)}, u32[]{:S(2)}, u32[]{:S(2)}) async-start(bf16[32,46,256]{2,1,0:T(8,128)(2,1)} %reshape_transpose_reshape.3), calls=%async_computation.1 | async-start | bytes 1572864 | tf_op jit(solution)/shard_map/all_to_all | solution.py:117
  58.8 0.0 copy-done.5
  58.8 3.7 %collective-permute-start.1 = (bf16[1,32,3,128]{3,1,2,0:T(8,128)(2,1)S(1)}, bf16[1,32,3,128]{3,1,2,0:T(8,128)(2,1)S(1)}, u32[]{:S(2)}, u32[]{:S(2)}) collective-permute-start(bf16[1,32,3,128]{3,1,2,0:T(8,128)(2,1)S(1)} %get-tuple-element.15), channel_id=1, source_target_pairs={{0,1},{1,2},{2,3},{3,4},{4,5},{5,6},{6,7},{7,8},{8,9},{9,10},{10,1... | collective-permute-start | bytes 73736 | tf_op jit(solution)/shard_map/ppermute | solution.py:16
  62.5 5.5 %collective-permute-start.2 = (bf16[1,32,3,128]{3,1,2,0:T(8,128)(2,1)S(1)}, bf16[1,32,3,128]{3,1,2,0:T(8,128)(2,1)S(1)}, u32[]{:S(2)}, u32[]{:S(2)}) collective-permute-start(bf16[1,32,3,128]{3,1,2,0:T(8,128)(2,1)S(1)} %get-tuple-element.16), channel_id=1, source_target_pairs={{1,0},{2,1},{3,2},{4,3},{5,4},{6,5},{7,6},{8,7},{9,8},{10,9},{11,1... | collective-permute-start | bytes 73736 | tf_op jit(solution)/shard_map/ppermute | solution.py:17
  68.0 0.0 copy-done
  68.0 4.0 %collective-permute-start = (f32[32,1,128]{2,0,1:T(8,128)S(1)}, f32[32,1,128]{2,0,1:T(8,128)S(1)}, u32[]{:S(2)}, u32[]{:S(2)}) collective-permute-start(f32[32,1,128]{2,0,1:T(8,128)S(1)} %bitcast.57), channel_id=1, source_target_pairs={{0,31},{1,0},{2,1},{3,2},{4,3},{5,4},{6,5},{7,6},{8,7},{9,8},{10,9... | collective-permute-start | bytes 49160 | tf_op jit(solution)/shard_map/ppermute | solution.py:131
  72.0 2.0 %fusion.78 = (f32[32,1,45,128]{3,1,2,0:T(1,128)S(1)}, f32[32,1,45,128]{3,1,2,0:T(1,128)}) fusion(f32[32,2,45,128]{3,1,2,0:T(2,128)S(1)} %copy-done), kind=kLoop, calls=%fused_computation.120 | loop fusion | bytes 2949120 | tf_op jit(solution)/shard_map/slice | solution.py:135
  74.0 1.0 copy.65
  74.9 4.0 %collective-permute-done.1 = bf16[1,32,3,128]{3,1,2,0:T(8,128)(2,1)S(1)} collective-permute-done((bf16[1,32,3,128]{3,1,2,0:T(8,128)(2,1)S(1)}, bf16[1,32,3,128]{3,1,2,0:T(8,128)(2,1)S(1)}, u32[]{:S(2)}, u32[]{:S(2)}) %collective-permute-start.1) | collective-permute-done | bytes 24608 | tf_op jit(solution)/shard_map/ppermute | solution.py:16
  78.9 0.0 collective-permute-done.2
  78.9 0.1 maximum_convert_fusion
  79.0 0.1 fusion.39
  79.1 0.2 slice_subtract_fusion.5
  79.3 1.2 %all-to-all-done.1 = bf16[32,46,256]{2,1,0:T(8,128)(2,1)S(1)} async-done(((bf16[32,46,256]{2,1,0:T(8,128)(2,1)}), bf16[32,46,256]{2,1,0:T(8,128)(2,1)S(1)}, u32[]{:S(2)}, u32[]{:S(2)}) %all-to-all-start.1) | async-done | bytes 753696 | tf_op jit(solution)/shard_map/all_to_all | solution.py:117
  80.6 1.4 %copy_convert_fusion = f32[32,46,256]{2,0,1:T(8,128)} fusion(bf16[32,46,256]{2,1,0:T(8,128)(2,1)S(1)} %all-to-all-done.1), kind=kLoop, calls=%fused_computation.61 | loop fusion | flops 376832 | bytes 2260992 | tf_op jit(solution)/shard_map/convert_element_type | solution.py:134
  81.9 3.0 %reshape.338 = f32[32,46,2,128]{3,2,0,1:T(2,128)} reshape(f32[32,46,256]{2,0,1:T(8,128)} %copy_convert_fusion) | data formatting | bytes 3014656 | tf_op jit(solution)/shard_map/convert_element_type | solution.py:134
  84.9 2.2 %slice.183 = f32[32,45,1,128]{3,2,0,1:T(1,128)S(1)} slice(f32[32,46,2,128]{3,2,0,1:T(2,128)} %reshape.338), slice={[0:32], [0:45], [1:2], [0:128]} | slice | bytes 1474560 | tf_op jit(solution)/shard_map/slice | solution.py:137
  87.1 0.0 collective-permute-done
  87.1 0.0 copy-done.2
  87.1 0.0 slice-done
  87.2 0.5 fusion.49
  87.6 0.0 copy-start.1
  87.6 0.1 fusion.54
  87.8 1.0 copy-done.1
  88.7 0.1 fusion.56
  88.9 0.1 pad_maximum_fusion.6
  89.0 1.9 %collective-permute-start.3 = (bf16[2,3,45,128]{3,1,2,0:T(4,128)(2,1)S(1)}, bf16[2,3,45,128]{3,1,2,0:T(4,128)(2,1)S(1)}, u32[]{:S(2)}, u32[]{:S(2)}) collective-permute-start(bf16[2,3,45,128]{3,1,2,0:T(4,128)(2,1)S(1)} %get-tuple-element.12), channel_id=1, source_target_pairs={{32,0},{64,32},{96,64},{128,96},{160,128},{192,160},{224,192},{256... | collective-permute-start | bytes 207368 | tf_op jit(solution)/shard_map/ppermute | solution.py:17
  90.9 2.4 %collective-permute-start.4 = (bf16[2,3,45,128]{3,1,2,0:T(4,128)(2,1)S(1)}, bf16[2,3,45,128]{3,1,2,0:T(4,128)(2,1)S(1)}, u32[]{:S(2)}, u32[]{:S(2)}) collective-permute-start(bf16[2,3,45,128]{3,1,2,0:T(4,128)(2,1)S(1)} %get-tuple-element.11), channel_id=1, source_target_pairs={{0,32},{32,64},{64,96},{96,128},{128,160},{160,192},{192,224},{224... | collective-permute-start | bytes 207368 | tf_op jit(solution)/shard_map/ppermute | solution.py:16
  93.3 0.0 collective-permute-done.3
  93.3 4.6 %collective-permute-done.4 = bf16[2,3,45,128]{3,1,2,0:T(4,128)(2,1)S(1)} collective-permute-done((bf16[2,3,45,128]{3,1,2,0:T(4,128)(2,1)S(1)}, bf16[2,3,45,128]{3,1,2,0:T(4,128)(2,1)S(1)}, u32[]{:S(2)}, u32[]{:S(2)}) %collective-permute-start.4) | collective-permute-done | bytes 69152 | tf_op jit(solution)/shard_map/ppermute | solution.py:16
  98.0 0.2 fusion.57
  98.2 0.3 fusion.31
  98.5 0.3 slice_subtract_fusion.1
  98.8 0.9 fusion.24
  99.7 0.9 fusion.52
  (13 shorter events, 0.1 us)
Async XLA Ops:
  0.0 16.5 %copy-start.7 = (s32[32]{0:T(128)S(1)}, s32[32]{0:T(128)}, u32[]{:S(2)}) copy-start(s32[32]{0:T(128)} %param.7) | copy-start | bytes 388
  0.0 16.5 %copy-start.8 = (s32[32]{0:T(128)S(1)}, s32[32]{0:T(128)}, u32[]{:S(2)}) copy-start(s32[32]{0:T(128)} %param.8) | copy-start | bytes 388
  0.0 16.5 %copy-start.6 = (f32[32,721]{1,0:T(8,128)S(1)}, f32[32,721]{1,0:T(8,128)}, u32[]{:S(2)}) copy-start(f32[32,721]{1,0:T(8,128)} %param.9) | copy-start | bytes 276868
  3.3 36.1 %all-to-all-start = ((bf16[32,45,256]{2,1,0:T(8,128)(2,1)}), bf16[32,45,256]{2,1,0:T(8,128)(2,1)S(1)}, u32[]{:S(2)}, u32[]{:S(2)}) async-start(bf16[32,45,256]{2,1,0:T(8,128)(2,1)} %reshape.341), calls=%async_computation | async-start | bytes 1572864 | tf_op jit(solution)/shard_map/all_to_all | solution.py:97
  40.5 10.5 %copy-start.4 = (bf16[1472,721]{1,0:T(8,128)(2,1)S(1)}, bf16[1472,721]{1,0:T(8,128)(2,1)}, u32[]{:S(2)}) copy-start(bf16[1472,721]{1,0:T(8,128)(2,1)} %sub.117) | copy-start | bytes 6367876
  44.9 6.1 %copy-start.3 = (bf16[1472,721]{1,0:T(8,128)(2,1)S(1)}, bf16[1472,721]{1,0:T(8,128)(2,1)}, u32[]{:S(2)}) copy-start(bf16[1472,721]{1,0:T(8,128)(2,1)} %neg.10) | copy-start | bytes 6367876
  52.5 6.2 %copy-start.5 = (bf16[1,32,45,128]{3,1,2,0:T(8,128)(2,1)S(1)}, bf16[1,32,45,128]{3,1,2,0:T(8,128)(2,1)}, u32[]{:S(2)}) copy-start(bf16[1,32,45,128]{3,1,2,0:T(8,128)(2,1)} %param.5) | copy-start | bytes 1105924
  52.5 15.4 %copy-start = (f32[32,2,45,128]{3,1,2,0:T(2,128)S(1)}, f32[32,2,45,128]{3,1,2,0:T(2,128)}, u32[]{:S(2)}) copy-start(f32[32,2,45,128]{3,1,2,0:T(2,128)} %param.6) | copy-start | bytes 4423684
  53.6 26.9 %all-to-all-start.1 = ((bf16[32,46,256]{2,1,0:T(8,128)(2,1)}), bf16[32,46,256]{2,1,0:T(8,128)(2,1)S(1)}, u32[]{:S(2)}, u32[]{:S(2)}) async-start(bf16[32,46,256]{2,1,0:T(8,128)(2,1)} %reshape_transpose_reshape.3), calls=%async_computation.1 | async-start | bytes 1572864 | tf_op jit(solution)/shard_map/all_to_all | solution.py:117
  58.8 20.1 %collective-permute-start.1 = (bf16[1,32,3,128]{3,1,2,0:T(8,128)(2,1)S(1)}, bf16[1,32,3,128]{3,1,2,0:T(8,128)(2,1)S(1)}, u32[]{:S(2)}, u32[]{:S(2)}) collective-permute-start(bf16[1,32,3,128]{3,1,2,0:T(8,128)(2,1)S(1)} %get-tuple-element.15), channel_id=1, source_target_pairs={{0,1},{1,2},{2,3},{3,4},{4,5},{5,6},{6,7},{7,8},{8,9},{9,10},{10,1... | collective-permute-start | bytes 73736 | tf_op jit(solution)/shard_map/ppermute | solution.py:16
  62.5 16.4 %collective-permute-start.2 = (bf16[1,32,3,128]{3,1,2,0:T(8,128)(2,1)S(1)}, bf16[1,32,3,128]{3,1,2,0:T(8,128)(2,1)S(1)}, u32[]{:S(2)}, u32[]{:S(2)}) collective-permute-start(bf16[1,32,3,128]{3,1,2,0:T(8,128)(2,1)S(1)} %get-tuple-element.16), channel_id=1, source_target_pairs={{1,0},{2,1},{3,2},{4,3},{5,4},{6,5},{7,6},{8,7},{9,8},{10,9},{11,1... | collective-permute-start | bytes 73736 | tf_op jit(solution)/shard_map/ppermute | solution.py:17
  68.0 19.1 %collective-permute-start = (f32[32,1,128]{2,0,1:T(8,128)S(1)}, f32[32,1,128]{2,0,1:T(8,128)S(1)}, u32[]{:S(2)}, u32[]{:S(2)}) collective-permute-start(f32[32,1,128]{2,0,1:T(8,128)S(1)} %bitcast.57), channel_id=1, source_target_pairs={{0,31},{1,0},{2,1},{3,2},{4,3},{5,4},{6,5},{7,6},{8,7},{9,8},{10,9... | collective-permute-start | bytes 49160 | tf_op jit(solution)/shard_map/ppermute | solution.py:131
  81.9 5.2 %copy-start.2 = (f32[32,1,45,128]{3,0,2,1:T(8,128)S(1)}, f32[32,1,45,128]{3,0,2,1:T(8,128)}, u32[]{:S(2)}) copy-start(f32[32,1,45,128]{3,0,2,1:T(8,128)} %copy.65) | copy-start | bytes 2211844
  84.9 2.3 %slice-start = ((f32[32,46,2,128]{3,2,0,1:T(2,128)}), f32[32,46,1,128]{3,2,0,1:T(1,128)S(1)}, s32[]{:S(2)}) async-start(f32[32,46,2,128]{3,2,0,1:T(2,128)} %reshape.338), calls=%async_computation.2 | async-start | bytes 1507328 | tf_op jit(solution)/shard_map/slice | solution.py:136
  87.6 1.1 %copy-start.1 = (f32[32,1,45,128]{3,1,2,0:T(1,128)S(1)}, f32[32,1,45,128]{3,1,2,0:T(1,128)}, u32[]{:S(2)}) copy-start(f32[32,1,45,128]{3,1,2,0:T(1,128)} %get-tuple-element.6) | copy-start | bytes 2211844
  89.0 4.4 %collective-permute-start.3 = (bf16[2,3,45,128]{3,1,2,0:T(4,128)(2,1)S(1)}, bf16[2,3,45,128]{3,1,2,0:T(4,128)(2,1)S(1)}, u32[]{:S(2)}, u32[]{:S(2)}) collective-permute-start(bf16[2,3,45,128]{3,1,2,0:T(4,128)(2,1)S(1)} %get-tuple-element.12), channel_id=1, source_target_pairs={{32,0},{64,32},{96,64},{128,96},{160,128},{192,160},{224,192},{256... | collective-permute-start | bytes 207368 | tf_op jit(solution)/shard_map/ppermute | solution.py:17
  90.9 7.1 %collective-permute-start.4 = (bf16[2,3,45,128]{3,1,2,0:T(4,128)(2,1)S(1)}, bf16[2,3,45,128]{3,1,2,0:T(4,128)(2,1)S(1)}, u32[]{:S(2)}, u32[]{:S(2)}) collective-permute-start(bf16[2,3,45,128]{3,1,2,0:T(4,128)(2,1)S(1)} %get-tuple-element.11), channel_id=1, source_target_pairs={{0,32},{32,64},{64,96},{96,128},{128,160},{160,192},{192,224},{224... | collective-permute-start | bytes 207368 | tf_op jit(solution)/shard_map/ppermute | solution.py:16

commit v3 on v1

--- a/solution.py
+++ b/solution.py
@@ -98,15 +98,21 @@
     first_row = lax.axis_index("lon") * per_device
     local_removal = lax.dynamic_slice_in_dim(removal, first_row, per_device, 0)
     spectrum = jnp.einsum(
-        "drjcl,djm->rcml", level_block, forward_table, preferred_element_type=jnp.float32
-    ).reshape(per_device, 2 * mode_count, levels)
-    weighted = (spectrum * local_removal[:, :, None]).astype(jnp.bfloat16)
+        "mdj,drjcl->mrcl",
+        forward_table.transpose(2, 0, 1),
+        level_block,
+        preferred_element_type=jnp.float32,
+    )
+    pair_removal = local_removal.reshape(per_device // 2, 2, 2 * mode_count).transpose(2, 0, 1)
+    weighted = (spectrum * pair_removal[:, :, :, None]).astype(jnp.bfloat16)
     correction = jnp.einsum(
-        "rcml,djm->drjcl",
-        weighted.reshape(per_device // 2, 2, 2 * mode_count, levels),
-        inverse_table,
+        "pm,mrcl->prcl",
+        inverse_table.reshape(blocks * (lon_local + 1), 2 * mode_count),
+        weighted,
         preferred_element_type=jnp.float32,
     ).astype(jnp.bfloat16)
+    correction = correction.reshape(blocks, lon_local + 1, per_device // 2, 2, levels)
+    correction = correction.transpose(0, 2, 1, 3, 4)
     correction = correction.reshape(blocks, per_device * (lon_local + 1), levels)
     returned = lax.all_to_all(correction, "lon", split_axis=0, concat_axis=0, tiled=True)
     return returned.reshape(row_count, lon_local + 1, 2, levels)
@@ -129,14 +135,30 @@
     zonal_courant = jnp.concatenate([courant[:, 0], east_column], axis=1)
     zonal_faces = (zonal_courant - correction[:, :, 0]).astype(jnp.bfloat16)
     meridional_filtered = (courant[:, 1] - correction[:, :lon_local, 1]).astype(jnp.bfloat16)
-    middle = (
-        tracers.astype(jnp.float32)
-        + ppm_change(tracer_wide, zonal_faces.astype(jnp.float32)[None], 2, lon_local)
-    ).astype(jnp.bfloat16)
-    meridional_stack = jnp.concatenate([middle, meridional_filtered[None]], axis=0)
-    meridional_band = padded(meridional_stack, (("lat", 1),), 3, False)
-    middle_wide = meridional_band[:tracer_count].astype(jnp.float32)
-    meridional_faces = meridional_band[tracer_count, 3 : rows_local + 4].astype(jnp.float32)
+    def zonal_step(low, high):
+        return (
+            tracers[:, low:high].astype(jnp.float32)
+            + ppm_change(
+                tracer_wide[:, low:high],
+                zonal_faces[low:high].astype(jnp.float32)[None],
+                2,
+                lon_local,
+            )
+        ).astype(jnp.bfloat16)
+
+    lat_size = lax.axis_size("lat")
+    southward = jnp.concatenate(
+        [zonal_step(0, 3), meridional_filtered[None, 0:1]], axis=1
+    )
+    northward = zonal_step(rows_local - 3, rows_local)
+    from_north = lax.ppermute(southward, "lat", [(i, i - 1) for i in range(1, lat_size)])
+    from_south = lax.ppermute(northward, "lat", [(i, i + 1) for i in range(lat_size - 1)])
+    middle = zonal_step(0, rows_local)
+    middle_wide = jnp.concatenate([from_south, middle, from_north[:, 0:3]], axis=1)
+    middle_wide = middle_wide.astype(jnp.float32)
+    meridional_faces = jnp.concatenate(
+        [meridional_filtered, from_north[0, 3:4]], axis=0
+    ).astype(jnp.float32)
     face_rows = lax.axis_index("lat") * rows_local + jnp.arange(rows_local + 1, dtype=jnp.int32)
     meridional_faces = jnp.where(face_rows[:, None, None] > 0, meridional_faces, 0.0)
     return (

time: 88.1 us -> 120 us (1.36)
  local copies, waits for them, and re-layouts: 8.14 us -> 35.9 us
  waiting for transfers between devices: 25.5 us -> 20.2 us
  matrix products: 5.84 us -> 9.46 us
  starting transfers between devices: 35.8 us -> 38.9 us
  other arithmetic: 12 us -> 14.1 us
    all_to_all x1, waiting for transfers between devices: 15.7 us -> 0.01 us  [filter_correction(): lax.all_to_all(outgoing, 'lon', split_axis=0, concat_axis=0, tiled=True)]
    all_to_all x1, waiting for transfers between devices: 1.21 us -> 16.6 us  [filter_correction(): lax.all_to_all(correction, 'lon', split_axis=0, concat_axis=0, tiled=True)]
    ppermute x2 -> x1, waiting for transfers between devices: 8.59 us -> 0.01 us  [padded(): before = lax.ppermute(last, axis, up)]
    neg x0 -> x2, local copies, waits for them, and re-layouts: none -> 8.55 us  [spectral_basis(): table = jnp.concatenate([cosine, -sine], axis=2)]
    sub x0 -> x2, local copies, waits for them, and re-layouts: none -> 6.56 us  [spectral_basis(): cosine = cc * cf - sc * sf]
    convert_element_type x1, local copies, waits for them, and re-layouts: 0.29 us -> 6.18 us  [filter_correction(): correction = jnp.einsum('pm,mrcl->prcl', inverse_table.reshape(blocks * (...]
    ppermute x0 -> x2, starting transfers between devices: none -> 4.33 us  [the longest x1 2.41 us: local(): lax.ppermute(northward, 'lat', [(i, i + 1) for i in range(lat_size - 1)])]
    ppermute x2 -> x1, starting transfers between devices: 6.1 us -> 1.92 us  [padded(): before = lax.ppermute(last, axis, up)]
  transfers between devices with their start and end apart: 7 -> 7, of which waited for: 4 -> 2; matrix products, arithmetic and copies ran while one was open for 13% -> 44% of each run, Pallas kernels for 0% -> 0%
where the time goes in v3:
time: 120 us; the launch traced here: 119 us
  starting transfers between devices  38.9 us (32%)
  local copies, waits for them, and re-layouts  35.9 us (30%)
  waiting for transfers between devices  20.2 us (17%)
  other arithmetic  14.1 us (12%)
  matrix products  9.46 us (8%)
    all_to_all x1, waiting for transfers between devices, filter_correction(): lax.all_to_all(correction, 'lon', split_axis=0, concat_axis=0, tiled=True)  16.6 us
    all_to_all x1, starting transfers between devices, filter_correction(): lax.all_to_all(outgoing, 'lon', split_axis=0, concat_axis=0, tiled=True)  13.2 us
    dot_general x1, matrix products, filter_correction(): jnp.einsum('pm,mrcl->prcl', inverse_table.reshape(blocks * (lon_local + 1...  9.46 us
    neg x2, local copies, waits for them, and re-layouts, spectral_basis(): table = jnp.concatenate([cosine, -sine], axis=2)  8.55 us
    ppermute x1, starting transfers between devices, local(): lax.ppermute(courant[:, 0, 0:1], 'lon', [(i, (i - 1) % lon_size) for i in...  7.23 us
    ppermute x1, starting transfers between devices, padded(): after = lax.ppermute(leading, axis, down)  7.1 us
    sub x2, local copies, waits for them, and re-layouts, spectral_basis(): cosine = cc * cf - sc * sf  6.56 us
    convert_element_type x1, local copies, waits for them, and re-layouts, filter_correction(): correction = jnp.einsum('pm,mrcl->prcl', inverse_table.reshape(blocks * (...  6.18 us
  transfers between devices with their start and end apart: 7, of which 2 were waited for; matrix products, arithmetic and copies ran while one was open for 44% of the time, Pallas kernels for 0%

profile of v3, /device:TPU:32, one launch (start us, length us, event | category | flops | bytes accessed | tf_op | source)
XLA Modules:
  0.0 118.9 jit_solution(12601642226475588039)
XLA Ops:
  0.0 1.6 %copy.88 = bf16[32,2,45,128]{3,0,1,2:T(8,128)(2,1)S(1)} copy(f32[32,2,45,128]{3,1,2,0:T(2,128)} %param.6) | data formatting | bytes 2211840 | tf_op args[1]
  1.6 1.2 copy.66
  2.8 13.2 %all-to-all-start = ((bf16[32,90,128]{2,1,0:T(8,128)(2,1)}), bf16[32,90,128]{2,1,0:T(8,128)(2,1)S(1)}, u32[]{:S(2)}, u32[]{:S(2)}) async-start(bf16[32,90,128]{2,1,0:T(8,128)(2,1)} %copy.66), calls=%async_computation | async-start | bytes 1572864 | tf_op jit(solution)/shard_map/all_to_all | solution.py:96
  16.0 0.6 fusion.126
  16.6 7.1 %collective-permute-start.2 = (bf16[1,32,3,128]{3,1,2,0:T(8,128)(2,1)}, bf16[1,32,3,128]{3,1,2,0:T(8,128)(2,1)}, u32[]{:S(2)}, u32[]{:S(2)}) collective-permute-start(bf16[1,32,3,128]{3,1,2,0:T(8,128)(2,1)} %get-tuple-element.24), channel_id=1, source_target_pairs={{1,0},{2,1},{3,2},{4,3},{5,4},{6,5},{7,6},{8,7},{9,8},{10,9},{11,1... | collective-permute-start | bytes 73736 | tf_op jit(solution)/shard_map/ppermute | solution.py:17
  23.7 1.9 %collective-permute-start.1 = (bf16[1,32,3,128]{3,1,2,0:T(8,128)(2,1)S(1)}, bf16[1,32,3,128]{3,1,2,0:T(8,128)(2,1)}, u32[]{:S(2)}, u32[]{:S(2)}) collective-permute-start(bf16[1,32,3,128]{3,1,2,0:T(8,128)(2,1)S(1)} %get-tuple-element.23), channel_id=1, source_target_pairs={{0,1},{1,2},{2,3},{3,4},{4,5},{5,6},{6,7},{7,8},{8,9},{9,10},{10,1... | collective-permute-start | bytes 73736 | tf_op jit(solution)/shard_map/ppermute | solution.py:16
  25.6 1.4 %slice.239 = f32[32,1,1,128]{3,1,2,0:T(1,128)} slice(f32[32,2,45,128]{3,1,2,0:T(2,128)} %param.6), slice={[0:32], [0:1], [0:1], [0:128]} | slice | bytes 32768 | tf_op jit(solution)/shard_map/slice | solution.py:132
  27.0 7.2 %collective-permute-start = (f32[32,1,128]{2,0,1:T(8,128)}, f32[32,1,128]{2,0,1:T(8,128)S(1)}, u32[]{:S(2)}, u32[]{:S(2)}) collective-permute-start(f32[32,1,128]{2,0,1:T(8,128)} %bitcast.1), channel_id=1, source_target_pairs={{0,31},{1,0},{2,1},{3,2},{4,3},{5,4},{6,5},{7,6},{8,7},{9,8},{10,9... | collective-permute-start | bytes 49160 | tf_op jit(solution)/shard_map/ppermute | solution.py:131
  34.2 0.6 fusion.63
  34.9 0.5 fusion.81
  35.4 3.0 %subtract_convert_fusion = (bf16[32,46,721]{2,1,0:T(8,128)(2,1)S(1)}, bf16[32,46,721]{2,1,0:T(8,128)(2,1)}) fusion(f32[46,721]{1,0:T(8,128)S(1)} %get-tuple-element.29, f32[32,721]{1,0:T(8,128)S(1)} %get-tuple-element.28, f32[46,721]{1,0:T(8,128)S(1)} %get-tuple-element.30, f32[32,721]{1,0:T(8,128)S(1)} %get-tuple-element.27), kind=kLoop, calls=%fused_computation.5 | loop fusion | flops 9551808 | bytes 4695152 | tf_op jit(solution)/shard_map/convert.7
  38.4 4.3 %neg.10 = bf16[1472,721]{1,0:T(8,128)(2,1)} reshape(bf16[32,46,721]{2,1,0:T(8,128)(2,1)} %get-tuple-element.18) | data formatting | bytes 4245248 | tf_op jit(solution)/shard_map/neg | solution.py:77
  42.7 4.3 %copy.64 = bf16[1472,721]{0,1:T(8,128)(2,1)} copy(bf16[1472,721]{1,0:T(8,128)(2,1)} %neg.10) | data formatting | bytes 4245248 | tf_op jit(solution)/shard_map/neg | solution.py:77
  46.9 2.4 %sub.178 = bf16[1472,721]{1,0:T(8,128)(2,1)} reshape(bf16[32,46,721]{2,1,0:T(8,128)(2,1)S(1)} %get-tuple-element.17) | data formatting | bytes 4245248 | tf_op jit(solution)/shard_map/sub | solution.py:75
  49.3 4.2 %copy.63 = bf16[1472,721]{0,1:T(8,128)(2,1)} copy(bf16[1472,721]{1,0:T(8,128)(2,1)} %sub.178) | data formatting | bytes 4245248 | tf_op jit(solution)/shard_map/sub | solution.py:75
  53.5 0.7 broadcast_subtract_fusion
  54.2 0.7 broadcast_compare_fusion
  54.8 1.0 select_subtract_fusion
  55.8 0.7 broadcast_in_dim.26
  56.5 1.7 %reshape.460 = f32[64,721]{1,0:T(8,128)} reshape(f32[32,2,721]{2,1,0:T(2,128)} %broadcast_in_dim.26) | data formatting | bytes 369152 | tf_op jit(solution)/shard_map/reshape | solution.py:94
  58.3 0.1 pad_maximum_fusion.2
  58.4 1.5 %multiply_bitcast_fusion = f32[1442,2]{0,1:T(2,128)} fusion(s32[]{:T(128)S(6)} %select_n.98, f32[64,721]{1,0:T(8,128)} %reshape.460, f32[1442]{0:T(1024)S(1)} %pad_maximum_fusion.2), kind=kLoop, calls=%fused_computation.170 | loop fusion | flops 5768 | bytes 201884 | tf_op jit(solution)/shard_map/mul | solution.py:107
  59.9 1.2 copy.67
  61.0 9.5 %fusion.13 = bf16[1472,2,128]{2,0,1:T(8,128)(2,1)} fusion(bf16[1472,721]{0,1:T(8,128)(2,1)} %copy.64, bf16[1472,721]{0,1:T(8,128)(2,1)} %copy.63, bf16[32,46,721]{2,1,0:T(8,128)(2,1)} %get-tuple-element.18, bf16[32,46,721]{2,1,0:T(8,128)(2,1)S(1)} %get-tuple-element.17, bf16[32,45,2,128]{3,0,2,1:T(8,128)(2,1)} %bitcast.160, f32[1442,2]{0,1:T(2,128)} %multiply_bitcast_fusion), kind=kOutput, calls=%fused_computation.12 | convolution fusion | flops 2167852800 | bytes 9992976 | tf_op jit(solution)/shard_map/pm,mrcl->prcl/dot_general | solution.py:108
  70.5 6.2 %copy.69 = bf16[1472,2,128]{2,1,0:T(2,128)(2,1)S(1)} copy(bf16[1472,2,128]{2,0,1:T(8,128)(2,1)} %fusion.13) | data formatting | bytes 1507328 | tf_op jit(solution)/shard_map/convert_element_type | solution.py:113
  76.7 1.1 reshape_transpose_reshape.3
  77.8 5.2 %all-to-all-start.1 = ((bf16[32,92,128]{2,1,0:T(8,128)(2,1)}), bf16[32,92,128]{2,1,0:T(8,128)(2,1)}, u32[]{:S(2)}, u32[]{:S(2)}) async-start(bf16[32,92,128]{2,1,0:T(8,128)(2,1)} %reshape_transpose_reshape.3), calls=%async_computation.1 | async-start | bytes 1572864 | tf_op jit(solution)/shard_map/all_to_all | solution.py:117
  83.0 2.0 %fusion.125 = (f32[32,1,45,128]{3,1,2,0:T(1,128)S(1)}, f32[32,1,45,128]{3,1,2,0:T(1,128)}) fusion(f32[32,2,45,128]{3,1,2,0:T(2,128)S(1)} %copy-done), kind=kLoop, calls=%fused_computation.182 | loop fusion | bytes 2949120 | tf_op jit(solution)/shard_map/slice | solution.py:135
  85.0 0.1 copy.89
  85.1 0.0 collective-permute-done.1
  85.1 0.8 maximum_convert_fusion.1
  85.9 0.1 fusion.73
  86.0 0.0 copy-start.3
  86.0 0.6 copy-done.3
  86.7 0.0 copy-done.5
  86.7 0.8 fusion.84
  87.5 0.1 fusion.38
  87.7 0.2 slice_subtract_fusion.5
  87.9 16.6 %all-to-all-done.1 = bf16[32,92,128]{2,1,0:T(8,128)(2,1)} async-done(((bf16[32,92,128]{2,1,0:T(8,128)(2,1)}), bf16[32,92,128]{2,1,0:T(8,128)(2,1)}, u32[]{:S(2)}, u32[]{:S(2)}) %all-to-all-start.1) | async-done | bytes 753696 | tf_op jit(solution)/shard_map/all_to_all | solution.py:117
  104.5 1.5 %copy.70 = bf16[32,92,128]{2,0,1:T(8,128)(2,1)S(1)} copy(bf16[32,92,128]{2,1,0:T(8,128)(2,1)} %all-to-all-done.1) | data formatting | bytes 1507328 | tf_op jit(solution)/shard_map/all_to_all | solution.py:117
  106.0 0.2 convert.18
  106.2 0.0 copy-start.4
  106.3 0.1 fusion.56
  106.5 0.2 fusion.51
  106.6 0.5 copy-done.4
  107.1 0.0 copy-done.6
  107.2 0.0 copy-done.7
  107.2 0.0 copy-done.8
  107.3 0.0 copy-done.9
  107.3 0.0 copy-done.10
  107.4 0.2 fusion.90
  107.6 0.1 fusion.117
  107.7 0.1 pad_maximum_fusion.1
  107.7 1.9 %collective-permute-start.3 = (bf16[1,4,45,128]{3,1,2,0:T(4,128)(2,1)S(1)}, bf16[1,4,45,128]{3,1,2,0:T(4,128)(2,1)S(1)}, u32[]{:S(2)}, u32[]{:S(2)}) collective-permute-start(bf16[1,4,45,128]{3,1,2,0:T(4,128)(2,1)S(1)} %pad_maximum_fusion.1), channel_id=1, source_target_pairs={{32,0},{64,32},{96,64},{128,96},{160,128},{192,160},{224,192},{256... | collective-permute-start | bytes 138248 | tf_op jit(solution)/shard_map/ppermute | solution.py:154
  109.7 2.4 %collective-permute-start.4 = (bf16[1,3,45,128]{3,1,2,0:T(4,128)(2,1)S(1)}, bf16[1,3,45,128]{3,1,2,0:T(4,128)(2,1)S(1)}, u32[]{:S(2)}, u32[]{:S(2)}) collective-permute-start(bf16[1,3,45,128]{3,1,2,0:T(4,128)(2,1)S(1)} %get-tuple-element.21), channel_id=1, source_target_pairs={{0,32},{32,64},{64,96},{96,128},{128,160},{160,192},{192,224},{224... | collective-permute-start | bytes 103688 | tf_op jit(solution)/shard_map/ppermute | solution.py:155
  112.1 0.5 fusion.49
  112.6 0.1 fusion.58
  112.7 3.6 %collective-permute-done.4 = bf16[1,3,45,128]{3,1,2,0:T(4,128)(2,1)S(1)} collective-permute-done((bf16[1,3,45,128]{3,1,2,0:T(4,128)(2,1)S(1)}, bf16[1,3,45,128]{3,1,2,0:T(4,128)(2,1)S(1)}, u32[]{:S(2)}, u32[]{:S(2)}) %collective-permute-start.4) | collective-permute-done | bytes 34592 | tf_op jit(solution)/shard_map/ppermute | solution.py:155
  116.2 0.0 collective-permute-done.3
  116.3 0.2 maximum_convert_fusion
  116.4 0.3 fusion.30
  116.8 0.3 slice_subtract_fusion.1
  117.2 0.9 fusion.23
  118.0 0.9 fusion.54
  (20 shorter events, 0.1 us)
Async XLA Ops:
  0.0 16.0 %copy-start.2 = (bf16[1,32,45,128]{3,1,2,0:T(8,128)(2,1)S(1)}, bf16[1,32,45,128]{3,1,2,0:T(8,128)(2,1)}, u32[]{:S(2)}) copy-start(bf16[1,32,45,128]{3,1,2,0:T(8,128)(2,1)} %param.5) | copy-start | bytes 1105924
  2.8 57.0 %all-to-all-start = ((bf16[32,90,128]{2,1,0:T(8,128)(2,1)}), bf16[32,90,128]{2,1,0:T(8,128)(2,1)S(1)}, u32[]{:S(2)}, u32[]{:S(2)}) async-start(bf16[32,90,128]{2,1,0:T(8,128)(2,1)} %copy.66), calls=%async_computation | async-start | bytes 1572864 | tf_op jit(solution)/shard_map/all_to_all | solution.py:96
  16.6 68.5 %collective-permute-start.2 = (bf16[1,32,3,128]{3,1,2,0:T(8,128)(2,1)}, bf16[1,32,3,128]{3,1,2,0:T(8,128)(2,1)}, u32[]{:S(2)}, u32[]{:S(2)}) collective-permute-start(bf16[1,32,3,128]{3,1,2,0:T(8,128)(2,1)} %get-tuple-element.24), channel_id=1, source_target_pairs={{1,0},{2,1},{3,2},{4,3},{5,4},{6,5},{7,6},{8,7},{9,8},{10,9},{11,1... | collective-permute-start | bytes 73736 | tf_op jit(solution)/shard_map/ppermute | solution.py:17
  23.7 61.4 %collective-permute-start.1 = (bf16[1,32,3,128]{3,1,2,0:T(8,128)(2,1)S(1)}, bf16[1,32,3,128]{3,1,2,0:T(8,128)(2,1)}, u32[]{:S(2)}, u32[]{:S(2)}) collective-permute-start(bf16[1,32,3,128]{3,1,2,0:T(8,128)(2,1)S(1)} %get-tuple-element.23), channel_id=1, source_target_pairs={{0,1},{1,2},{2,3},{3,4},{4,5},{5,6},{6,7},{7,8},{8,9},{9,10},{10,1... | collective-permute-start | bytes 73736 | tf_op jit(solution)/shard_map/ppermute | solution.py:16
  27.0 79.4 %collective-permute-start = (f32[32,1,128]{2,0,1:T(8,128)}, f32[32,1,128]{2,0,1:T(8,128)S(1)}, u32[]{:S(2)}, u32[]{:S(2)}) collective-permute-start(f32[32,1,128]{2,0,1:T(8,128)} %bitcast.1), channel_id=1, source_target_pairs={{0,31},{1,0},{2,1},{3,2},{4,3},{5,4},{6,5},{7,6},{8,7},{9,8},{10,9... | collective-permute-start | bytes 49160 | tf_op jit(solution)/shard_map/ppermute | solution.py:131
  70.5 12.5 %copy-start = (f32[32,2,45,128]{3,1,2,0:T(2,128)S(1)}, f32[32,2,45,128]{3,1,2,0:T(2,128)}, u32[]{:S(2)}) copy-start(f32[32,2,45,128]{3,1,2,0:T(2,128)} %param.6) | copy-start | bytes 4423684
  77.8 26.8 %all-to-all-start.1 = ((bf16[32,92,128]{2,1,0:T(8,128)(2,1)}), bf16[32,92,128]{2,1,0:T(8,128)(2,1)}, u32[]{:S(2)}, u32[]{:S(2)}) async-start(bf16[32,92,128]{2,1,0:T(8,128)(2,1)} %reshape_transpose_reshape.3), calls=%async_computation.1 | async-start | bytes 1572864 | tf_op jit(solution)/shard_map/all_to_all | solution.py:117
  86.0 0.6 copy-start.3
  86.0 0.7 copy-start.5
  104.5 1.8 %copy-start.1 = (f32[32,1,45,128]{3,1,2,0:T(1,128)S(1)}, f32[32,1,45,128]{3,1,2,0:T(1,128)}, u32[]{:S(2)}) copy-start(f32[32,1,45,128]{3,1,2,0:T(1,128)} %get-tuple-element.6) | copy-start | bytes 2211844
  106.2 0.9 copy-start.4
  106.2 0.9 copy-start.6
  106.2 1.0 copy-start.7
  106.3 1.0 copy-start.8
  106.3 1.1 copy-start.9
  106.3 1.1 copy-start.10
  107.7 8.5 %collective-permute-start.3 = (bf16[1,4,45,128]{3,1,2,0:T(4,128)(2,1)S(1)}, bf16[1,4,45,128]{3,1,2,0:T(4,128)(2,1)S(1)}, u32[]{:S(2)}, u32[]{:S(2)}) collective-permute-start(bf16[1,4,45,128]{3,1,2,0:T(4,128)(2,1)S(1)} %pad_maximum_fusion.1), channel_id=1, source_target_pairs={{32,0},{64,32},{96,64},{128,96},{160,128},{192,160},{224,192},{256... | collective-permute-start | bytes 138248 | tf_op jit(solution)/shard_map/ppermute | solution.py:154
  109.7 6.6 %collective-permute-start.4 = (bf16[1,3,45,128]{3,1,2,0:T(4,128)(2,1)S(1)}, bf16[1,3,45,128]{3,1,2,0:T(4,128)(2,1)S(1)}, u32[]{:S(2)}, u32[]{:S(2)}) collective-permute-start(bf16[1,3,45,128]{3,1,2,0:T(4,128)(2,1)S(1)} %get-tuple-element.21), channel_id=1, source_target_pairs={{0,32},{32,64},{64,96},{96,128},{128,160},{160,192},{192,224},{224... | collective-permute-start | bytes 103688 | tf_op jit(solution)/shard_map/ppermute | solution.py:155

commit v4 on v3

--- a/solution.py
+++ b/solution.py
@@ -98,21 +98,15 @@
     first_row = lax.axis_index("lon") * per_device
     local_removal = lax.dynamic_slice_in_dim(removal, first_row, per_device, 0)
     spectrum = jnp.einsum(
-        "mdj,drjcl->mrcl",
-        forward_table.transpose(2, 0, 1),
-        level_block,
-        preferred_element_type=jnp.float32,
-    )
-    pair_removal = local_removal.reshape(per_device // 2, 2, 2 * mode_count).transpose(2, 0, 1)
-    weighted = (spectrum * pair_removal[:, :, :, None]).astype(jnp.bfloat16)
+        "drjcl,djm->rcml", level_block, forward_table, preferred_element_type=jnp.float32
+    ).reshape(per_device, 2 * mode_count, levels)
+    weighted = (spectrum * local_removal[:, :, None]).astype(jnp.bfloat16)
     correction = jnp.einsum(
-        "pm,mrcl->prcl",
-        inverse_table.reshape(blocks * (lon_local + 1), 2 * mode_count),
-        weighted,
+        "rcml,djm->drjcl",
+        weighted.reshape(per_device // 2, 2, 2 * mode_count, levels),
+        inverse_table,
         preferred_element_type=jnp.float32,
     ).astype(jnp.bfloat16)
-    correction = correction.reshape(blocks, lon_local + 1, per_device // 2, 2, levels)
-    correction = correction.transpose(0, 2, 1, 3, 4)
     correction = correction.reshape(blocks, per_device * (lon_local + 1), levels)
     returned = lax.all_to_all(correction, "lon", split_axis=0, concat_axis=0, tiled=True)
     return returned.reshape(row_count, lon_local + 1, 2, levels)

time: 120 us -> 89.8 us (0.75)
  local copies, waits for them, and re-layouts: 35.9 us -> 9.86 us
  matrix products: 9.46 us -> 5.72 us
    neg x2 -> x0, local copies, waits for them, and re-layouts: 8.55 us -> none  [spectral_basis(): table = jnp.concatenate([cosine, -sine], axis=2)]
    sub x2 -> x0, local copies, waits for them, and re-layouts: 6.56 us -> none  [spectral_basis(): cosine = cc * cf - sc * sf]
    convert_element_type x1, local copies, waits for them, and re-layouts: 6.18 us -> 0.29 us  [filter_correction(): correction = jnp.einsum('rcml,djm->drjcl', weighted.reshape(per_device //...]
    convert_element_type x0 -> x1, other arithmetic: none -> 3.86 us  [filter_correction(): inverse_table = table.astype(jnp.bfloat16)]
    dot_general x1 -> x2, matrix products: 9.46 us -> 5.72 us  [the longest x1 4.27 us: filter_correction(): jnp.einsum('drjcl,djm->rcml', level_block, forward_table, preferred_eleme...]
    another operation x1 -> x0, other arithmetic: 3.01 us -> none
    sub x0 -> x1, other arithmetic: none -> 1.62 us  [spectral_basis(): cosine = cc * cf - sc * sf]
    reshape x1, local copies, waits for them, and re-layouts: 1.74 us -> 0.14 us  [filter_correction(): pair_factor = jnp.repeat(1.0 - row_factor, 2, axis=0)]
  transfers between devices with their start and end apart: 7 -> 7, of which waited for: 2 -> 2; matrix products, arithmetic and copies ran while one was open for 44% -> 25% of each run, Pallas kernels for 0% -> 0%
where the time goes in v4:
time: 89.8 us; the launch traced here: 89.4 us
  starting transfers between devices  38.9 us (43%)
  waiting for transfers between devices  21.1 us (23%)
  other arithmetic  13.4 us (15%)
  local copies, waits for them, and re-layouts  9.86 us (11%)
  matrix products  5.72 us (6%)
    all_to_all x1, waiting for transfers between devices, filter_correction(): lax.all_to_all(correction, 'lon', split_axis=0, concat_axis=0, tiled=True)  17.5 us
    all_to_all x1, starting transfers between devices, filter_correction(): lax.all_to_all(outgoing, 'lon', split_axis=0, concat_axis=0, tiled=True)  13.2 us
    ppermute x1, starting transfers between devices, padded(): after = lax.ppermute(leading, axis, down)  7.24 us
    ppermute x1, starting transfers between devices, local(): lax.ppermute(courant[:, 0, 0:1], 'lon', [(i, (i - 1) % lon_size) for i in...  7.1 us
    all_to_all x1, starting transfers between devices, filter_correction(): lax.all_to_all(correction, 'lon', split_axis=0, concat_axis=0, tiled=True)  5.13 us
    dot_general x1, matrix products, filter_correction(): jnp.einsum('drjcl,djm->rcml', level_block, forward_table, preferred_eleme...  4.27 us
    convert_element_type x1, other arithmetic, filter_correction(): inverse_table = table.astype(jnp.bfloat16)  3.86 us
    ppermute x1, waiting for transfers between devices, local(): lax.ppermute(northward, 'lat', [(i, i + 1) for i in range(lat_size - 1)])  3.57 us
  transfers between devices with their start and end apart: 7, of which 2 were waited for; matrix products, arithmetic and copies ran while one was open for 25% of the time, Pallas kernels for 0%

profile of v4, /device:TPU:32, one launch (start us, length us, event | category | flops | bytes accessed | tf_op | source)
XLA Modules:
  0.0 89.4 jit_solution(5010283094108816433)
XLA Ops:
  0.0 0.0 copy-start.10
  0.0 1.7 %copy.59 = bf16[32,2,45,128]{3,0,1,2:T(8,128)(2,1)S(1)} copy(f32[32,2,45,128]{3,1,2,0:T(2,128)} %param.6) | data formatting | bytes 2211840 | tf_op args[1]
  1.7 1.2 %copy.36 = bf16[32,90,128]{2,1,0:T(8,128)(2,1)} copy(bf16[32,90,128]{2,0,1:T(8,128)(2,1)S(1)} %bitcast.163) | data formatting | bytes 1474560 | tf_op jit(solution)/shard_map/reshape | solution.py:93
  3.0 13.2 %all-to-all-start = ((bf16[32,90,128]{2,1,0:T(8,128)(2,1)}), bf16[32,90,128]{2,1,0:T(8,128)(2,1)S(1)}, u32[]{:S(2)}, u32[]{:S(2)}) async-start(bf16[32,90,128]{2,1,0:T(8,128)(2,1)} %copy.36), calls=%async_computation | async-start | bytes 1572864 | tf_op jit(solution)/shard_map/all_to_all | solution.py:96
  16.1 0.6 slice.239
  16.8 7.1 %collective-permute-start = (f32[32,1,128]{2,0,1:T(8,128)}, f32[32,1,128]{2,0,1:T(8,128)S(1)}, u32[]{:S(2)}, u32[]{:S(2)}) collective-permute-start(f32[32,1,128]{2,0,1:T(8,128)} %bitcast.1), channel_id=1, source_target_pairs={{0,31},{1,0},{2,1},{3,2},{4,3},{5,4},{6,5},{7,6},{8,7},{9,8},{10,9... | collective-permute-start | bytes 49160 | tf_op jit(solution)/shard_map/ppermute | solution.py:125
  23.9 1.9 %collective-permute-start.1 = (bf16[1,32,3,128]{3,1,2,0:T(8,128)(2,1)S(1)}, bf16[1,32,3,128]{3,1,2,0:T(8,128)(2,1)S(1)}, u32[]{:S(2)}, u32[]{:S(2)}) collective-permute-start(bf16[1,32,3,128]{3,1,2,0:T(8,128)(2,1)S(1)} %get-tuple-element.23), channel_id=1, source_target_pairs={{0,1},{1,2},{2,3},{3,4},{4,5},{5,6},{6,7},{7,8},{8,9},{9,10},{10,1... | collective-permute-start | bytes 73736 | tf_op jit(solution)/shard_map/ppermute | solution.py:16
  25.8 7.2 %collective-permute-start.2 = (bf16[1,32,3,128]{3,1,2,0:T(8,128)(2,1)S(1)}, bf16[1,32,3,128]{3,1,2,0:T(8,128)(2,1)S(1)}, u32[]{:S(2)}, u32[]{:S(2)}) collective-permute-start(bf16[1,32,3,128]{3,1,2,0:T(8,128)(2,1)S(1)} %get-tuple-element.24), channel_id=1, source_target_pairs={{1,0},{2,1},{3,2},{4,3},{5,4},{6,5},{7,6},{8,7},{9,8},{10,9},{11,1... | collective-permute-start | bytes 73736 | tf_op jit(solution)/shard_map/ppermute | solution.py:17
  33.1 0.6 fusion.52
  33.7 0.0 copy-done.10
  33.7 0.1 pad_maximum_fusion.1
  33.8 0.1 select_subtract_fusion
  33.9 0.1 broadcast_in_dim.26
  34.0 0.1 reshape.440
  34.2 0.5 fusion.70
  34.7 1.6 %multiply_subtract_fusion = (bf16[32,46,721]{2,1,0:T(8,128)(2,1)S(1)}, bf16[32,46,721]{2,1,0:T(8,128)(2,1)S(1)}) fusion(f32[46,721]{1,0:T(8,128)S(1)} %get-tuple-element.29, f32[32,721]{1,0:T(8,128)S(1)} %get-tuple-element.28, f32[46,721]{1,0:T(8,128)S(1)} %get-tuple-element.30, f32[32,721]{1,0:T(8,128)S(1)} %get-tuple-element.27), kind=kLoop, calls=%fused_computation.6 | loop fusion | flops 9551808 | bytes 4695152 | tf_op jit(solution)/shard_map/sub | solution.py:75
  36.3 3.9 %maximum_convert_fusion = bf16[32,46,1442]{2,1,0:T(8,128)(2,1)} fusion(bf16[32,46,721]{2,1,0:T(8,128)(2,1)S(1)} %get-tuple-element.18, bf16[32,46,721]{2,1,0:T(8,128)(2,1)S(1)} %get-tuple-element.17), kind=kLoop, calls=%fused_computation | loop fusion | flops 8490496 | bytes 8490496 | tf_op jit(solution)/shard_map/convert_element_type | solution.py:91
  40.1 0.1 fusion.110
  40.2 0.0 all-to-all-done
  40.2 0.3 copy.37
  40.5 0.0 slice-start.1
  40.5 4.3 %fusion.6 = bf16[2,1442,128,1]{2,1,0,3:T(8,128)(2,1)S(1)} fusion(bf16[32,46,1442]{2,1,0:T(8,128)(2,1)} %maximum_convert_fusion, bf16[32,45,2,128]{3,0,2,1:T(8,128)(2,1)S(1)} %bitcast.165, f32[2,1442]{1,0:T(2,128)S(1)} %fusion.110), kind=kOutput, calls=%fused_computation.10 | convolution fusion | flops 1063896064 | bytes 5732368 | tf_op jit(solution)/shard_map/drjcl,djm->rcml/dot_general | solution.py:100
  44.8 0.0 slice-done
  44.8 0.0 slice-done.1
  44.8 1.4 %fusion.7 = bf16[32,46,2,128]{3,1,2,0:T(8,128)(2,1)S(1)} fusion(bf16[2,1442,128,1]{2,1,0,3:T(8,128)(2,1)S(1)} %fusion.6, bf16[32,46,1442]{2,1,0:T(8,128)(2,1)S(1)} %bitcast.160), kind=kOutput, calls=%fused_computation.17 | convolution fusion | flops 1087160320 | bytes 5737216 | tf_op jit(solution)/shard_map/rcml,djm->drjcl/dot_general | solution.py:104
  46.3 0.3 copy.39
  46.6 1.2 %copy.40 = bf16[32,92,128]{2,1,0:T(8,128)(2,1)} copy(bf16[32,92,128]{2,0,1:T(8,128)(2,1)S(1)} %bitcast.161) | data formatting | bytes 1507328 | tf_op jit(solution)/shard_map/reshape | solution.py:110
  47.8 5.1 %all-to-all-start.1 = ((bf16[32,92,128]{2,1,0:T(8,128)(2,1)}), bf16[32,92,128]{2,1,0:T(8,128)(2,1)}, u32[]{:S(2)}, u32[]{:S(2)}) async-start(bf16[32,92,128]{2,1,0:T(8,128)(2,1)} %copy.40), calls=%async_computation.1 | async-start | bytes 1572864 | tf_op jit(solution)/shard_map/all_to_all | solution.py:111
  53.0 2.0 %fusion.113 = (f32[32,1,45,128]{3,1,2,0:T(1,128)S(1)}, f32[32,1,45,128]{3,1,2,0:T(1,128)}) fusion(f32[32,2,45,128]{3,1,2,0:T(2,128)S(1)} %copy-done), kind=kLoop, calls=%fused_computation.178 | loop fusion | bytes 2949120 | tf_op jit(solution)/shard_map/slice | solution.py:129
  55.0 0.1 copy.60
  55.1 0.0 collective-permute-done.1
  55.1 0.0 collective-permute-done.2
  55.1 0.1 maximum_convert_fusion.2
  55.2 0.1 fusion.62
  55.3 0.0 copy-start.2
  55.3 0.6 copy-done.2
  55.9 0.8 fusion.73
  56.7 0.1 fusion.29
  56.9 0.2 slice_subtract_fusion.5
  57.1 17.5 %all-to-all-done.1 = bf16[32,92,128]{2,1,0:T(8,128)(2,1)} async-done(((bf16[32,92,128]{2,1,0:T(8,128)(2,1)}), bf16[32,92,128]{2,1,0:T(8,128)(2,1)}, u32[]{:S(2)}, u32[]{:S(2)}) %all-to-all-start.1) | async-done | bytes 753696 | tf_op jit(solution)/shard_map/all_to_all | solution.py:111
  74.6 1.5 %copy.41 = bf16[32,92,128]{2,0,1:T(8,128)(2,1)S(1)} copy(bf16[32,92,128]{2,1,0:T(8,128)(2,1)} %all-to-all-done.1) | data formatting | bytes 1507328 | tf_op jit(solution)/shard_map/all_to_all | solution.py:111
  76.1 0.2 convert.2
  76.3 1.2 %fusion.45 = bf16[32,45,128]{2,0,1:T(8,128)(2,1)S(1)} fusion(f32[32,46,2,128]{3,0,2,1:T(8,128)S(1)} %convert.2, f32[32,1,45,128]{3,1,2,0:T(1,128)} %get-tuple-element.6), kind=kLoop, calls=%fused_computation.67 | loop fusion | flops 368640 | bytes 1843200 | tf_op jit(solution)/shard_map/convert_element_type | solution.py:131
  77.6 0.0 collective-permute-done
  77.6 0.2 fusion.41
  77.7 0.0 copy-done.3
  77.7 0.0 copy-done.4
  77.7 0.0 copy-done.5
  77.8 0.0 copy-done.6
  77.8 0.0 copy-done.7
  77.8 0.2 fusion.79
  78.0 0.1 fusion.106
  78.1 0.1 pad_maximum_fusion
  78.1 1.9 %collective-permute-start.3 = (bf16[1,4,45,128]{3,1,2,0:T(4,128)(2,1)S(1)}, bf16[1,4,45,128]{3,1,2,0:T(4,128)(2,1)S(1)}, u32[]{:S(2)}, u32[]{:S(2)}) collective-permute-start(bf16[1,4,45,128]{3,1,2,0:T(4,128)(2,1)S(1)} %pad_maximum_fusion), channel_id=1, source_target_pairs={{32,0},{64,32},{96,64},{128,96},{160,128},{192,160},{224,192},{256... | collective-permute-start | bytes 138248 | tf_op jit(solution)/shard_map/ppermute | solution.py:148
  80.1 2.4 %collective-permute-start.4 = (bf16[1,3,45,128]{3,1,2,0:T(4,128)(2,1)S(1)}, bf16[1,3,45,128]{3,1,2,0:T(4,128)(2,1)S(1)}, u32[]{:S(2)}, u32[]{:S(2)}) collective-permute-start(bf16[1,3,45,128]{3,1,2,0:T(4,128)(2,1)S(1)} %get-tuple-element.21), channel_id=1, source_target_pairs={{0,32},{32,64},{64,96},{96,128},{128,160},{160,192},{192,224},{224... | collective-permute-start | bytes 103688 | tf_op jit(solution)/shard_map/ppermute | solution.py:149
  82.5 0.5 fusion.39
  83.0 0.1 fusion.47
  83.1 3.6 %collective-permute-done.4 = bf16[1,3,45,128]{3,1,2,0:T(4,128)(2,1)S(1)} collective-permute-done((bf16[1,3,45,128]{3,1,2,0:T(4,128)(2,1)S(1)}, bf16[1,3,45,128]{3,1,2,0:T(4,128)(2,1)S(1)}, u32[]{:S(2)}, u32[]{:S(2)}) %collective-permute-start.4) | collective-permute-done | bytes 34592 | tf_op jit(solution)/shard_map/ppermute | solution.py:149
  86.7 0.0 collective-permute-done.3
  86.7 0.2 maximum_convert_fusion.1
  86.9 0.3 fusion.21
  87.2 0.3 slice_subtract_fusion.1
  87.6 0.9 fusion.14
  88.4 0.9 %fusion.43 = bf16[1,32,45,128]{3,1,2,0:T(8,128)(2,1)} fusion(f32[1,33,45,128]{3,1,2,0:T(8,128)S(1)} %fusion.14, bf16[1,32,45,128]{3,1,2,0:T(8,128)(2,1)S(1)} %fusion.47), kind=kLoop, calls=%fused_computation.64 | loop fusion | flops 737280 | bytes 2211840 | tf_op jit(solution)/shard_map/convert_element_type | solution.py:160
  (23 shorter events, 0.1 us)
Async XLA Ops:
  0.0 16.1 %copy-start = (f32[32,2,45,128]{3,1,2,0:T(2,128)S(1)}, f32[32,2,45,128]{3,1,2,0:T(2,128)}, u32[]{:S(2)}) copy-start(f32[32,2,45,128]{3,1,2,0:T(2,128)} %param.6) | copy-start | bytes 4423684
  0.0 23.9 %copy-start.1 = (bf16[1,32,45,128]{3,1,2,0:T(8,128)(2,1)S(1)}, bf16[1,32,45,128]{3,1,2,0:T(8,128)(2,1)}, u32[]{:S(2)}) copy-start(bf16[1,32,45,128]{3,1,2,0:T(8,128)(2,1)} %param.5) | copy-start | bytes 1105924
  0.0 33.7 %copy-start.9 = (s32[32]{0:T(128)S(1)}, s32[32]{0:T(128)}, u32[]{:S(2)}) copy-start(s32[32]{0:T(128)} %param.7) | copy-start | bytes 388
  0.0 33.7 %copy-start.10 = (s32[32]{0:T(128)S(1)}, s32[32]{0:T(128)}, u32[]{:S(2)}) copy-start(s32[32]{0:T(128)} %param.8) | copy-start | bytes 388
  0.0 33.8 %copy-start.8 = (f32[32,721]{1,0:T(8,128)S(1)}, f32[32,721]{1,0:T(8,128)}, u32[]{:S(2)}) copy-start(f32[32,721]{1,0:T(8,128)} %param.9) | copy-start | bytes 276868
  3.0 37.3 %all-to-all-start = ((bf16[32,90,128]{2,1,0:T(8,128)(2,1)}), bf16[32,90,128]{2,1,0:T(8,128)(2,1)S(1)}, u32[]{:S(2)}, u32[]{:S(2)}) async-start(bf16[32,90,128]{2,1,0:T(8,128)(2,1)} %copy.36), calls=%async_computation | async-start | bytes 1572864 | tf_op jit(solution)/shard_map/all_to_all | solution.py:96
  16.8 60.8 %collective-permute-start = (f32[32,1,128]{2,0,1:T(8,128)}, f32[32,1,128]{2,0,1:T(8,128)S(1)}, u32[]{:S(2)}, u32[]{:S(2)}) collective-permute-start(f32[32,1,128]{2,0,1:T(8,128)} %bitcast.1), channel_id=1, source_target_pairs={{0,31},{1,0},{2,1},{3,2},{4,3},{5,4},{6,5},{7,6},{8,7},{9,8},{10,9... | collective-permute-start | bytes 49160 | tf_op jit(solution)/shard_map/ppermute | solution.py:125
  23.9 31.2 %collective-permute-start.1 = (bf16[1,32,3,128]{3,1,2,0:T(8,128)(2,1)S(1)}, bf16[1,32,3,128]{3,1,2,0:T(8,128)(2,1)S(1)}, u32[]{:S(2)}, u32[]{:S(2)}) collective-permute-start(bf16[1,32,3,128]{3,1,2,0:T(8,128)(2,1)S(1)} %get-tuple-element.23), channel_id=1, source_target_pairs={{0,1},{1,2},{2,3},{3,4},{4,5},{5,6},{6,7},{7,8},{8,9},{9,10},{10,1... | collective-permute-start | bytes 73736 | tf_op jit(solution)/shard_map/ppermute | solution.py:16
  25.8 29.3 %collective-permute-start.2 = (bf16[1,32,3,128]{3,1,2,0:T(8,128)(2,1)S(1)}, bf16[1,32,3,128]{3,1,2,0:T(8,128)(2,1)S(1)}, u32[]{:S(2)}, u32[]{:S(2)}) collective-permute-start(bf16[1,32,3,128]{3,1,2,0:T(8,128)(2,1)S(1)} %get-tuple-element.24), channel_id=1, source_target_pairs={{1,0},{2,1},{3,2},{4,3},{5,4},{6,5},{7,6},{8,7},{9,8},{10,9},{11,1... | collective-permute-start | bytes 73736 | tf_op jit(solution)/shard_map/ppermute | solution.py:17
  40.2 4.6 %slice-start = ((s8[4718592]{0:T(1024)(128)(4,1)}), s8[4194304]{0:T(1024)(128)(4,1)S(1)}, s32[]{:S(2)}) async-start(s8[4718592]{0:T(1024)(128)(4,1)} %bitcast.159), calls=%async_computation.2 | async-start | bytes 8388608
  40.5 4.3 %slice-start.1 = ((s8[4718592]{0:T(1024)(128)(4,1)}), s8[524288]{0:T(1024)(128)(4,1)S(1)}, s32[]{:S(2)}) async-start(s8[4718592]{0:T(1024)(128)(4,1)} %bitcast.159), calls=%async_computation.3 | async-start | bytes 1048576
  47.8 26.7 %all-to-all-start.1 = ((bf16[32,92,128]{2,1,0:T(8,128)(2,1)}), bf16[32,92,128]{2,1,0:T(8,128)(2,1)}, u32[]{:S(2)}, u32[]{:S(2)}) async-start(bf16[32,92,128]{2,1,0:T(8,128)(2,1)} %copy.40), calls=%async_computation.1 | async-start | bytes 1572864 | tf_op jit(solution)/shard_map/all_to_all | solution.py:111
  55.3 0.6 copy-start.2
  74.6 3.2 %copy-start.3 = (f32[1,3,48,128]{3,1,2,0:T(4,128)S(1)}, f32[1,3,48,128]{3,1,2,0:T(4,128)}, u32[]{:S(2)}) copy-start(f32[1,3,48,128]{3,1,2,0:T(4,128)} %copy-done.2) | copy-start | bytes 221188
  74.6 3.2 %copy-start.4 = (f32[1,3,47,128]{3,1,2,0:T(4,128)S(1)}, f32[1,3,47,128]{3,1,2,0:T(4,128)}, u32[]{:S(2)}) copy-start(f32[1,3,47,128]{3,1,2,0:T(4,128)} %get-tuple-element.9) | copy-start | bytes 216580
  74.6 3.2 %copy-start.5 = (f32[1,3,47,128]{3,1,2,0:T(4,128)S(1)}, f32[1,3,47,128]{3,1,2,0:T(4,128)}, u32[]{:S(2)}) copy-start(f32[1,3,47,128]{3,1,2,0:T(4,128)} %get-tuple-element.10) | copy-start | bytes 216580
  74.6 3.2 %copy-start.6 = (f32[1,3,47,128]{3,1,2,0:T(4,128)S(1)}, f32[1,3,47,128]{3,1,2,0:T(4,128)}, u32[]{:S(2)}) copy-start(f32[1,3,47,128]{3,1,2,0:T(4,128)} %get-tuple-element.25) | copy-start | bytes 216580
  74.6 3.2 %copy-start.7 = (f32[1,3,47,128]{3,1,2,0:T(4,128)S(1)}, f32[1,3,47,128]{3,1,2,0:T(4,128)}, u32[]{:S(2)}) copy-start(f32[1,3,47,128]{3,1,2,0:T(4,128)} %get-tuple-element.26) | copy-start | bytes 216580
  78.1 8.5 %collective-permute-start.3 = (bf16[1,4,45,128]{3,1,2,0:T(4,128)(2,1)S(1)}, bf16[1,4,45,128]{3,1,2,0:T(4,128)(2,1)S(1)}, u32[]{:S(2)}, u32[]{:S(2)}) collective-permute-start(bf16[1,4,45,128]{3,1,2,0:T(4,128)(2,1)S(1)} %pad_maximum_fusion), channel_id=1, source_target_pairs={{32,0},{64,32},{96,64},{128,96},{160,128},{192,160},{224,192},{256... | collective-permute-start | bytes 138248 | tf_op jit(solution)/shard_map/ppermute | solution.py:148
  80.1 6.6 %collective-permute-start.4 = (bf16[1,3,45,128]{3,1,2,0:T(4,128)(2,1)S(1)}, bf16[1,3,45,128]{3,1,2,0:T(4,128)(2,1)S(1)}, u32[]{:S(2)}, u32[]{:S(2)}) collective-permute-start(bf16[1,3,45,128]{3,1,2,0:T(4,128)(2,1)S(1)} %get-tuple-element.21), channel_id=1, source_target_pairs={{0,32},{32,64},{64,96},{96,128},{128,160},{160,192},{192,224},{224... | collective-permute-start | bytes 103688 | tf_op jit(solution)/shard_map/ppermute | solution.py:149

commit v5 on v1

--- a/solution.py
+++ b/solution.py
@@ -87,7 +87,7 @@
     mode_count = row_factor.shape[1]
     per_device = 2 * row_count // blocks
     table, mode_weight = spectral_basis(blocks, lon_local, lon_local + 1, mode_count)
-    forward_table = table[:, :lon_local].astype(jnp.bfloat16)
+    forward_table = spectral_basis(blocks, lon_local, lon_local, mode_count)[0].astype(jnp.bfloat16)
     inverse_table = table.astype(jnp.bfloat16)
     outgoing = courant.transpose(0, 2, 1, 3).astype(jnp.bfloat16)
     outgoing = outgoing.reshape(blocks, (2 * row_count // blocks) * lon_local, levels)
@@ -100,7 +100,7 @@
     spectrum = jnp.einsum(
         "drjcl,djm->rcml", level_block, forward_table, preferred_element_type=jnp.float32
     ).reshape(per_device, 2 * mode_count, levels)
-    weighted = (spectrum * local_removal[:, :, None]).astype(jnp.bfloat16)
+    weighted = lax.optimization_barrier((spectrum * local_removal[:, :, None]).astype(jnp.bfloat16))
     correction = jnp.einsum(
         "rcml,djm->drjcl",
         weighted.reshape(per_device // 2, 2, 2 * mode_count, levels),

time: 88.1 us -> 88.7 us (level)
  waiting for transfers between devices: 25.5 us -> 21.4 us
  other arithmetic: 12 us -> 15.2 us
  local copies, waits for them, and re-layouts: 8.14 us -> 9.69 us
    another operation x0 -> x2, other arithmetic: none -> 7.81 us
    all_to_all x1, waiting for transfers between devices: 15.7 us -> 11.4 us  [filter_correction(): lax.all_to_all(outgoing, 'lon', split_axis=0, concat_axis=0, tiled=True)]
    convert_element_type x1 -> x0, other arithmetic: 3.86 us -> none  [filter_correction(): inverse_table = table.astype(jnp.bfloat16)]
    sin x1 -> x2, other arithmetic: 0.63 us -> 2.64 us  [spectral_basis(): cf, sf = (jnp.cos(fine_angle)[None], jnp.sin(fine_angle)[None])]
    sub x1 -> x0, other arithmetic: 1.62 us -> none  [spectral_basis(): cosine = cc * cf - sc * sf]
    unnamed x18 -> x22, local copies, waits for them, and re-layouts: 2.6 us -> 4.17 us
    select_n x2, other arithmetic: 2.46 us -> 1.34 us  [ppm_change(): face_flux = jnp.where(courant_faces > 0, upwind_plus, upwind_minus)]
  transfers between devices with their start and end apart: 7 -> 7, of which waited for: 4 -> 4; matrix products, arithmetic and copies ran while one was open for 13% -> 17% of each run, Pallas kernels for 0% -> 0%
where the time goes in v5:
time: 88.7 us; the launch traced here: 88.2 us
  starting transfers between devices  35.6 us (40%)
  waiting for transfers between devices  21.4 us (24%)
  other arithmetic  15.2 us (17%)
  local copies, waits for them, and re-layouts  9.69 us (11%)
  matrix products  5.92 us (7%)
    all_to_all x1, starting transfers between devices, filter_correction(): lax.all_to_all(outgoing, 'lon', split_axis=0, concat_axis=0, tiled=True)  13.2 us
    all_to_all x1, waiting for transfers between devices, filter_correction(): lax.all_to_all(outgoing, 'lon', split_axis=0, concat_axis=0, tiled=True)  11.4 us
    ppermute x2, waiting for transfers between devices, padded(): before = lax.ppermute(last, axis, up)  8.75 us
    another operation x2, other arithmetic  7.81 us
    ppermute x2, starting transfers between devices, padded(): after = lax.ppermute(leading, axis, down)  7.39 us
    ppermute x2, starting transfers between devices, padded(): before = lax.ppermute(last, axis, up)  6.1 us
    all_to_all x1, starting transfers between devices, filter_correction(): lax.all_to_all(correction, 'lon', split_axis=0, concat_axis=0, tiled=True)  5.13 us
    dot_general x1, matrix products, filter_correction(): jnp.einsum('drjcl,djm->rcml', level_block, forward_table, preferred_eleme...  4.39 us
  transfers between devices with their start and end apart: 7, of which 4 were waited for; matrix products, arithmetic and copies ran while one was open for 17% of the time, Pallas kernels for 0%

profile of v5, /device:TPU:32, one launch (start us, length us, event | category | flops | bytes accessed | tf_op | source)
XLA Modules:
  0.0 88.2 jit_solution(10627644013777894078)
XLA Ops:
  0.0 1.6 %copy.40 = bf16[32,2,45,128]{3,0,1,2:T(8,128)(2,1)S(1)} copy(f32[32,2,45,128]{3,1,2,0:T(2,128)} %param.6) | data formatting | bytes 2211840 | tf_op args[1]
  1.6 0.0 copy-start.8
  1.6 0.0 copy-start.9
  1.6 0.0 copy-start.7
  1.6 1.2 %copy.19 = bf16[32,90,128]{2,1,0:T(8,128)(2,1)} copy(bf16[32,90,128]{2,0,1:T(8,128)(2,1)S(1)} %bitcast.68) | data formatting | bytes 1474560 | tf_op jit(solution)/shard_map/reshape | solution.py:93
  2.8 13.2 %all-to-all-start = ((bf16[32,90,128]{2,1,0:T(8,128)(2,1)}), bf16[32,90,128]{2,1,0:T(8,128)(2,1)S(1)}, u32[]{:S(2)}, u32[]{:S(2)}) async-start(bf16[32,90,128]{2,1,0:T(8,128)(2,1)} %copy.19), calls=%async_computation | async-start | bytes 1572864 | tf_op jit(solution)/shard_map/all_to_all | solution.py:96
  16.0 1.4 %fusion.56 = (f32[45,721]{1,0:T(8,128)}, f32[45,721]{1,0:T(8,128)}) fusion(), kind=kLoop, calls=%fused_computation.97 | loop fusion | flops 292005 | bytes 259560 | tf_op jit(solution)/shard_map/sin | solution.py:74
  17.3 1.3 %fusion.60 = (f32[46,721]{1,0:T(8,128)S(1)}, f32[46,721]{1,0:T(8,128)}) fusion(), kind=kLoop, calls=%fused_computation.102 | loop fusion | flops 298494 | bytes 265328 | tf_op jit(solution)/shard_map/sin | solution.py:74
  18.6 0.0 copy-done.8
  18.6 0.0 copy-done.9
  18.7 0.1 pad_maximum_fusion.7
  18.7 0.0 copy-done.7
  18.7 0.1 select_subtract_fusion
  18.8 0.1 broadcast_in_dim.20
  18.9 0.1 reshape.344
  19.1 0.5 fusion.69
  19.6 0.0 copy-start.6
  19.6 4.1 %subtract_convert_fusion = (bf16[32,45,721]{2,1,0:T(8,128)(2,1)S(1)}, bf16[32,45,721]{2,1,0:T(8,128)(2,1)}) fusion(f32[45,721]{1,0:T(8,128)} %get-tuple-element.23, f32[32,721]{1,0:T(8,128)S(1)} %get-tuple-element.20, f32[45,721]{1,0:T(8,128)} %get-tuple-element.24, f32[32,721]{1,0:T(8,128)S(1)} %get-tuple-element.19), kind=kLoop, calls=%fused_computation.9 | loop fusion | flops 9344160 | bytes 4597096 | tf_op jit(solution)/shard_map/convert.1
  23.6 0.0 copy-done.6
  23.6 3.7 %subtract_convert_fusion.1 = (bf16[32,46,721]{2,1,0:T(8,128)(2,1)}, bf16[32,46,721]{2,1,0:T(8,128)(2,1)}) fusion(f32[46,721]{1,0:T(8,128)S(1)} %get-tuple-element.21, f32[32,721]{1,0:T(8,128)S(1)} %get-tuple-element.20, f32[46,721]{1,0:T(8,128)S(1)} %copy-done.6, f32[32,721]{1,0:T(8,128)S(1)} %get-tuple-element.19), kind=kLoop, calls=%fused_computation.11 | loop fusion | flops 9551808 | bytes 4695152 | tf_op jit(solution)/shard_map/convert.3
  27.4 0.1 fusion.73
  27.5 11.4 %all-to-all-done = bf16[32,90,128]{2,1,0:T(8,128)(2,1)S(1)} async-done(((bf16[32,90,128]{2,1,0:T(8,128)(2,1)}), bf16[32,90,128]{2,1,0:T(8,128)(2,1)S(1)}, u32[]{:S(2)}, u32[]{:S(2)}) %all-to-all-start) | async-done | bytes 737312 | tf_op jit(solution)/shard_map/all_to_all | solution.py:96
  38.9 0.3 copy.20
  39.1 0.0 copy-start.3
  39.2 0.0 copy-start.4
  39.2 4.4 %fusion.8 = bf16[2,1442,128]{2,1,0:T(8,128)(2,1)S(1)} fusion(bf16[32,45,721]{2,1,0:T(8,128)(2,1)} %get-tuple-element.14, bf16[32,45,721]{2,1,0:T(8,128)(2,1)S(1)} %get-tuple-element.13, bf16[32,45,2,128]{3,0,2,1:T(8,128)(2,1)S(1)} %bitcast.69, f32[2,1442]{1,0:T(2,128)S(1)} %fusion.73), kind=kOutput, calls=%fused_computation.14 | convolution fusion | flops 1072201984 | bytes 5640080 | tf_op jit(solution)/shard_map/drjcl,djm->rcml/dot_general | solution.py:100
  43.6 0.0 copy-done.3
  43.6 0.0 copy-done.4
  43.6 1.5 %fusion.9 = bf16[32,46,2,128]{3,1,2,0:T(8,128)(2,1)S(1)} fusion(bf16[32,46,721]{2,1,0:T(8,128)(2,1)S(1)} %copy-done.4, bf16[32,46,721]{2,1,0:T(8,128)(2,1)S(1)} %copy-done.3, bf16[2,1442,128]{2,1,0:T(8,128)(2,1)S(1)} %fusion.8), kind=kOutput, calls=%fused_computation.21 | convolution fusion | flops 1095650816 | bytes 5737216 | tf_op jit(solution)/shard_map/rcml,djm->drjcl/dot_general | solution.py:104
  45.1 0.0 copy-start
  45.1 0.3 copy.22
  45.4 1.2 %copy.23 = bf16[32,92,128]{2,1,0:T(8,128)(2,1)} copy(bf16[32,92,128]{2,0,1:T(8,128)(2,1)S(1)} %bitcast.65) | data formatting | bytes 1507328 | tf_op jit(solution)/shard_map/reshape | solution.py:110
  46.6 5.1 %all-to-all-start.1 = ((bf16[32,92,128]{2,1,0:T(8,128)(2,1)}), bf16[32,92,128]{2,1,0:T(8,128)(2,1)S(1)}, u32[]{:S(2)}, u32[]{:S(2)}) async-start(bf16[32,92,128]{2,1,0:T(8,128)(2,1)} %copy.23), calls=%async_computation.1 | async-start | bytes 1572864 | tf_op jit(solution)/shard_map/all_to_all | solution.py:111
  51.8 0.0 copy-done.5
  51.8 3.7 %collective-permute-start.1 = (bf16[1,32,3,128]{3,1,2,0:T(8,128)(2,1)S(1)}, bf16[1,32,3,128]{3,1,2,0:T(8,128)(2,1)S(1)}, u32[]{:S(2)}, u32[]{:S(2)}) collective-permute-start(bf16[1,32,3,128]{3,1,2,0:T(8,128)(2,1)S(1)} %get-tuple-element.17), channel_id=1, source_target_pairs={{0,1},{1,2},{2,3},{3,4},{4,5},{5,6},{6,7},{7,8},{8,9},{9,10},{10,1... | collective-permute-start | bytes 73736 | tf_op jit(solution)/shard_map/ppermute | solution.py:16
  55.5 5.5 %collective-permute-start.2 = (bf16[1,32,3,128]{3,1,2,0:T(8,128)(2,1)S(1)}, bf16[1,32,3,128]{3,1,2,0:T(8,128)(2,1)S(1)}, u32[]{:S(2)}, u32[]{:S(2)}) collective-permute-start(bf16[1,32,3,128]{3,1,2,0:T(8,128)(2,1)S(1)} %get-tuple-element.18), channel_id=1, source_target_pairs={{1,0},{2,1},{3,2},{4,3},{5,4},{6,5},{7,6},{8,7},{9,8},{10,9},{11,1... | collective-permute-start | bytes 73736 | tf_op jit(solution)/shard_map/ppermute | solution.py:17
  61.0 0.0 copy-done
  61.0 3.8 %collective-permute-start = (f32[32,1,128]{2,0,1:T(8,128)S(1)}, f32[32,1,128]{2,0,1:T(8,128)S(1)}, u32[]{:S(2)}, u32[]{:S(2)}) collective-permute-start(f32[32,1,128]{2,0,1:T(8,128)S(1)} %bitcast.71), channel_id=1, source_target_pairs={{0,31},{1,0},{2,1},{3,2},{4,3},{5,4},{6,5},{7,6},{8,7},{9,8},{10,9... | collective-permute-start | bytes 49160 | tf_op jit(solution)/shard_map/ppermute | solution.py:125
  64.8 2.0 %fusion.78 = (f32[32,1,45,128]{3,1,2,0:T(1,128)S(1)}, f32[32,1,45,128]{3,1,2,0:T(1,128)}) fusion(f32[32,2,45,128]{3,1,2,0:T(2,128)S(1)} %copy-done), kind=kLoop, calls=%fused_computation.133 | loop fusion | bytes 2949120 | tf_op jit(solution)/shard_map/slice | solution.py:129
  66.8 1.0 %copy.41 = f32[32,1,45,128]{3,0,2,1:T(8,128)} copy(f32[32,1,45,128]{3,1,2,0:T(1,128)S(1)} %get-tuple-element.5) | data formatting | bytes 1474560
  67.8 4.1 %collective-permute-done.1 = bf16[1,32,3,128]{3,1,2,0:T(8,128)(2,1)S(1)} collective-permute-done((bf16[1,32,3,128]{3,1,2,0:T(8,128)(2,1)S(1)}, bf16[1,32,3,128]{3,1,2,0:T(8,128)(2,1)S(1)}, u32[]{:S(2)}, u32[]{:S(2)}) %collective-permute-start.1) | collective-permute-done | bytes 24608 | tf_op jit(solution)/shard_map/ppermute | solution.py:16
  71.9 0.0 collective-permute-done.2
  71.9 0.1 maximum_convert_fusion
  72.0 0.1 fusion.29
  72.1 0.2 slice_subtract_fusion.5
  72.4 1.2 %all-to-all-done.1 = bf16[32,92,128]{2,1,0:T(8,128)(2,1)S(1)} async-done(((bf16[32,92,128]{2,1,0:T(8,128)(2,1)}), bf16[32,92,128]{2,1,0:T(8,128)(2,1)S(1)}, u32[]{:S(2)}, u32[]{:S(2)}) %all-to-all-start.1) | async-done | bytes 753696 | tf_op jit(solution)/shard_map/all_to_all | solution.py:111
  73.6 0.3 copy.24
  73.9 0.2 convert.17
  74.1 0.0 collective-permute-done
  74.1 0.6 copy-done.2
  74.7 0.5 fusion.39
  75.2 0.1 fusion.48
  75.3 1.0 %copy-done.1 = f32[32,1,45,128]{3,1,2,0:T(1,128)S(1)} copy-done((f32[32,1,45,128]{3,1,2,0:T(1,128)S(1)}, f32[32,1,45,128]{3,1,2,0:T(1,128)}, u32[]{:S(2)}) %copy-start.1) | copy-done | bytes 737304
  76.3 0.1 fusion.46
  76.4 0.1 pad_maximum_fusion.5
  76.5 1.9 %collective-permute-start.3 = (bf16[2,3,45,128]{3,1,2,0:T(4,128)(2,1)S(1)}, bf16[2,3,45,128]{3,1,2,0:T(4,128)(2,1)S(1)}, u32[]{:S(2)}, u32[]{:S(2)}) collective-permute-start(bf16[2,3,45,128]{3,1,2,0:T(4,128)(2,1)S(1)} %get-tuple-element.12), channel_id=1, source_target_pairs={{32,0},{64,32},{96,64},{128,96},{160,128},{192,160},{224,192},{256... | collective-permute-start | bytes 207368 | tf_op jit(solution)/shard_map/ppermute | solution.py:17
  78.4 2.4 %collective-permute-start.4 = (bf16[2,3,45,128]{3,1,2,0:T(4,128)(2,1)S(1)}, bf16[2,3,45,128]{3,1,2,0:T(4,128)(2,1)S(1)}, u32[]{:S(2)}, u32[]{:S(2)}) collective-permute-start(bf16[2,3,45,128]{3,1,2,0:T(4,128)(2,1)S(1)} %get-tuple-element.11), channel_id=1, source_target_pairs={{0,32},{32,64},{64,96},{96,128},{128,160},{160,192},{192,224},{224... | collective-permute-start | bytes 207368 | tf_op jit(solution)/shard_map/ppermute | solution.py:16
  80.9 0.0 collective-permute-done.3
  80.9 4.6 %collective-permute-done.4 = bf16[2,3,45,128]{3,1,2,0:T(4,128)(2,1)S(1)} collective-permute-done((bf16[2,3,45,128]{3,1,2,0:T(4,128)(2,1)S(1)}, bf16[2,3,45,128]{3,1,2,0:T(4,128)(2,1)S(1)}, u32[]{:S(2)}, u32[]{:S(2)}) %collective-permute-start.4) | collective-permute-done | bytes 69152 | tf_op jit(solution)/shard_map/ppermute | solution.py:16
  85.5 0.2 fusion.49
  85.7 0.3 fusion.21
  86.0 0.3 slice_subtract_fusion.1
  86.4 0.9 fusion.14
  87.2 0.9 %fusion.44 = bf16[1,32,45,128]{3,1,2,0:T(8,128)(2,1)} fusion(f32[1,33,45,128]{3,1,2,0:T(8,128)S(1)} %fusion.14, bf16[1,32,45,128]{3,1,2,0:T(8,128)(2,1)S(1)} %fusion.48), kind=kLoop, calls=%fused_computation.68 | loop fusion | flops 737280 | bytes 2211840 | tf_op jit(solution)/shard_map/convert_element_type | solution.py:144
  (10 shorter events, 0.1 us)
Async XLA Ops:
  1.6 17.1 %copy-start.8 = (s32[32]{0:T(128)S(1)}, s32[32]{0:T(128)}, u32[]{:S(2)}) copy-start(s32[32]{0:T(128)} %param.7) | copy-start | bytes 388
  1.6 17.1 %copy-start.9 = (s32[32]{0:T(128)S(1)}, s32[32]{0:T(128)}, u32[]{:S(2)}) copy-start(s32[32]{0:T(128)} %param.8) | copy-start | bytes 388
  1.6 17.1 %copy-start.7 = (f32[32,721]{1,0:T(8,128)S(1)}, f32[32,721]{1,0:T(8,128)}, u32[]{:S(2)}) copy-start(f32[32,721]{1,0:T(8,128)} %param.9) | copy-start | bytes 276868
  2.8 36.1 %all-to-all-start = ((bf16[32,90,128]{2,1,0:T(8,128)(2,1)}), bf16[32,90,128]{2,1,0:T(8,128)(2,1)S(1)}, u32[]{:S(2)}, u32[]{:S(2)}) async-start(bf16[32,90,128]{2,1,0:T(8,128)(2,1)} %copy.19), calls=%async_computation | async-start | bytes 1572864 | tf_op jit(solution)/shard_map/all_to_all | solution.py:96
  19.6 4.1 %copy-start.6 = (f32[46,721]{1,0:T(8,128)S(1)}, f32[46,721]{1,0:T(8,128)}, u32[]{:S(2)}) copy-start(f32[46,721]{1,0:T(8,128)} %get-tuple-element.22) | copy-start | bytes 397996
  39.1 4.4 %copy-start.3 = (bf16[32,46,721]{2,1,0:T(8,128)(2,1)S(1)}, bf16[32,46,721]{2,1,0:T(8,128)(2,1)}, u32[]{:S(2)}) copy-start(bf16[32,46,721]{2,1,0:T(8,128)(2,1)} %get-tuple-element.15) | copy-start | bytes 6367876
  39.2 4.4 %copy-start.4 = (bf16[32,46,721]{2,1,0:T(8,128)(2,1)S(1)}, bf16[32,46,721]{2,1,0:T(8,128)(2,1)}, u32[]{:S(2)}) copy-start(bf16[32,46,721]{2,1,0:T(8,128)(2,1)} %get-tuple-element.16) | copy-start | bytes 6367876
  45.1 6.7 %copy-start.5 = (bf16[1,32,45,128]{3,1,2,0:T(8,128)(2,1)S(1)}, bf16[1,32,45,128]{3,1,2,0:T(8,128)(2,1)}, u32[]{:S(2)}) copy-start(bf16[1,32,45,128]{3,1,2,0:T(8,128)(2,1)} %param.5) | copy-start | bytes 1105924
  45.1 15.9 %copy-start = (f32[32,2,45,128]{3,1,2,0:T(2,128)S(1)}, f32[32,2,45,128]{3,1,2,0:T(2,128)}, u32[]{:S(2)}) copy-start(f32[32,2,45,128]{3,1,2,0:T(2,128)} %param.6) | copy-start | bytes 4423684
  46.6 27.0 %all-to-all-start.1 = ((bf16[32,92,128]{2,1,0:T(8,128)(2,1)}), bf16[32,92,128]{2,1,0:T(8,128)(2,1)S(1)}, u32[]{:S(2)}, u32[]{:S(2)}) async-start(bf16[32,92,128]{2,1,0:T(8,128)(2,1)} %copy.23), calls=%async_computation.1 | async-start | bytes 1572864 | tf_op jit(solution)/shard_map/all_to_all | solution.py:111
  51.8 20.1 %collective-permute-start.1 = (bf16[1,32,3,128]{3,1,2,0:T(8,128)(2,1)S(1)}, bf16[1,32,3,128]{3,1,2,0:T(8,128)(2,1)S(1)}, u32[]{:S(2)}, u32[]{:S(2)}) collective-permute-start(bf16[1,32,3,128]{3,1,2,0:T(8,128)(2,1)S(1)} %get-tuple-element.17), channel_id=1, source_target_pairs={{0,1},{1,2},{2,3},{3,4},{4,5},{5,6},{6,7},{7,8},{8,9},{9,10},{10,1... | collective-permute-start | bytes 73736 | tf_op jit(solution)/shard_map/ppermute | solution.py:16
  55.5 16.4 %collective-permute-start.2 = (bf16[1,32,3,128]{3,1,2,0:T(8,128)(2,1)S(1)}, bf16[1,32,3,128]{3,1,2,0:T(8,128)(2,1)S(1)}, u32[]{:S(2)}, u32[]{:S(2)}) collective-permute-start(bf16[1,32,3,128]{3,1,2,0:T(8,128)(2,1)S(1)} %get-tuple-element.18), channel_id=1, source_target_pairs={{1,0},{2,1},{3,2},{4,3},{5,4},{6,5},{7,6},{8,7},{9,8},{10,9},{11,1... | collective-permute-start | bytes 73736 | tf_op jit(solution)/shard_map/ppermute | solution.py:17
  61.0 13.1 %collective-permute-start = (f32[32,1,128]{2,0,1:T(8,128)S(1)}, f32[32,1,128]{2,0,1:T(8,128)S(1)}, u32[]{:S(2)}, u32[]{:S(2)}) collective-permute-start(f32[32,1,128]{2,0,1:T(8,128)S(1)} %bitcast.71), channel_id=1, source_target_pairs={{0,31},{1,0},{2,1},{3,2},{4,3},{5,4},{6,5},{7,6},{8,7},{9,8},{10,9... | collective-permute-start | bytes 49160 | tf_op jit(solution)/shard_map/ppermute | solution.py:125
  73.6 1.1 %copy-start.2 = (f32[32,1,45,128]{3,0,2,1:T(8,128)S(1)}, f32[32,1,45,128]{3,0,2,1:T(8,128)}, u32[]{:S(2)}) copy-start(f32[32,1,45,128]{3,0,2,1:T(8,128)} %copy.41) | copy-start | bytes 2211844
  75.2 1.1 %copy-start.1 = (f32[32,1,45,128]{3,1,2,0:T(1,128)S(1)}, f32[32,1,45,128]{3,1,2,0:T(1,128)}, u32[]{:S(2)}) copy-start(f32[32,1,45,128]{3,1,2,0:T(1,128)} %get-tuple-element.6) | copy-start | bytes 2211844
  76.5 4.4 %collective-permute-start.3 = (bf16[2,3,45,128]{3,1,2,0:T(4,128)(2,1)S(1)}, bf16[2,3,45,128]{3,1,2,0:T(4,128)(2,1)S(1)}, u32[]{:S(2)}, u32[]{:S(2)}) collective-permute-start(bf16[2,3,45,128]{3,1,2,0:T(4,128)(2,1)S(1)} %get-tuple-element.12), channel_id=1, source_target_pairs={{32,0},{64,32},{96,64},{128,96},{160,128},{192,160},{224,192},{256... | collective-permute-start | bytes 207368 | tf_op jit(solution)/shard_map/ppermute | solution.py:17
  78.4 7.1 %collective-permute-start.4 = (bf16[2,3,45,128]{3,1,2,0:T(4,128)(2,1)S(1)}, bf16[2,3,45,128]{3,1,2,0:T(4,128)(2,1)S(1)}, u32[]{:S(2)}, u32[]{:S(2)}) collective-permute-start(bf16[2,3,45,128]{3,1,2,0:T(4,128)(2,1)S(1)} %get-tuple-element.11), channel_id=1, source_target_pairs={{0,32},{32,64},{64,96},{96,128},{128,160},{160,192},{192,224},{224... | collective-permute-start | bytes 207368 | tf_op jit(solution)/shard_map/ppermute | solution.py:16

commit v6 on v5

--- a/solution.py
+++ b/solution.py
@@ -81,32 +81,45 @@
     return table, jnp.concatenate([mode_weight, mode_weight], axis=0)
 
 
+def spectral_basis_by_mode(blocks, block_len, mode_count):
+    total_lon = blocks * block_len
+    scale = 2.0 * math.pi / total_lon
+    mode_index = jnp.arange(mode_count, dtype=jnp.int32)[:, None]
+    coarse = jnp.arange(blocks, dtype=jnp.int32)[None, :]
+    fine = jnp.arange(block_len, dtype=jnp.int32)[None, :]
+    coarse_angle = ((block_len * coarse * mode_index) % total_lon).astype(jnp.float32) * scale
+    fine_angle = ((fine * mode_index) % total_lon).astype(jnp.float32) * scale
+    cc, sc = jnp.cos(coarse_angle)[:, :, None], jnp.sin(coarse_angle)[:, :, None]
+    cf, sf = jnp.cos(fine_angle)[:, None, :], jnp.sin(fine_angle)[:, None, :]
+    cosine = cc * cf - sc * sf
+    sine = sc * cf + cc * sf
+    return jnp.concatenate([cosine, -sine], axis=0).reshape(2 * mode_count, total_lon)
+
+
 def filter_correction(courant, row_factor):
     row_count, _, lon_local, levels = courant.shape
     blocks = lax.axis_size("lon")
     mode_count = row_factor.shape[1]
     per_device = 2 * row_count // blocks
+    rows_here = per_device // 2
     table, mode_weight = spectral_basis(blocks, lon_local, lon_local + 1, mode_count)
-    forward_table = spectral_basis(blocks, lon_local, lon_local, mode_count)[0].astype(jnp.bfloat16)
-    inverse_table = table.astype(jnp.bfloat16)
+    forward_table = spectral_basis_by_mode(blocks, lon_local, mode_count).astype(jnp.bfloat16)
+    inverse_table = table.reshape(blocks * (lon_local + 1), 2 * mode_count).astype(jnp.bfloat16)
     outgoing = courant.transpose(0, 2, 1, 3).astype(jnp.bfloat16)
-    outgoing = outgoing.reshape(blocks, (2 * row_count // blocks) * lon_local, levels)
+    outgoing = outgoing.reshape(blocks, rows_here * lon_local * 2, levels)
     pair_factor = jnp.repeat(1.0 - row_factor, 2, axis=0)
     removal = jnp.concatenate([pair_factor, pair_factor], axis=1) * mode_weight[None, :]
     arrived = lax.all_to_all(outgoing, "lon", split_axis=0, concat_axis=0, tiled=True)
-    level_block = arrived.reshape(blocks, per_device // 2, lon_local, 2, levels)
+    gathered = arrived.reshape(blocks, rows_here, lon_local, 2 * levels).transpose(0, 2, 1, 3)
+    gathered = gathered.reshape(blocks * lon_local, rows_here * 2 * levels)
     first_row = lax.axis_index("lon") * per_device
     local_removal = lax.dynamic_slice_in_dim(removal, first_row, per_device, 0)
-    spectrum = jnp.einsum(
-        "drjcl,djm->rcml", level_block, forward_table, preferred_element_type=jnp.float32
-    ).reshape(per_device, 2 * mode_count, levels)
-    weighted = lax.optimization_barrier((spectrum * local_removal[:, :, None]).astype(jnp.bfloat16))
-    correction = jnp.einsum(
-        "rcml,djm->drjcl",
-        weighted.reshape(per_device // 2, 2, 2 * mode_count, levels),
-        inverse_table,
-        preferred_element_type=jnp.float32,
-    ).astype(jnp.bfloat16)
+    spread_removal = jnp.repeat(local_removal.T, levels, axis=1)
+    spectrum = jnp.dot(forward_table, gathered, preferred_element_type=jnp.float32)
+    weighted = lax.optimization_barrier((spectrum * spread_removal).astype(jnp.bfloat16))
+    correction = jnp.dot(inverse_table, weighted, preferred_element_type=jnp.float32)
+    correction = correction.astype(jnp.bfloat16).reshape(blocks, lon_local + 1, rows_here, 2 * levels)
+    correction = correction.transpose(0, 2, 1, 3)
     correction = correction.reshape(blocks, per_device * (lon_local + 1), levels)
     returned = lax.all_to_all(correction, "lon", split_axis=0, concat_axis=0, tiled=True)
     return returned.reshape(row_count, lon_local + 1, 2, levels)

time: 88.7 us -> 99.4 us (1.12)
  the two profiles are of different devices: /device:TPU:32 before, /device:TPU:38 now
where the time goes in v6:
time: 99.4 us; the launch traced here: 98.8 us
  starting transfers between devices  36.1 us (36%)
  local copies, waits for them, and re-layouts  28.4 us (29%)
  waiting for transfers between devices  14.7 us (15%)
  other arithmetic  12.6 us (13%)
  matrix products  6.67 us (7%)
    all_to_all x1, starting transfers between devices, filter_correction(): lax.all_to_all(outgoing, 'lon', split_axis=0, concat_axis=0, tiled=True)  13.4 us
    all_to_all x1, starting transfers between devices, filter_correction(): lax.all_to_all(correction, 'lon', split_axis=0, concat_axis=0, tiled=True)  9.77 us
    ppermute x2, waiting for transfers between devices, padded(): before = lax.ppermute(last, axis, up)  8.83 us
    another operation x2, other arithmetic  6.03 us
    unnamed x22, local copies, waits for them, and re-layouts  6.01 us
    ppermute x2, starting transfers between devices, padded(): before = lax.ppermute(last, axis, up)  5.78 us
    dot_general x1, matrix products, filter_correction(): jnp.dot(forward_table, gathered, preferred_element_type=jnp.float32)  5.19 us
    ppermute x2, starting transfers between devices, padded(): after = lax.ppermute(leading, axis, down)  4.39 us
  transfers between devices with their start and end apart: 7, of which 4 were waited for; matrix products, arithmetic and copies ran while one was open for 32% of the time, Pallas kernels for 0%

profile of v6, /device:TPU:38, one launch (start us, length us, event | category | flops | bytes accessed | tf_op | source)
XLA Modules:
  0.0 98.8 jit_solution(13242600210075464553)
XLA Ops:
  0.0 1.6 %copy.52 = bf16[32,2,45,128]{3,0,1,2:T(8,128)(2,1)S(1)} copy(f32[32,2,45,128]{3,1,2,0:T(2,128)} %param.6) | data formatting | bytes 2211840 | tf_op args[1]
  1.6 1.2 %copy.37 = bf16[32,90,128]{2,1,0:T(8,128)(2,1)} copy(bf16[32,90,128]{2,0,1:T(8,128)(2,1)S(1)} %bitcast.46) | data formatting | bytes 1474560 | tf_op jit(solution)/shard_map/reshape | solution.py:109
  2.8 13.4 %all-to-all-start = ((bf16[32,90,128]{2,1,0:T(8,128)(2,1)}), bf16[32,90,128]{2,1,0:T(8,128)(2,1)S(1)}, u32[]{:S(2)}, u32[]{:S(2)}) async-start(bf16[32,90,128]{2,1,0:T(8,128)(2,1)} %copy.37), calls=%async_computation | async-start | bytes 1572864 | tf_op jit(solution)/shard_map/all_to_all | solution.py:112
  16.3 0.0 copy-done.8
  16.3 0.1 select_subtract_fusion
  16.4 0.1 broadcast_in_dim.22
  16.5 0.1 reshape.414
  16.6 0.1 pad_maximum_fusion.7
  16.7 0.1 multiply_bitcast_fusion
  16.8 0.3 copy.38
  17.1 3.3 %broadcast_in_dim.25 = f32[1442,2,128]{2,1,0:T(2,128)S(1)} broadcast(f32[1442,2]{1,0:T(8,128)S(1)} %copy.38), dimensions={0,1} | broadcast | bytes 1488144 | tf_op jit(solution)/shard_map/broadcast_in_dim | solution.py:117
  20.4 0.6 pad.33
  21.0 1.2 %copy.46 = f32[181,8,2,128]{3,1,2,0:T(8,128)} copy(f32[181,8,2,128]{3,2,1,0:T(2,128)S(1)} %bitcast.43) | data formatting | bytes 2965504
  22.3 0.6 fusion.61
  22.9 0.5 fusion.76
  23.4 3.0 %subtract_convert_fusion = (bf16[721,32,45]{0,2,1:T(8,128)(2,1)S(1)}, bf16[721,32,45]{0,2,1:T(8,128)(2,1)}) fusion(f32[721,45]{0,1:T(8,128)S(1)} %get-tuple-element.23, f32[721,32]{0,1:T(8,128)S(1)} %get-tuple-element.22, f32[721,45]{0,1:T(8,128)S(1)} %get-tuple-element.24, f32[721,32]{0,1:T(8,128)S(1)} %get-tuple-element.21), kind=kLoop, calls=%fused_computation.1 | loop fusion | flops 9344160 | bytes 4597096 | tf_op jit(solution)/shard_map/convert.4
  26.4 4.3 %neg.17 = bf16[721,1440]{0,1:T(8,128)(2,1)} reshape(bf16[721,32,45]{0,2,1:T(8,128)(2,1)} %get-tuple-element.16) | data formatting | bytes 4152960 | tf_op jit(solution)/shard_map/neg | solution.py:96
  30.7 2.4 %sub.124 = bf16[721,1440]{0,1:T(8,128)(2,1)} reshape(bf16[721,32,45]{0,2,1:T(8,128)(2,1)S(1)} %get-tuple-element.15) | data formatting | bytes 4152960 | tf_op jit(solution)/shard_map/sub | solution.py:94
  33.1 0.6 fusion.65
  33.8 0.5 fusion.80
  34.3 3.0 %subtract_convert_fusion.1 = (bf16[32,46,721]{2,1,0:T(8,128)(2,1)S(1)}, bf16[32,46,721]{2,1,0:T(8,128)(2,1)}) fusion(f32[46,721]{1,0:T(8,128)S(1)} %get-tuple-element.25, f32[32,721]{1,0:T(8,128)S(1)} %get-tuple-element.20, f32[46,721]{1,0:T(8,128)S(1)} %get-tuple-element.26, f32[32,721]{1,0:T(8,128)S(1)} %get-tuple-element.19), kind=kLoop, calls=%fused_computation.3 | loop fusion | flops 9551808 | bytes 4695152 | tf_op jit(solution)/shard_map/convert.8
  37.3 4.3 %neg.15 = bf16[1472,721]{1,0:T(8,128)(2,1)} reshape(bf16[32,46,721]{2,1,0:T(8,128)(2,1)} %get-tuple-element.14) | data formatting | bytes 4245248 | tf_op jit(solution)/shard_map/neg | solution.py:77
  41.6 2.4 %sub.122 = bf16[1472,721]{1,0:T(8,128)(2,1)} reshape(bf16[32,46,721]{2,1,0:T(8,128)(2,1)S(1)} %get-tuple-element.13) | data formatting | bytes 4245248 | tf_op jit(solution)/shard_map/sub | solution.py:75
  44.0 0.0 all-to-all-done
  44.0 0.3 reshape_transpose_reshape.6
  44.3 0.0 copy-start.3
  44.3 0.0 copy-start.4
  44.3 5.2 %fusion.14 = bf16[1442,256]{1,0:T(8,128)(2,1)S(1)} fusion(f32[1442,256]{1,0:T(8,128)} %bitcast.47, bf16[1440,256]{1,0:T(8,128)(2,1)S(1)} %reshape_transpose_reshape.6, bf16[721,1440]{0,1:T(8,128)(2,1)} %neg.17, bf16[721,1440]{0,1:T(8,128)(2,1)} %sub.124), kind=kOutput, calls=%fused_computation.14 | convolution fusion | flops 1072201984 | bytes 7105152 | tf_op jit(solution)/shard_map/dot_general | solution.py:118
  49.5 1.5 %fusion.11 = bf16[1472,256]{1,0:T(8,128)(2,1)S(1)} fusion(bf16[1442,256]{1,0:T(8,128)(2,1)S(1)} %fusion.14, bf16[1472,721]{1,0:T(8,128)(2,1)S(1)} %copy-done.3, bf16[1472,721]{1,0:T(8,128)(2,1)S(1)} %copy-done.4), kind=kOutput, calls=%fused_computation.13 | convolution fusion | flops 1095650816 | bytes 5737216 | tf_op jit(solution)/shard_map/dot_general | solution.py:120
  51.0 0.0 copy-start.5
  51.0 0.0 copy-start
  51.1 1.2 %reshape_transpose_reshape.7 = bf16[32,92,128]{2,1,0:T(8,128)(2,1)} reshape(bf16[1472,256]{1,0:T(8,128)(2,1)S(1)} %fusion.11) | data formatting | bytes 1507328 | tf_op jit(solution)/shard_map/reshape;transpose;reshape | solution.py:123
  52.3 9.8 %all-to-all-start.1 = ((bf16[32,92,128]{2,1,0:T(8,128)(2,1)}), bf16[32,92,128]{2,1,0:T(8,128)(2,1)S(1)}, u32[]{:S(2)}, u32[]{:S(2)}) async-start(bf16[32,92,128]{2,1,0:T(8,128)(2,1)} %reshape_transpose_reshape.7), calls=%async_computation.1 | async-start | bytes 1572864 | tf_op jit(solution)/shard_map/all_to_all | solution.py:124
  62.0 0.0 copy-done.5
  62.1 3.4 %collective-permute-start.1 = (bf16[1,32,3,128]{3,1,2,0:T(8,128)(2,1)S(1)}, bf16[1,32,3,128]{3,1,2,0:T(8,128)(2,1)S(1)}, u32[]{:S(2)}, u32[]{:S(2)}) collective-permute-start(bf16[1,32,3,128]{3,1,2,0:T(8,128)(2,1)S(1)} %get-tuple-element.17), channel_id=1, source_target_pairs={{0,1},{1,2},{2,3},{3,4},{4,5},{5,6},{6,7},{7,8},{8,9},{9,10},{10,1... | collective-permute-start | bytes 73736 | tf_op jit(solution)/shard_map/ppermute | solution.py:16
  65.4 2.5 %collective-permute-start.2 = (bf16[1,32,3,128]{3,1,2,0:T(8,128)(2,1)S(1)}, bf16[1,32,3,128]{3,1,2,0:T(8,128)(2,1)S(1)}, u32[]{:S(2)}, u32[]{:S(2)}) collective-permute-start(bf16[1,32,3,128]{3,1,2,0:T(8,128)(2,1)S(1)} %get-tuple-element.18), channel_id=1, source_target_pairs={{1,0},{2,1},{3,2},{4,3},{5,4},{6,5},{7,6},{8,7},{9,8},{10,9},{11,1... | collective-permute-start | bytes 73736 | tf_op jit(solution)/shard_map/ppermute | solution.py:17
  68.0 2.8 %collective-permute-start = (f32[32,1,128]{2,0,1:T(8,128)S(1)}, f32[32,1,128]{2,0,1:T(8,128)S(1)}, u32[]{:S(2)}, u32[]{:S(2)}) collective-permute-start(f32[32,1,128]{2,0,1:T(8,128)S(1)} %bitcast.49), channel_id=1, source_target_pairs={{0,31},{1,0},{2,1},{3,2},{4,3},{5,4},{6,5},{7,6},{8,7},{9,8},{10,9... | collective-permute-start | bytes 49160 | tf_op jit(solution)/shard_map/ppermute | solution.py:138
  70.7 2.0 %fusion.89 = (f32[32,1,45,128]{3,1,2,0:T(1,128)S(1)}, f32[32,1,45,128]{3,1,2,0:T(1,128)}) fusion(f32[32,2,45,128]{3,1,2,0:T(2,128)S(1)} %copy-done), kind=kLoop, calls=%fused_computation.139 | loop fusion | bytes 2949120 | tf_op jit(solution)/shard_map/slice | solution.py:142
  72.8 1.0 copy.53
  73.7 4.2 %collective-permute-done.1 = bf16[1,32,3,128]{3,1,2,0:T(8,128)(2,1)S(1)} collective-permute-done((bf16[1,32,3,128]{3,1,2,0:T(8,128)(2,1)S(1)}, bf16[1,32,3,128]{3,1,2,0:T(8,128)(2,1)S(1)}, u32[]{:S(2)}, u32[]{:S(2)}) %collective-permute-start.1) | collective-permute-done | bytes 24608 | tf_op jit(solution)/shard_map/ppermute | solution.py:16
  77.9 2.7 %collective-permute-done.2 = bf16[1,32,3,128]{3,1,2,0:T(8,128)(2,1)S(1)} collective-permute-done((bf16[1,32,3,128]{3,1,2,0:T(8,128)(2,1)S(1)}, bf16[1,32,3,128]{3,1,2,0:T(8,128)(2,1)S(1)}, u32[]{:S(2)}, u32[]{:S(2)}) %collective-permute-start.2) | collective-permute-done | bytes 24608 | tf_op jit(solution)/shard_map/ppermute | solution.py:17
  80.6 0.1 maximum_convert_fusion
  80.7 0.1 fusion.36
  80.9 0.2 slice_subtract_fusion.5
  81.1 3.1 %all-to-all-done.1 = bf16[32,92,128]{2,1,0:T(8,128)(2,1)S(1)} async-done(((bf16[32,92,128]{2,1,0:T(8,128)(2,1)}), bf16[32,92,128]{2,1,0:T(8,128)(2,1)S(1)}, u32[]{:S(2)}, u32[]{:S(2)}) %all-to-all-start.1) | async-done | bytes 753696 | tf_op jit(solution)/shard_map/all_to_all | solution.py:124
  84.2 0.3 copy.39
  84.5 0.2 convert.21
  84.7 0.0 collective-permute-done
  84.7 0.6 copy-done.2
  85.3 0.5 fusion.45
  85.8 0.0 copy-start.1
  85.8 0.1 fusion.53
  85.9 1.0 copy-done.1
  86.9 0.1 fusion.51
  87.0 0.1 pad_maximum_fusion.5
  87.1 1.9 %collective-permute-start.3 = (bf16[2,3,45,128]{3,1,2,0:T(4,128)(2,1)S(1)}, bf16[2,3,45,128]{3,1,2,0:T(4,128)(2,1)S(1)}, u32[]{:S(2)}, u32[]{:S(2)}) collective-permute-start(bf16[2,3,45,128]{3,1,2,0:T(4,128)(2,1)S(1)} %get-tuple-element.12), channel_id=1, source_target_pairs={{32,0},{64,32},{96,64},{128,96},{160,128},{192,160},{224,192},{256... | collective-permute-start | bytes 207368 | tf_op jit(solution)/shard_map/ppermute | solution.py:17
  89.1 2.4 %collective-permute-start.4 = (bf16[2,3,45,128]{3,1,2,0:T(4,128)(2,1)S(1)}, bf16[2,3,45,128]{3,1,2,0:T(4,128)(2,1)S(1)}, u32[]{:S(2)}, u32[]{:S(2)}) collective-permute-start(bf16[2,3,45,128]{3,1,2,0:T(4,128)(2,1)S(1)} %get-tuple-element.11), channel_id=1, source_target_pairs={{0,32},{32,64},{64,96},{96,128},{128,160},{160,192},{192,224},{224... | collective-permute-start | bytes 207368 | tf_op jit(solution)/shard_map/ppermute | solution.py:16
  91.5 0.0 collective-permute-done.3
  91.5 4.6 %collective-permute-done.4 = bf16[2,3,45,128]{3,1,2,0:T(4,128)(2,1)S(1)} collective-permute-done((bf16[2,3,45,128]{3,1,2,0:T(4,128)(2,1)S(1)}, bf16[2,3,45,128]{3,1,2,0:T(4,128)(2,1)S(1)}, u32[]{:S(2)}, u32[]{:S(2)}) %collective-permute-start.4) | collective-permute-done | bytes 69152 | tf_op jit(solution)/shard_map/ppermute | solution.py:16
  96.1 0.2 fusion.54
  96.3 0.3 fusion.28
  96.7 0.3 slice_subtract_fusion.1
  97.0 0.9 fusion.21
  97.9 0.9 fusion.49
  (16 shorter events, 0.1 us)
Async XLA Ops:
  0.0 16.3 %copy-start.7 = (s32[32]{0:T(128)S(1)}, s32[32]{0:T(128)}, u32[]{:S(2)}) copy-start(s32[32]{0:T(128)} %param.7) | copy-start | bytes 388
  0.0 16.3 %copy-start.8 = (s32[32]{0:T(128)S(1)}, s32[32]{0:T(128)}, u32[]{:S(2)}) copy-start(s32[32]{0:T(128)} %param.8) | copy-start | bytes 388
  0.0 16.3 %copy-start.6 = (f32[32,721]{1,0:T(8,128)S(1)}, f32[32,721]{1,0:T(8,128)}, u32[]{:S(2)}) copy-start(f32[32,721]{1,0:T(8,128)} %param.9) | copy-start | bytes 276868
  2.8 41.1 %all-to-all-start = ((bf16[32,90,128]{2,1,0:T(8,128)(2,1)}), bf16[32,90,128]{2,1,0:T(8,128)(2,1)S(1)}, u32[]{:S(2)}, u32[]{:S(2)}) async-start(bf16[32,90,128]{2,1,0:T(8,128)(2,1)} %copy.37), calls=%async_computation | async-start | bytes 1572864 | tf_op jit(solution)/shard_map/all_to_all | solution.py:112
  44.3 5.2 %copy-start.3 = (bf16[1472,721]{1,0:T(8,128)(2,1)S(1)}, bf16[1472,721]{1,0:T(8,128)(2,1)}, u32[]{:S(2)}) copy-start(bf16[1472,721]{1,0:T(8,128)(2,1)} %neg.15) | copy-start | bytes 6367876
  44.3 5.2 %copy-start.4 = (bf16[1472,721]{1,0:T(8,128)(2,1)S(1)}, bf16[1472,721]{1,0:T(8,128)(2,1)}, u32[]{:S(2)}) copy-start(bf16[1472,721]{1,0:T(8,128)(2,1)} %sub.122) | copy-start | bytes 6367876
  51.0 11.0 %copy-start.5 = (bf16[1,32,45,128]{3,1,2,0:T(8,128)(2,1)S(1)}, bf16[1,32,45,128]{3,1,2,0:T(8,128)(2,1)}, u32[]{:S(2)}) copy-start(bf16[1,32,45,128]{3,1,2,0:T(8,128)(2,1)} %param.5) | copy-start | bytes 1105924
  51.0 16.9 %copy-start = (f32[32,2,45,128]{3,1,2,0:T(2,128)S(1)}, f32[32,2,45,128]{3,1,2,0:T(2,128)}, u32[]{:S(2)}) copy-start(f32[32,2,45,128]{3,1,2,0:T(2,128)} %param.6) | copy-start | bytes 4423684
  52.3 31.9 %all-to-all-start.1 = ((bf16[32,92,128]{2,1,0:T(8,128)(2,1)}), bf16[32,92,128]{2,1,0:T(8,128)(2,1)S(1)}, u32[]{:S(2)}, u32[]{:S(2)}) async-start(bf16[32,92,128]{2,1,0:T(8,128)(2,1)} %reshape_transpose_reshape.7), calls=%async_computation.1 | async-start | bytes 1572864 | tf_op jit(solution)/shard_map/all_to_all | solution.py:124
  62.1 15.9 %collective-permute-start.1 = (bf16[1,32,3,128]{3,1,2,0:T(8,128)(2,1)S(1)}, bf16[1,32,3,128]{3,1,2,0:T(8,128)(2,1)S(1)}, u32[]{:S(2)}, u32[]{:S(2)}) collective-permute-start(bf16[1,32,3,128]{3,1,2,0:T(8,128)(2,1)S(1)} %get-tuple-element.17), channel_id=1, source_target_pairs={{0,1},{1,2},{2,3},{3,4},{4,5},{5,6},{6,7},{7,8},{8,9},{9,10},{10,1... | collective-permute-start | bytes 73736 | tf_op jit(solution)/shard_map/ppermute | solution.py:16
  65.4 15.2 %collective-permute-start.2 = (bf16[1,32,3,128]{3,1,2,0:T(8,128)(2,1)S(1)}, bf16[1,32,3,128]{3,1,2,0:T(8,128)(2,1)S(1)}, u32[]{:S(2)}, u32[]{:S(2)}) collective-permute-start(bf16[1,32,3,128]{3,1,2,0:T(8,128)(2,1)S(1)} %get-tuple-element.18), channel_id=1, source_target_pairs={{1,0},{2,1},{3,2},{4,3},{5,4},{6,5},{7,6},{8,7},{9,8},{10,9},{11,1... | collective-permute-start | bytes 73736 | tf_op jit(solution)/shard_map/ppermute | solution.py:17
  68.0 16.8 %collective-permute-start = (f32[32,1,128]{2,0,1:T(8,128)S(1)}, f32[32,1,128]{2,0,1:T(8,128)S(1)}, u32[]{:S(2)}, u32[]{:S(2)}) collective-permute-start(f32[32,1,128]{2,0,1:T(8,128)S(1)} %bitcast.49), channel_id=1, source_target_pairs={{0,31},{1,0},{2,1},{3,2},{4,3},{5,4},{6,5},{7,6},{8,7},{9,8},{10,9... | collective-permute-start | bytes 49160 | tf_op jit(solution)/shard_map/ppermute | solution.py:138
  84.2 1.1 %copy-start.2 = (f32[32,1,45,128]{3,0,2,1:T(8,128)S(1)}, f32[32,1,45,128]{3,0,2,1:T(8,128)}, u32[]{:S(2)}) copy-start(f32[32,1,45,128]{3,0,2,1:T(8,128)} %copy.53) | copy-start | bytes 2211844
  85.8 1.1 %copy-start.1 = (f32[32,1,45,128]{3,1,2,0:T(1,128)S(1)}, f32[32,1,45,128]{3,1,2,0:T(1,128)}, u32[]{:S(2)}) copy-start(f32[32,1,45,128]{3,1,2,0:T(1,128)} %get-tuple-element.6) | copy-start | bytes 2211844
  87.1 4.4 %collective-permute-start.3 = (bf16[2,3,45,128]{3,1,2,0:T(4,128)(2,1)S(1)}, bf16[2,3,45,128]{3,1,2,0:T(4,128)(2,1)S(1)}, u32[]{:S(2)}, u32[]{:S(2)}) collective-permute-start(bf16[2,3,45,128]{3,1,2,0:T(4,128)(2,1)S(1)} %get-tuple-element.12), channel_id=1, source_target_pairs={{32,0},{64,32},{96,64},{128,96},{160,128},{192,160},{224,192},{256... | collective-permute-start | bytes 207368 | tf_op jit(solution)/shard_map/ppermute | solution.py:17
  89.1 7.1 %collective-permute-start.4 = (bf16[2,3,45,128]{3,1,2,0:T(4,128)(2,1)S(1)}, bf16[2,3,45,128]{3,1,2,0:T(4,128)(2,1)S(1)}, u32[]{:S(2)}, u32[]{:S(2)}) collective-permute-start(bf16[2,3,45,128]{3,1,2,0:T(4,128)(2,1)S(1)} %get-tuple-element.11), channel_id=1, source_target_pairs={{0,32},{32,64},{64,96},{96,128},{128,160},{160,192},{192,224},{224... | collective-permute-start | bytes 207368 | tf_op jit(solution)/shard_map/ppermute | solution.py:16

commit v7 on v1

--- a/solution.py
+++ b/solution.py
@@ -3,6 +3,7 @@
 import jax
 import jax.numpy as jnp
 from jax import lax
+from jax.experimental import pallas as pl
 from jax.sharding import PartitionSpec as P
 
 
@@ -139,9 +140,23 @@
     meridional_faces = meridional_band[tracer_count, 3 : rows_local + 4].astype(jnp.float32)
     face_rows = lax.axis_index("lat") * rows_local + jnp.arange(rows_local + 1, dtype=jnp.int32)
     meridional_faces = jnp.where(face_rows[:, None, None] > 0, meridional_faces, 0.0)
-    return (
-        middle.astype(jnp.float32) + ppm_change(middle_wide, meridional_faces[None], 1, rows_local)
-    ).astype(jnp.bfloat16)
+    return meridional_step(middle_wide, meridional_faces[None], middle)
+
+
+def meridional_kernel(wide_ref, faces_ref, middle_ref, out_ref):
+    rows = out_ref.shape[1]
+    change = ppm_change(wide_ref[0], faces_ref[0], 0, rows)
+    out_ref[0] = (middle_ref[0].astype(jnp.float32) + change).astype(out_ref.dtype)
+
+
+def meridional_step(middle_wide, meridional_faces, middle):
+    return pl.pallas_call(
+        meridional_kernel,
+        out_shape=jax.ShapeDtypeStruct(middle.shape, middle.dtype),
+        cost_estimate=pl.CostEstimate(
+            flops=40 * middle.size, transcendentals=0, bytes_accessed=12 * middle.size
+        ),
+    )(middle_wide, meridional_faces, middle)
 
 
 def solution(mesh):

time: 88.1 us -> 92.3 us (1.048)
  the two profiles are of different devices: /device:TPU:32 before, /device:TPU:38 now
where the time goes in v7:
time: 92.3 us; the launch traced here: 91.8 us
  starting transfers between devices  32.1 us (35%)
  waiting for transfers between devices  28.6 us (31%)
  other arithmetic  11.2 us (12%)
  local copies, waits for them, and re-layouts  10.5 us (11%)
  matrix products  5.84 us (6%)
  Pallas kernels  3.08 us (3%)
    all_to_all x1, waiting for transfers between devices, filter_correction(): lax.all_to_all(outgoing, 'lon', split_axis=0, concat_axis=0, tiled=True)  15.3 us
    all_to_all x1, starting transfers between devices, filter_correction(): lax.all_to_all(outgoing, 'lon', split_axis=0, concat_axis=0, tiled=True)  13.4 us
    ppermute x2, waiting for transfers between devices, padded(): before = lax.ppermute(last, axis, up)  7.88 us
    ppermute x2, starting transfers between devices, padded(): before = lax.ppermute(last, axis, up)  5.78 us
    all_to_all x1, starting transfers between devices, filter_correction(): lax.all_to_all(correction, 'lon', split_axis=0, concat_axis=0, tiled=True)  5.61 us
    ppermute x2, starting transfers between devices, padded(): after = lax.ppermute(leading, axis, down)  4.39 us
    dot_general x1, matrix products, filter_correction(): jnp.einsum('drjcl,djm->rcml', level_block, forward_table, preferred_eleme...  4.39 us
    convert_element_type x1, other arithmetic, filter_correction(): inverse_table = table.astype(jnp.bfloat16)  3.86 us
  transfers between devices with their start and end apart: 7, of which 5 were waited for; matrix products, arithmetic and copies ran while one was open for 14% of the time, Pallas kernels for 0%

profile of v7, /device:TPU:38, one launch (start us, length us, event | category | flops | bytes accessed | tf_op | source)
XLA Modules:
  0.0 91.8 jit_solution(10545681303693707776)
XLA Ops:
  0.0 0.0 copy-start.5
  0.0 0.0 copy-start.6
  0.0 0.0 copy-start.4
  0.0 1.6 %copy.69 = bf16[32,2,45,128]{3,0,1,2:T(8,128)(2,1)S(1)} copy(f32[32,2,45,128]{3,1,2,0:T(2,128)} %param.6) | data formatting | bytes 2211840 | tf_op args[1]
  1.6 1.2 %copy.31 = bf16[32,90,128]{2,1,0:T(8,128)(2,1)} copy(bf16[32,90,128]{2,0,1:T(8,128)(2,1)S(1)} %bitcast.70) | data formatting | bytes 1474560 | tf_op jit(solution)/shard_map/reshape | solution.py:94
  2.8 13.4 %all-to-all-start = ((bf16[32,90,128]{2,1,0:T(8,128)(2,1)}), bf16[32,90,128]{2,1,0:T(8,128)(2,1)S(1)}, u32[]{:S(2)}, u32[]{:S(2)}) async-start(bf16[32,90,128]{2,1,0:T(8,128)(2,1)} %copy.31), calls=%async_computation | async-start | bytes 1572864 | tf_op jit(solution)/shard_map/all_to_all | solution.py:97
  16.3 0.6 fusion.36
  16.9 0.0 copy-done.5
  16.9 0.0 copy-done.6
  16.9 0.1 pad_maximum_fusion.7
  17.0 0.0 copy-done.4
  17.0 0.1 select_subtract_fusion
  17.1 0.1 broadcast_in_dim.20
  17.2 0.1 reshape.306
  17.3 0.5 fusion.44
  17.8 1.6 %multiply_subtract_fusion = (bf16[32,46,721]{2,1,0:T(8,128)(2,1)S(1)}, bf16[32,46,721]{2,1,0:T(8,128)(2,1)S(1)}) fusion(f32[46,721]{1,0:T(8,128)S(1)} %get-tuple-element.17, f32[32,721]{1,0:T(8,128)S(1)} %get-tuple-element.16, f32[46,721]{1,0:T(8,128)S(1)} %get-tuple-element.18, f32[32,721]{1,0:T(8,128)S(1)} %get-tuple-element.15), kind=kLoop, calls=%fused_computation.6 | loop fusion | flops 9551808 | bytes 4695152 | tf_op jit(solution)/shard_map/sub | solution.py:76
  19.5 3.9 %maximum_convert_fusion = bf16[32,46,1442]{2,1,0:T(8,128)(2,1)} fusion(bf16[32,46,721]{2,1,0:T(8,128)(2,1)S(1)} %get-tuple-element.12, bf16[32,46,721]{2,1,0:T(8,128)(2,1)S(1)} %get-tuple-element.11), kind=kLoop, calls=%fused_computation | loop fusion | flops 8490496 | bytes 8490496 | tf_op jit(solution)/shard_map/convert_element_type | solution.py:92
  23.3 0.1 fusion.48
  23.4 15.3 %all-to-all-done = bf16[32,90,128]{2,1,0:T(8,128)(2,1)S(1)} async-done(((bf16[32,90,128]{2,1,0:T(8,128)(2,1)}), bf16[32,90,128]{2,1,0:T(8,128)(2,1)S(1)}, u32[]{:S(2)}, u32[]{:S(2)}) %all-to-all-start) | async-done | bytes 737312 | tf_op jit(solution)/shard_map/all_to_all | solution.py:97
  38.7 0.0 slice-start
  38.7 0.3 copy.32
  39.0 0.0 slice-start.1
  39.0 4.4 %fusion.6 = bf16[2,1442,128,1]{2,1,0,3:T(8,128)(2,1)S(1)} fusion(bf16[32,46,1442]{2,1,0:T(8,128)(2,1)} %maximum_convert_fusion, bf16[32,45,2,128]{3,0,2,1:T(8,128)(2,1)S(1)} %bitcast.71, f32[2,1442]{1,0:T(2,128)S(1)} %fusion.48), kind=kOutput, calls=%fused_computation.10 | convolution fusion | flops 1063896064 | bytes 5732368 | tf_op jit(solution)/shard_map/drjcl,djm->rcml/dot_general | solution.py:101
  43.4 0.0 slice-done
  43.4 0.0 slice-done.1
  43.4 1.4 %fusion.7 = bf16[32,46,2,128]{3,1,2,0:T(8,128)(2,1)S(1)} fusion(bf16[2,1442,128,1]{2,1,0,3:T(8,128)(2,1)S(1)} %fusion.6, bf16[32,46,1442]{2,1,0:T(8,128)(2,1)S(1)} %bitcast.67), kind=kOutput, calls=%fused_computation.17 | convolution fusion | flops 1087160320 | bytes 5737216 | tf_op jit(solution)/shard_map/rcml,djm->drjcl/dot_general | solution.py:105
  44.9 0.0 copy-start.3
  44.9 0.0 copy-start.1
  44.9 0.3 copy.34
  45.2 1.2 %copy.35 = bf16[32,92,128]{2,1,0:T(8,128)(2,1)} copy(bf16[32,92,128]{2,0,1:T(8,128)(2,1)S(1)} %bitcast.69) | data formatting | bytes 1507328 | tf_op jit(solution)/shard_map/reshape | solution.py:111
  46.4 5.6 %all-to-all-start.1 = ((bf16[32,92,128]{2,1,0:T(8,128)(2,1)}), bf16[32,92,128]{2,1,0:T(8,128)(2,1)}, u32[]{:S(2)}, u32[]{:S(2)}) async-start(bf16[32,92,128]{2,1,0:T(8,128)(2,1)} %copy.35), calls=%async_computation.1 | async-start | bytes 1572864 | tf_op jit(solution)/shard_map/all_to_all | solution.py:112
  52.1 0.0 copy-done.3
  52.1 0.2 copy.27
  52.3 3.4 %collective-permute-start.1 = (bf16[1,32,3,128]{3,2,1,0:T(4,128)(2,1)S(1)}, bf16[1,32,3,128]{3,2,1,0:T(4,128)(2,1)S(1)}, u32[]{:S(2)}, u32[]{:S(2)}) collective-permute-start(bf16[1,32,3,128]{3,2,1,0:T(4,128)(2,1)S(1)} %get-tuple-element.13), channel_id=1, source_target_pairs={{0,1},{1,2},{2,3},{3,4},{4,5},{5,6},{6,7},{7,8},{8,9},{9,10},{10,1... | collective-permute-start | bytes 73736 | tf_op jit(solution)/shard_map/ppermute | solution.py:17
  55.7 2.5 %collective-permute-start.2 = (bf16[1,32,3,128]{3,2,1,0:T(4,128)(2,1)S(1)}, bf16[1,32,3,128]{3,2,1,0:T(4,128)(2,1)S(1)}, u32[]{:S(2)}, u32[]{:S(2)}) collective-permute-start(bf16[1,32,3,128]{3,2,1,0:T(4,128)(2,1)S(1)} %get-tuple-element.14), channel_id=1, source_target_pairs={{1,0},{2,1},{3,2},{4,3},{5,4},{6,5},{7,6},{8,7},{9,8},{10,9},{11,1... | collective-permute-start | bytes 73736 | tf_op jit(solution)/shard_map/ppermute | solution.py:18
  58.1 0.0 copy-done.1
  58.2 2.9 %collective-permute-start = (f32[32,1,128]{2,0,1:T(8,128)S(1)}, f32[32,1,128]{2,0,1:T(8,128)S(1)}, u32[]{:S(2)}, u32[]{:S(2)}) collective-permute-start(f32[32,1,128]{2,0,1:T(8,128)S(1)} %bitcast.73), channel_id=1, source_target_pairs={{0,31},{1,0},{2,1},{3,2},{4,3},{5,4},{6,5},{7,6},{8,7},{9,8},{10,9... | collective-permute-start | bytes 49160 | tf_op jit(solution)/shard_map/ppermute | solution.py:126
  61.1 2.0 %fusion.51 = (f32[32,1,45,128]{3,1,2,0:T(1,128)S(1)}, f32[32,1,45,128]{3,1,2,0:T(1,128)}) fusion(f32[32,2,45,128]{3,1,2,0:T(2,128)S(1)} %copy-done.1), kind=kLoop, calls=%fused_computation.94 | loop fusion | bytes 2949120 | tf_op jit(solution)/shard_map/slice | solution.py:130
  63.1 0.1 copy.70
  63.2 4.5 %collective-permute-done.1 = bf16[1,32,3,128]{3,2,1,0:T(4,128)(2,1)S(1)} collective-permute-done((bf16[1,32,3,128]{3,2,1,0:T(4,128)(2,1)S(1)}, bf16[1,32,3,128]{3,2,1,0:T(4,128)(2,1)S(1)}, u32[]{:S(2)}, u32[]{:S(2)}) %collective-permute-start.1) | collective-permute-done | bytes 24608 | tf_op jit(solution)/shard_map/ppermute | solution.py:17
  67.7 2.6 %collective-permute-done.2 = bf16[1,32,3,128]{3,2,1,0:T(4,128)(2,1)S(1)} collective-permute-done((bf16[1,32,3,128]{3,2,1,0:T(4,128)(2,1)S(1)}, bf16[1,32,3,128]{3,2,1,0:T(4,128)(2,1)S(1)}, u32[]{:S(2)}, u32[]{:S(2)}) %collective-permute-start.2) | collective-permute-done | bytes 24608 | tf_op jit(solution)/shard_map/ppermute | solution.py:18
  70.2 0.2 maximum_convert_fusion.1
  70.4 0.3 fusion.25
  70.7 0.3 slice_subtract_fusion.2
  70.9 2.8 %all-to-all-done.1 = bf16[32,92,128]{2,1,0:T(8,128)(2,1)} async-done(((bf16[32,92,128]{2,1,0:T(8,128)(2,1)}), bf16[32,92,128]{2,1,0:T(8,128)(2,1)}, u32[]{:S(2)}, u32[]{:S(2)}) %all-to-all-start.1) | async-done | bytes 753696 | tf_op jit(solution)/shard_map/all_to_all | solution.py:112
  73.8 1.4 %copy.36 = bf16[32,92,128]{2,0,1:T(8,128)(2,1)S(1)} copy(bf16[32,92,128]{2,1,0:T(8,128)(2,1)} %all-to-all-done.1) | data formatting | bytes 1507328 | tf_op jit(solution)/shard_map/all_to_all | solution.py:112
  75.2 0.1 slice.110
  75.3 0.0 copy-start.2
  75.3 0.1 slice.127
  75.3 0.0 collective-permute-done
  75.4 0.9 fusion.20
  76.3 0.2 fusion.22.middle_ref
  76.5 0.0 copy-start
  76.5 0.0 copy-done.2
  76.5 0.5 fusion.29
  77.0 1.9 %collective-permute-start.4 = (bf16[2,3,45,128]{3,2,1,0:T(8,128)(2,1)S(1)}, bf16[2,3,45,128]{3,2,1,0:T(8,128)(2,1)S(1)}, u32[]{:S(2)}, u32[]{:S(2)}) collective-permute-start(bf16[2,3,45,128]{3,2,1,0:T(8,128)(2,1)S(1)} %get-tuple-element.8), channel_id=1, source_target_pairs={{32,0},{64,32},{96,64},{128,96},{160,128},{192,160},{224,192},{256... | collective-permute-start | bytes 207368 | tf_op jit(solution)/shard_map/ppermute | solution.py:18
  78.9 2.4 %collective-permute-start.3 = (bf16[2,3,45,128]{3,2,1,0:T(8,128)(2,1)S(1)}, bf16[2,3,45,128]{3,2,1,0:T(8,128)(2,1)S(1)}, u32[]{:S(2)}, u32[]{:S(2)}) collective-permute-start(bf16[2,3,45,128]{3,2,1,0:T(8,128)(2,1)S(1)} %get-tuple-element.7), channel_id=1, source_target_pairs={{0,32},{32,64},{64,96},{96,128},{128,160},{160,192},{192,224},{224... | collective-permute-start | bytes 207368 | tf_op jit(solution)/shard_map/ppermute | solution.py:17
  81.3 0.0 collective-permute-done.4
  81.3 1.0 %convert_select_fusion.faces_ref = f32[1,33,45,128]{3,2,1,0:T(8,128)} fusion(bf16[2,3,45,128]{3,2,1,0:T(8,128)(2,1)S(1)} %collective-permute-done.4, bf16[1,32,45,128]{3,2,1,0:T(8,128)(2,1)S(1)} %fusion.29, bf16[1,32,45,128]{3,2,1,0:T(8,128)(2,1)S(1)} %fusion.22.middle_ref, pred[33]{0:T(512)(128)(4,1)S(1)} %add_compare_fusion), kind=kLoop, calls=%fused_computation.22 | loop fusion | flops 760320 | bytes 1566753 | tf_op jit(solution)/shard_map/jit(_where)/select_n | solution.py:142
  82.4 3.4 %collective-permute-done.3 = bf16[2,3,45,128]{3,2,1,0:T(8,128)(2,1)S(1)} collective-permute-done((bf16[2,3,45,128]{3,2,1,0:T(8,128)(2,1)S(1)}, bf16[2,3,45,128]{3,2,1,0:T(8,128)(2,1)S(1)}, u32[]{:S(2)}, u32[]{:S(2)}) %collective-permute-start.3) | collective-permute-done | bytes 69152 | tf_op jit(solution)/shard_map/ppermute | solution.py:17
  85.8 1.0 %fusion.31.wide_ref = f32[1,38,45,128]{3,2,1,0:T(8,128)} fusion(bf16[2,3,45,128]{3,2,1,0:T(8,128)(2,1)S(1)} %collective-permute-done.4, bf16[2,3,45,128]{3,2,1,0:T(8,128)(2,1)S(1)} %collective-permute-done.3, bf16[1,32,45,128]{3,2,1,0:T(8,128)(2,1)S(1)} %fusion.29, bf16[1,32,45,128]{3,2,1,0:T(8,128)(2,1)S(1)} %fusion.22.middle_ref), kind=kLoop, calls=%fused_computation.51 | loop fusion | flops 875520 | bytes 1751040 | tf_op jit(solution)/shard_map/convert_element_type | solution.py:139
  86.8 0.0 copy-done
  86.8 3.1 %shard_map.55 = bf16[1,32,45,128]{3,2,1,0:T(8,128)(2,1)} custom-call(f32[1,38,45,128]{3,2,1,0:T(8,128)} %fusion.31.wide_ref, f32[1,33,45,128]{3,2,1,0:T(8,128)} %convert_select_fusion.faces_ref, bf16[1,32,45,128]{3,2,1,0:T(8,128)(2,1)} %copy-done), custom_call_target="tpu_custom_call" | custom-call | flops 7372800 | bytes 2211840 | tf_op jit(solution)/shard_map/pallas_call | solution.py:153
  89.9 1.8 %copy.43 = bf16[1,32,45,128]{3,1,2,0:T(8,128)(2,1)} copy(bf16[1,32,45,128]{3,2,1,0:T(8,128)(2,1)} %shard_map.55) | data formatting | bytes 737280 | tf_op jit(solution)/shard_map/pallas_call | solution.py:153
  (9 shorter events, 0.1 us)
Async XLA Ops:
  0.0 16.9 %copy-start.5 = (s32[32]{0:T(128)S(1)}, s32[32]{0:T(128)}, u32[]{:S(2)}) copy-start(s32[32]{0:T(128)} %param.7) | copy-start | bytes 388
  0.0 16.9 %copy-start.6 = (s32[32]{0:T(128)S(1)}, s32[32]{0:T(128)}, u32[]{:S(2)}) copy-start(s32[32]{0:T(128)} %param.8) | copy-start | bytes 388
  0.0 17.0 %copy-start.4 = (f32[32,721]{1,0:T(8,128)S(1)}, f32[32,721]{1,0:T(8,128)}, u32[]{:S(2)}) copy-start(f32[32,721]{1,0:T(8,128)} %param.9) | copy-start | bytes 276868
  2.8 35.9 %all-to-all-start = ((bf16[32,90,128]{2,1,0:T(8,128)(2,1)}), bf16[32,90,128]{2,1,0:T(8,128)(2,1)S(1)}, u32[]{:S(2)}, u32[]{:S(2)}) async-start(bf16[32,90,128]{2,1,0:T(8,128)(2,1)} %copy.31), calls=%async_computation | async-start | bytes 1572864 | tf_op jit(solution)/shard_map/all_to_all | solution.py:97
  38.7 4.7 %slice-start = ((s8[4718592]{0:T(1024)(128)(4,1)}), s8[4194304]{0:T(1024)(128)(4,1)S(1)}, s32[]{:S(2)}) async-start(s8[4718592]{0:T(1024)(128)(4,1)} %bitcast.66), calls=%async_computation.2 | async-start | bytes 8388608
  39.0 4.4 %slice-start.1 = ((s8[4718592]{0:T(1024)(128)(4,1)}), s8[524288]{0:T(1024)(128)(4,1)S(1)}, s32[]{:S(2)}) async-start(s8[4718592]{0:T(1024)(128)(4,1)} %bitcast.66), calls=%async_computation.3 | async-start | bytes 1048576
  44.9 7.2 %copy-start.3 = (bf16[1,32,45,128]{3,1,2,0:T(8,128)(2,1)S(1)}, bf16[1,32,45,128]{3,1,2,0:T(8,128)(2,1)}, u32[]{:S(2)}) copy-start(bf16[1,32,45,128]{3,1,2,0:T(8,128)(2,1)} %param.5) | copy-start | bytes 1105924
  44.9 13.2 %copy-start.1 = (f32[32,2,45,128]{3,1,2,0:T(2,128)S(1)}, f32[32,2,45,128]{3,1,2,0:T(2,128)}, u32[]{:S(2)}) copy-start(f32[32,2,45,128]{3,1,2,0:T(2,128)} %param.6) | copy-start | bytes 4423684
  46.4 27.3 %all-to-all-start.1 = ((bf16[32,92,128]{2,1,0:T(8,128)(2,1)}), bf16[32,92,128]{2,1,0:T(8,128)(2,1)}, u32[]{:S(2)}, u32[]{:S(2)}) async-start(bf16[32,92,128]{2,1,0:T(8,128)(2,1)} %copy.35), calls=%async_computation.1 | async-start | bytes 1572864 | tf_op jit(solution)/shard_map/all_to_all | solution.py:112
  52.3 15.4 %collective-permute-start.1 = (bf16[1,32,3,128]{3,2,1,0:T(4,128)(2,1)S(1)}, bf16[1,32,3,128]{3,2,1,0:T(4,128)(2,1)S(1)}, u32[]{:S(2)}, u32[]{:S(2)}) collective-permute-start(bf16[1,32,3,128]{3,2,1,0:T(4,128)(2,1)S(1)} %get-tuple-element.13), channel_id=1, source_target_pairs={{0,1},{1,2},{2,3},{3,4},{4,5},{5,6},{6,7},{7,8},{8,9},{9,10},{10,1... | collective-permute-start | bytes 73736 | tf_op jit(solution)/shard_map/ppermute | solution.py:17
  55.7 14.6 %collective-permute-start.2 = (bf16[1,32,3,128]{3,2,1,0:T(4,128)(2,1)S(1)}, bf16[1,32,3,128]{3,2,1,0:T(4,128)(2,1)S(1)}, u32[]{:S(2)}, u32[]{:S(2)}) collective-permute-start(bf16[1,32,3,128]{3,2,1,0:T(4,128)(2,1)S(1)} %get-tuple-element.14), channel_id=1, source_target_pairs={{1,0},{2,1},{3,2},{4,3},{5,4},{6,5},{7,6},{8,7},{9,8},{10,9},{11,1... | collective-permute-start | bytes 73736 | tf_op jit(solution)/shard_map/ppermute | solution.py:18
  58.2 17.2 %collective-permute-start = (f32[32,1,128]{2,0,1:T(8,128)S(1)}, f32[32,1,128]{2,0,1:T(8,128)S(1)}, u32[]{:S(2)}, u32[]{:S(2)}) collective-permute-start(f32[32,1,128]{2,0,1:T(8,128)S(1)} %bitcast.73), channel_id=1, source_target_pairs={{0,31},{1,0},{2,1},{3,2},{4,3},{5,4},{6,5},{7,6},{8,7},{9,8},{10,9... | collective-permute-start | bytes 49160 | tf_op jit(solution)/shard_map/ppermute | solution.py:126
  75.3 1.2 %copy-start.2 = (f32[32,1,45,128]{3,1,2,0:T(1,128)S(1)}, f32[32,1,45,128]{3,1,2,0:T(1,128)}, u32[]{:S(2)}) copy-start(f32[32,1,45,128]{3,1,2,0:T(1,128)} %get-tuple-element.6) | copy-start | bytes 2211844
  76.5 10.4 %copy-start = (bf16[1,32,45,128]{3,2,1,0:T(8,128)(2,1)}, bf16[1,32,45,128]{3,2,1,0:T(8,128)(2,1)S(1)}, u32[]{:S(2)}) copy-start(bf16[1,32,45,128]{3,2,1,0:T(8,128)(2,1)S(1)} %fusion.22.middle_ref) | copy-start | bytes 1105924
  77.0 4.4 %collective-permute-start.4 = (bf16[2,3,45,128]{3,2,1,0:T(8,128)(2,1)S(1)}, bf16[2,3,45,128]{3,2,1,0:T(8,128)(2,1)S(1)}, u32[]{:S(2)}, u32[]{:S(2)}) collective-permute-start(bf16[2,3,45,128]{3,2,1,0:T(8,128)(2,1)S(1)} %get-tuple-element.8), channel_id=1, source_target_pairs={{32,0},{64,32},{96,64},{128,96},{160,128},{192,160},{224,192},{256... | collective-permute-start | bytes 207368 | tf_op jit(solution)/shard_map/ppermute | solution.py:18
  78.9 6.9 %collective-permute-start.3 = (bf16[2,3,45,128]{3,2,1,0:T(8,128)(2,1)S(1)}, bf16[2,3,45,128]{3,2,1,0:T(8,128)(2,1)S(1)}, u32[]{:S(2)}, u32[]{:S(2)}) collective-permute-start(bf16[2,3,45,128]{3,2,1,0:T(8,128)(2,1)S(1)} %get-tuple-element.7), channel_id=1, source_target_pairs={{0,32},{32,64},{64,96},{96,128},{128,160},{160,192},{192,224},{224... | collective-permute-start | bytes 207368 | tf_op jit(solution)/shard_map/ppermute | solution.py:17

commit v8 on v5

--- a/solution.py
+++ b/solution.py
@@ -87,14 +87,14 @@
     mode_count = row_factor.shape[1]
     per_device = 2 * row_count // blocks
     table, mode_weight = spectral_basis(blocks, lon_local, lon_local + 1, mode_count)
-    forward_table = spectral_basis(blocks, lon_local, lon_local, mode_count)[0].astype(jnp.bfloat16)
+    forward_table = table[:, :lon_local].astype(jnp.bfloat16)
     inverse_table = table.astype(jnp.bfloat16)
     outgoing = courant.transpose(0, 2, 1, 3).astype(jnp.bfloat16)
-    outgoing = outgoing.reshape(blocks, (2 * row_count // blocks) * lon_local, levels)
+    outgoing = outgoing.reshape(blocks, per_device // 2, lon_local, 2, levels)
     pair_factor = jnp.repeat(1.0 - row_factor, 2, axis=0)
     removal = jnp.concatenate([pair_factor, pair_factor], axis=1) * mode_weight[None, :]
     arrived = lax.all_to_all(outgoing, "lon", split_axis=0, concat_axis=0, tiled=True)
-    level_block = arrived.reshape(blocks, per_device // 2, lon_local, 2, levels)
+    level_block = arrived
     first_row = lax.axis_index("lon") * per_device
     local_removal = lax.dynamic_slice_in_dim(removal, first_row, per_device, 0)
     spectrum = jnp.einsum(
@@ -107,7 +107,6 @@
         inverse_table,
         preferred_element_type=jnp.float32,
     ).astype(jnp.bfloat16)
-    correction = correction.reshape(blocks, per_device * (lon_local + 1), levels)
     returned = lax.all_to_all(correction, "lon", split_axis=0, concat_axis=0, tiled=True)
     return returned.reshape(row_count, lon_local + 1, 2, levels)
 

time: 88.7 us -> 111 us (1.25)
  other arithmetic: 15.2 us -> 41.9 us
  local copies, waits for them, and re-layouts: 9.69 us -> 5.21 us
    select_n x2, other arithmetic: 1.34 us -> 10.9 us  [ppm_change(): face_flux = jnp.where(courant_faces > 0, upwind_plus, upwind_minus)]
    another operation x2 -> x0, other arithmetic: 7.81 us -> none
    sub x2, other arithmetic: 0.46 us -> 4.52 us  [ppm_change(): 7.0 / 12.0]
    convert_element_type x0 -> x1, other arithmetic: none -> 3.84 us  [filter_correction(): inverse_table = table.astype(jnp.bfloat16)]
    unnamed x22 -> x9, local copies, waits for them, and re-layouts: 4.17 us -> 0.59 us
    convert_element_type x1, other arithmetic: 0.19 us -> 3.66 us  [local(): middle_wide = meridional_band[:tracer_count].astype(jnp.float32)]
    sub x2, other arithmetic: 0.53 us -> 3.5 us  [ppm_change(): slope_edge = right_edge - left_edge]
    reshape x0 -> x1, other arithmetic: none -> 2.8 us  [filter_correction(): outgoing = outgoing.reshape(blocks, per_device // 2, lon_local, 2, levels)]
  transfers between devices with their start and end apart: 7 -> 7, of which waited for: 4 -> 3; matrix products, arithmetic and copies ran while one was open for 17% -> 18% of each run, Pallas kernels for 0% -> 0%
where the time goes in v8:
time: 111 us; the launch traced here: 110 us
  other arithmetic  41.9 us (38%)
  starting transfers between devices  35.8 us (32%)
  waiting for transfers between devices  21.5 us (19%)
  matrix products  5.62 us (5%)
  local copies, waits for them, and re-layouts  5.21 us (5%)
    all_to_all x1, starting transfers between devices, filter_correction(): lax.all_to_all(outgoing, 'lon', split_axis=0, concat_axis=0, tiled=True)  13.2 us
    all_to_all x1, waiting for transfers between devices, filter_correction(): lax.all_to_all(outgoing, 'lon', split_axis=0, concat_axis=0, tiled=True)  12.1 us
    select_n x2, other arithmetic, ppm_change(): face_flux = jnp.where(courant_faces > 0, upwind_plus, upwind_minus)  10.9 us
    ppermute x2, waiting for transfers between devices, padded(): before = lax.ppermute(last, axis, up)  9.36 us
    ppermute x2, starting transfers between devices, padded(): after = lax.ppermute(leading, axis, down)  7.39 us
    ppermute x2, starting transfers between devices, padded(): before = lax.ppermute(last, axis, up)  6.32 us
    all_to_all x1, starting transfers between devices, filter_correction(): lax.all_to_all(correction, 'lon', split_axis=0, concat_axis=0, tiled=True)  4.99 us
    sub x2, other arithmetic, ppm_change(): 7.0 / 12.0  4.52 us
  transfers between devices with their start and end apart: 7, of which 3 were waited for; matrix products, arithmetic and copies ran while one was open for 18% of the time, Pallas kernels for 0%

profile of v8, /device:TPU:32, one launch (start us, length us, event | category | flops | bytes accessed | tf_op | source)
XLA Modules:
  0.0 110.3 jit_solution(2210350781080877218)
XLA Ops:
  0.0 0.0 copy-start.3
  0.0 2.8 %convert_bitcast_fusion = bf16[32,1,45,2,128]{4,3,2,1,0:T(2,128)(2,1)} fusion(f32[32,2,45,128]{3,1,2,0:T(2,128)} %param.6), kind=kLoop, calls=%fused_computation.64 | loop fusion | flops 368640 | bytes 2211840 | tf_op jit(solution)/shard_map/reshape | solution.py:93
  2.8 13.2 %all-to-all-start = ((bf16[32,1,45,2,128]{4,3,2,1,0:T(2,128)(2,1)}), bf16[32,1,45,2,128]{4,3,2,1,0:T(2,128)(2,1)S(1)}, u32[]{:S(2)}, u32[]{:S(2)}) async-start(bf16[32,1,45,2,128]{4,3,2,1,0:T(2,128)(2,1)} %convert_bitcast_fusion), calls=%async_computation | async-start | bytes 1474560 | tf_op jit(solution)/shard_map/all_to_all | solution.py:96
  16.0 0.6 fusion.46
  16.6 0.7 broadcast_compare_fusion
  17.3 0.7 broadcast_subtract_fusion
  17.9 0.1 pad_maximum_fusion.7
  18.0 1.0 select_subtract_fusion
  19.0 0.1 broadcast_in_dim.20
  19.1 0.1 reshape.307
  19.2 0.0 copy-done.3
  19.2 0.6 copy.16
  19.8 0.5 fusion.54
  20.3 1.6 %multiply_subtract_fusion = (bf16[32,46,721]{2,1,0:T(8,128)(2,1)S(1)}, bf16[32,46,721]{2,1,0:T(8,128)(2,1)S(1)}) fusion(f32[46,721]{1,0:T(8,128)S(1)} %get-tuple-element.17, f32[32,721]{1,0:T(8,128)S(1)} %get-tuple-element.16, f32[46,721]{1,0:T(8,128)S(1)} %get-tuple-element.18, f32[32,721]{1,0:T(8,128)S(1)} %get-tuple-element.15), kind=kLoop, calls=%fused_computation.6 | loop fusion | flops 9551808 | bytes 4695152 | tf_op jit(solution)/shard_map/sub | solution.py:75
  21.9 3.8 %maximum_convert_fusion = bf16[32,46,1442]{2,1,0:T(8,128)(2,1)} fusion(bf16[32,46,721]{2,1,0:T(8,128)(2,1)S(1)} %get-tuple-element.14, bf16[32,46,721]{2,1,0:T(8,128)(2,1)S(1)} %get-tuple-element.13), kind=kLoop, calls=%fused_computation | loop fusion | flops 8490496 | bytes 8490496 | tf_op jit(solution)/shard_map/convert_element_type | solution.py:91
  25.8 0.1 fusion.58
  25.9 12.1 %all-to-all-done = bf16[32,1,45,2,128]{4,3,2,1,0:T(2,128)(2,1)S(1)} async-done(((bf16[32,1,45,2,128]{4,3,2,1,0:T(2,128)(2,1)}), bf16[32,1,45,2,128]{4,3,2,1,0:T(2,128)(2,1)S(1)}, u32[]{:S(2)}, u32[]{:S(2)}) %all-to-all-start) | async-done | bytes 737312 | tf_op jit(solution)/shard_map/all_to_all | solution.py:96
  37.9 0.0 copy-start.1
  38.0 4.2 %fusion.5 = bf16[2,1442,128]{2,1,0:T(8,128)(2,1)S(1)} fusion(bf16[32,46,1442]{2,1,0:T(8,128)(2,1)} %maximum_convert_fusion, bf16[32,1,45,2,128]{4,3,2,1,0:T(2,128)(2,1)S(1)} %all-to-all-done, f32[2,1442]{1,0:T(2,128)S(1)} %fusion.58), kind=kOutput, calls=%fused_computation.11 | convolution fusion | flops 1063896064 | bytes 5732368 | tf_op jit(solution)/shard_map/drjcl,djm->rcml/dot_general | solution.py:100
  42.1 0.0 copy-done.1
  42.1 0.0 copy-start
  42.2 1.4 %fusion.9 = bf16[32,1,46,2,128]{4,2,3,0,1:T(8,128)(2,1)S(1)} fusion(bf16[32,46,1442]{2,1,0:T(8,128)(2,1)S(1)} %copy-done.1, bf16[2,1442,128]{2,1,0:T(8,128)(2,1)S(1)} %fusion.5), kind=kOutput, calls=%fused_computation.14 | convolution fusion | flops 1087160320 | bytes 5737216 | tf_op jit(solution)/shard_map/rcml,djm->drjcl/dot_general | solution.py:104
  43.6 1.5 %copy.19 = bf16[32,1,46,2,128]{4,3,2,1,0:T(2,128)(2,1)} copy(bf16[32,1,46,2,128]{4,2,3,0,1:T(8,128)(2,1)S(1)} %fusion.9) | data formatting | bytes 1507328 | tf_op jit(solution)/shard_map/convert_element_type | solution.py:109
  45.1 5.0 %all-to-all-start.1 = ((bf16[32,1,46,2,128]{4,3,2,1,0:T(2,128)(2,1)}), bf16[32,1,46,2,128]{4,3,2,1,0:T(2,128)(2,1)S(1)}, u32[]{:S(2)}, u32[]{:S(2)}) async-start(bf16[32,1,46,2,128]{4,3,2,1,0:T(2,128)(2,1)} %copy.19), calls=%async_computation.1 | async-start | bytes 1507328 | tf_op jit(solution)/shard_map/all_to_all | solution.py:110
  50.1 0.1 fusion.61
  50.2 3.7 %collective-permute-start.1 = (bf16[1,32,3,128]{3,0,2,1:T(2,128)(2,1)S(1)}, bf16[1,32,3,128]{3,0,2,1:T(2,128)(2,1)S(1)}, u32[]{:S(2)}, u32[]{:S(2)}) collective-permute-start(bf16[1,32,3,128]{3,0,2,1:T(2,128)(2,1)S(1)} %get-tuple-element.11), channel_id=1, source_target_pairs={{0,1},{1,2},{2,3},{3,4},{4,5},{5,6},{6,7},{7,8},{8,9},{9,10},{10,1... | collective-permute-start | bytes 73736 | tf_op jit(solution)/shard_map/ppermute | solution.py:16
  53.9 5.5 %collective-permute-start.2 = (bf16[1,32,3,128]{3,0,2,1:T(2,128)(2,1)S(1)}, bf16[1,32,3,128]{3,0,2,1:T(2,128)(2,1)S(1)}, u32[]{:S(2)}, u32[]{:S(2)}) collective-permute-start(bf16[1,32,3,128]{3,0,2,1:T(2,128)(2,1)S(1)} %get-tuple-element.12), channel_id=1, source_target_pairs={{1,0},{2,1},{3,2},{4,3},{5,4},{6,5},{7,6},{8,7},{9,8},{10,9},{11,1... | collective-permute-start | bytes 73736 | tf_op jit(solution)/shard_map/ppermute | solution.py:17
  59.4 0.0 copy-done
  59.4 0.6 slice.129
  60.0 4.0 %collective-permute-start = (f32[32,1,128]{2,0,1:T(8,128)}, f32[32,1,128]{2,0,1:T(8,128)}, u32[]{:S(2)}, u32[]{:S(2)}) collective-permute-start(f32[32,1,128]{2,0,1:T(8,128)} %bitcast.1), channel_id=1, source_target_pairs={{0,31},{1,0},{2,1},{3,2},{4,3},{5,4},{6,5},{7,6},{8,7},{9,8},{10,9... | collective-permute-start | bytes 49160 | tf_op jit(solution)/shard_map/ppermute | solution.py:124
  64.0 1.4 %slice_bitcast_fusion.10 = f32[1,32,45,128]{3,0,2,1:T(1,128)} fusion(f32[32,2,45,128]{3,1,2,0:T(2,128)S(1)} %copy-done), kind=kLoop, calls=%fused_computation.65 | loop fusion | bytes 1474560 | tf_op jit(solution)/shard_map/concatenate | solution.py:128
  65.4 5.2 %collective-permute-done.1 = bf16[1,32,3,128]{3,0,2,1:T(2,128)(2,1)S(1)} collective-permute-done((bf16[1,32,3,128]{3,0,2,1:T(2,128)(2,1)S(1)}, bf16[1,32,3,128]{3,0,2,1:T(2,128)(2,1)S(1)}, u32[]{:S(2)}, u32[]{:S(2)}) %collective-permute-start.1) | collective-permute-done | bytes 24608 | tf_op jit(solution)/shard_map/ppermute | solution.py:16
  70.6 0.0 collective-permute-done.2
  70.6 1.2 %maximum_convert_fusion.1 = f32[1,32,51,128]{3,0,2,1:T(1,128)S(1)} fusion(bf16[1,32,3,128]{3,0,2,1:T(2,128)(2,1)S(1)} %collective-permute-done.2, bf16[1,32,45,128]{3,0,2,1:T(2,128)(2,1)S(1)} %copy.16, bf16[1,32,3,128]{3,0,2,1:T(2,128)(2,1)S(1)} %collective-permute-done.1), kind=kLoop, calls=%fused_computation.19 | loop fusion | flops 626688 | bytes 1253376 | tf_op jit(solution)/shard_map/convert_element_type | solution.py:123
  71.8 1.9 %fusion.17 = f32[1,32,48,128]{3,0,2,1:T(1,128)S(1)} fusion(f32[1,32,51,128]{3,0,2,1:T(1,128)S(1)} %maximum_convert_fusion.1), kind=kLoop, calls=%fused_computation.27 | loop fusion | flops 983040 | bytes 3932160 | tf_op jit(solution)/shard_map/sub | solution.py:27
  73.8 1.7 %slice_subtract_fusion.5 = (f32[1,32,47,128]{3,0,2,1:T(1,128)S(1)}, f32[1,32,47,128]{3,0,2,1:T(1,128)S(1)}) fusion(f32[1,32,48,128]{3,0,2,1:T(1,128)S(1)} %fusion.17, f32[1,32,51,128]{3,0,2,1:T(1,128)S(1)} %maximum_convert_fusion.1), kind=kLoop, calls=%fused_computation.69 | loop fusion | flops 962560 | bytes 3850240 | tf_op jit(solution)/shard_map/sub | solution.py:37
  75.5 0.0 all-to-all-done.1
  75.5 0.0 copy-start.2
  75.5 0.5 bitcast_convert_fusion
  76.1 2.7 %fusion.38 = bf16[1,32,45,128]{3,0,2,1:T(2,128)(2,1)S(1)} fusion(f32[32,46,2,128]{3,2,1,0:T(2,128)S(1)} %bitcast_convert_fusion, f32[32,2,45,128]{3,1,2,0:T(2,128)} %param.6), kind=kLoop, calls=%fused_computation.61 | loop fusion | flops 368640 | bytes 1843200 | tf_op jit(solution)/shard_map/convert_element_type | solution.py:130
  78.8 0.0 collective-permute-done
  78.8 0.0 copy-done.2
  78.8 4.3 %compare_select_fusion.1 = f32[1,32,46,128]{3,0,2,1:T(1,128)S(1)} fusion(f32[1,32,47,128]{3,0,2,1:T(1,128)S(1)} %get-tuple-element.10, f32[1,32,47,128]{3,0,2,1:T(1,128)S(1)} %get-tuple-element.9, f32[1,32,48,128]{3,0,2,1:T(1,128)S(1)} %fusion.17, f32[32,46,2,128]{3,2,1,0:T(2,128)S(1)} %bitcast_convert_fusion, f32[1,32,1,128]{3,0,2,1:T(1,128)} %bitcast.2, ...), kind=kLoop, calls=%fused_computation.8 | loop fusion | flops 3768320 | bytes 6029312 | tf_op jit(solution)/shard_map/jit(_where)/select_n | solution.py:59
  83.1 1.7 %fusion.40 = bf16[1,32,45,128]{3,0,2,1:T(2,128)(2,1)S(1)} fusion(f32[1,32,46,128]{3,0,2,1:T(1,128)S(1)} %compare_select_fusion.1, bf16[1,32,45,128]{3,1,2,0:T(8,128)(2,1)S(1)} %copy-done.3), kind=kLoop, calls=%fused_computation.66 | loop fusion | flops 737280 | bytes 2211840 | tf_op jit(solution)/shard_map/convert_element_type | solution.py:134
  84.8 0.3 pad_maximum_fusion.5
  85.1 1.9 %collective-permute-start.3 = (bf16[2,3,45,128]{3,0,2,1:T(2,128)(2,1)S(1)}, bf16[2,3,45,128]{3,0,2,1:T(2,128)(2,1)S(1)}, u32[]{:S(2)}, u32[]{:S(2)}) collective-permute-start(bf16[2,3,45,128]{3,0,2,1:T(2,128)(2,1)S(1)} %get-tuple-element.6), channel_id=1, source_target_pairs={{32,0},{64,32},{96,64},{128,96},{160,128},{192,160},{224,192},{256... | collective-permute-start | bytes 207368 | tf_op jit(solution)/shard_map/ppermute | solution.py:17
  87.1 2.6 %collective-permute-start.4 = (bf16[2,3,45,128]{3,0,2,1:T(2,128)(2,1)S(1)}, bf16[2,3,45,128]{3,0,2,1:T(2,128)(2,1)S(1)}, u32[]{:S(2)}, u32[]{:S(2)}) collective-permute-start(bf16[2,3,45,128]{3,0,2,1:T(2,128)(2,1)S(1)} %get-tuple-element.5), channel_id=1, source_target_pairs={{0,32},{32,64},{64,96},{96,128},{128,160},{160,192},{192,224},{224... | collective-permute-start | bytes 207368 | tf_op jit(solution)/shard_map/ppermute | solution.py:16
  89.7 0.0 collective-permute-done.3
  89.7 4.2 %collective-permute-done.4 = bf16[2,3,45,128]{3,0,2,1:T(2,128)(2,1)S(1)} collective-permute-done((bf16[2,3,45,128]{3,0,2,1:T(2,128)(2,1)S(1)}, bf16[2,3,45,128]{3,0,2,1:T(2,128)(2,1)S(1)}, u32[]{:S(2)}, u32[]{:S(2)}) %collective-permute-start.4) | collective-permute-done | bytes 69152 | tf_op jit(solution)/shard_map/ppermute | solution.py:16
  93.9 3.7 %fusion.12 = f32[1,38,45,128]{3,0,2,1:T(1,128)S(1)} fusion(bf16[2,3,45,128]{3,0,2,1:T(2,128)(2,1)S(1)} %collective-permute-done.3, bf16[2,3,45,128]{3,0,2,1:T(2,128)(2,1)S(1)} %collective-permute-done.4, bf16[1,32,45,128]{3,0,2,1:T(2,128)(2,1)S(1)} %fusion.38, bf16[1,32,45,128]{3,0,2,1:T(2,128)(2,1)S(1)} %fusion.40), kind=kLoop, calls=%fused_computation.16 | loop fusion | flops 1751040 | bytes 1751040 | tf_op jit(solution)/shard_map/convert_element_type | solution.py:137
  97.6 2.6 %fusion.14 = f32[1,35,45,128]{3,0,2,1:T(1,128)S(1)} fusion(f32[1,38,45,128]{3,0,2,1:T(1,128)S(1)} %fusion.12), kind=kLoop, calls=%fused_computation.22 | loop fusion | flops 1008000 | bytes 4032000 | tf_op jit(solution)/shard_map/sub | solution.py:27
  100.2 1.8 %slice_subtract_fusion.4 = (f32[1,34,45,128]{3,0,2,1:T(1,128)S(1)}, f32[1,34,45,128]{3,0,2,1:T(1,128)S(1)}) fusion(f32[1,35,45,128]{3,0,2,1:T(1,128)S(1)} %fusion.14, f32[1,38,45,128]{3,0,2,1:T(1,128)S(1)} %fusion.12), kind=kLoop, calls=%fused_computation.68 | loop fusion | flops 979200 | bytes 3916800 | tf_op jit(solution)/shard_map/sub | solution.py:37
  101.9 6.6 %compare_select_fusion = f32[1,33,45,128]{3,0,2,1:T(1,128)S(1)} fusion(f32[1,34,45,128]{3,0,2,1:T(1,128)S(1)} %get-tuple-element.8, f32[1,34,45,128]{3,0,2,1:T(1,128)S(1)} %get-tuple-element.7, f32[1,35,45,128]{3,0,2,1:T(1,128)S(1)} %fusion.14, bf16[2,3,45,128]{3,0,2,1:T(2,128)(2,1)S(1)} %collective-permute-done.3, bf16[1,32,45,128]{3,0,2,1:T(2,128)(2,1)S(1)} %fusion.38, ...), kind=kLoop, calls=%fused_computation.7 | loop fusion | flops 4371840 | bytes 5368353 | tf_op jit(solution)/shard_map/jit(_where)/select_n | solution.py:59
  108.5 1.0 fusion.41
  109.5 0.8 copy.23
  (3 shorter events, 0.0 us)
Async XLA Ops:
  0.0 19.2 %copy-start.3 = (bf16[1,32,45,128]{3,1,2,0:T(8,128)(2,1)S(1)}, bf16[1,32,45,128]{3,1,2,0:T(8,128)(2,1)}, u32[]{:S(2)}) copy-start(bf16[1,32,45,128]{3,1,2,0:T(8,128)(2,1)} %param.5) | copy-start | bytes 1105924
  2.8 35.1 %all-to-all-start = ((bf16[32,1,45,2,128]{4,3,2,1,0:T(2,128)(2,1)}), bf16[32,1,45,2,128]{4,3,2,1,0:T(2,128)(2,1)S(1)}, u32[]{:S(2)}, u32[]{:S(2)}) async-start(bf16[32,1,45,2,128]{4,3,2,1,0:T(2,128)(2,1)} %convert_bitcast_fusion), calls=%async_computation | async-start | bytes 1474560 | tf_op jit(solution)/shard_map/all_to_all | solution.py:96
  37.9 4.2 %copy-start.1 = (bf16[32,46,1442]{2,1,0:T(8,128)(2,1)S(1)}, bf16[32,46,1442]{2,1,0:T(8,128)(2,1)}, u32[]{:S(2)}) copy-start(bf16[32,46,1442]{2,1,0:T(8,128)(2,1)} %maximum_convert_fusion) | copy-start | bytes 12735748
  42.1 17.2 %copy-start = (f32[32,2,45,128]{3,1,2,0:T(2,128)S(1)}, f32[32,2,45,128]{3,1,2,0:T(2,128)}, u32[]{:S(2)}) copy-start(f32[32,2,45,128]{3,1,2,0:T(2,128)} %param.6) | copy-start | bytes 4423684
  45.1 30.4 %all-to-all-start.1 = ((bf16[32,1,46,2,128]{4,3,2,1,0:T(2,128)(2,1)}), bf16[32,1,46,2,128]{4,3,2,1,0:T(2,128)(2,1)S(1)}, u32[]{:S(2)}, u32[]{:S(2)}) async-start(bf16[32,1,46,2,128]{4,3,2,1,0:T(2,128)(2,1)} %copy.19), calls=%async_computation.1 | async-start | bytes 1507328 | tf_op jit(solution)/shard_map/all_to_all | solution.py:110
  50.2 20.4 %collective-permute-start.1 = (bf16[1,32,3,128]{3,0,2,1:T(2,128)(2,1)S(1)}, bf16[1,32,3,128]{3,0,2,1:T(2,128)(2,1)S(1)}, u32[]{:S(2)}, u32[]{:S(2)}) collective-permute-start(bf16[1,32,3,128]{3,0,2,1:T(2,128)(2,1)S(1)} %get-tuple-element.11), channel_id=1, source_target_pairs={{0,1},{1,2},{2,3},{3,4},{4,5},{5,6},{6,7},{7,8},{8,9},{9,10},{10,1... | collective-permute-start | bytes 73736 | tf_op jit(solution)/shard_map/ppermute | solution.py:16
  53.9 16.7 %collective-permute-start.2 = (bf16[1,32,3,128]{3,0,2,1:T(2,128)(2,1)S(1)}, bf16[1,32,3,128]{3,0,2,1:T(2,128)(2,1)S(1)}, u32[]{:S(2)}, u32[]{:S(2)}) collective-permute-start(bf16[1,32,3,128]{3,0,2,1:T(2,128)(2,1)S(1)} %get-tuple-element.12), channel_id=1, source_target_pairs={{1,0},{2,1},{3,2},{4,3},{5,4},{6,5},{7,6},{8,7},{9,8},{10,9},{11,1... | collective-permute-start | bytes 73736 | tf_op jit(solution)/shard_map/ppermute | solution.py:17
  60.0 18.8 %collective-permute-start = (f32[32,1,128]{2,0,1:T(8,128)}, f32[32,1,128]{2,0,1:T(8,128)}, u32[]{:S(2)}, u32[]{:S(2)}) collective-permute-start(f32[32,1,128]{2,0,1:T(8,128)} %bitcast.1), channel_id=1, source_target_pairs={{0,31},{1,0},{2,1},{3,2},{4,3},{5,4},{6,5},{7,6},{8,7},{9,8},{10,9... | collective-permute-start | bytes 49160 | tf_op jit(solution)/shard_map/ppermute | solution.py:124
  75.5 3.3 %copy-start.2 = (f32[1,32,45,128]{3,0,2,1:T(1,128)S(1)}, f32[1,32,45,128]{3,0,2,1:T(1,128)}, u32[]{:S(2)}) copy-start(f32[1,32,45,128]{3,0,2,1:T(1,128)} %slice_bitcast_fusion.10) | copy-start | bytes 2211844
  85.1 4.6 %collective-permute-start.3 = (bf16[2,3,45,128]{3,0,2,1:T(2,128)(2,1)S(1)}, bf16[2,3,45,128]{3,0,2,1:T(2,128)(2,1)S(1)}, u32[]{:S(2)}, u32[]{:S(2)}) collective-permute-start(bf16[2,3,45,128]{3,0,2,1:T(2,128)(2,1)S(1)} %get-tuple-element.6), channel_id=1, source_target_pairs={{32,0},{64,32},{96,64},{128,96},{160,128},{192,160},{224,192},{256... | collective-permute-start | bytes 207368 | tf_op jit(solution)/shard_map/ppermute | solution.py:17
  87.1 6.8 %collective-permute-start.4 = (bf16[2,3,45,128]{3,0,2,1:T(2,128)(2,1)S(1)}, bf16[2,3,45,128]{3,0,2,1:T(2,128)(2,1)S(1)}, u32[]{:S(2)}, u32[]{:S(2)}) collective-permute-start(bf16[2,3,45,128]{3,0,2,1:T(2,128)(2,1)S(1)} %get-tuple-element.5), channel_id=1, source_target_pairs={{0,32},{32,64},{64,96},{96,128},{128,160},{160,192},{192,224},{224... | collective-permute-start | bytes 207368 | tf_op jit(solution)/shard_map/ppermute | solution.py:16

commit v9 on v5

--- a/solution.py
+++ b/solution.py
@@ -86,27 +86,31 @@
     blocks = lax.axis_size("lon")
     mode_count = row_factor.shape[1]
     per_device = 2 * row_count // blocks
+    rows_here = per_device // 2
     table, mode_weight = spectral_basis(blocks, lon_local, lon_local + 1, mode_count)
-    forward_table = spectral_basis(blocks, lon_local, lon_local, mode_count)[0].astype(jnp.bfloat16)
+    forward_table = spectral_basis(blocks, lon_local, lon_local, mode_count)[0]
+    forward_table = forward_table.reshape(blocks * lon_local, 2 * mode_count).astype(jnp.bfloat16)
+    forward_table = lax.optimization_barrier(forward_table.T)
     inverse_table = table.astype(jnp.bfloat16)
     outgoing = courant.transpose(0, 2, 1, 3).astype(jnp.bfloat16)
-    outgoing = outgoing.reshape(blocks, (2 * row_count // blocks) * lon_local, levels)
+    outgoing = outgoing.reshape(blocks, rows_here * lon_local * 2, levels)
     pair_factor = jnp.repeat(1.0 - row_factor, 2, axis=0)
     removal = jnp.concatenate([pair_factor, pair_factor], axis=1) * mode_weight[None, :]
     arrived = lax.all_to_all(outgoing, "lon", split_axis=0, concat_axis=0, tiled=True)
-    level_block = arrived.reshape(blocks, per_device // 2, lon_local, 2, levels)
+    gathered = arrived.reshape(blocks, rows_here, lon_local, 2 * levels).transpose(0, 2, 1, 3)
+    gathered = gathered.reshape(blocks * lon_local, rows_here * 2 * levels)
     first_row = lax.axis_index("lon") * per_device
     local_removal = lax.dynamic_slice_in_dim(removal, first_row, per_device, 0)
-    spectrum = jnp.einsum(
-        "drjcl,djm->rcml", level_block, forward_table, preferred_element_type=jnp.float32
-    ).reshape(per_device, 2 * mode_count, levels)
-    weighted = lax.optimization_barrier((spectrum * local_removal[:, :, None]).astype(jnp.bfloat16))
+    row_removal = local_removal.reshape(rows_here, 2, 2 * mode_count)[:, 0].T
+    spectrum = jnp.dot(forward_table, gathered, preferred_element_type=jnp.float32)
+    spectrum = spectrum.reshape(2 * mode_count, rows_here, 2 * levels)
+    weighted = (spectrum * row_removal[:, :, None]).reshape(2 * mode_count, rows_here * 2 * levels)
+    weighted = lax.optimization_barrier(weighted.astype(jnp.bfloat16))
     correction = jnp.einsum(
-        "rcml,djm->drjcl",
-        weighted.reshape(per_device // 2, 2, 2 * mode_count, levels),
-        inverse_table,
-        preferred_element_type=jnp.float32,
+        "mk,djm->djk", weighted, inverse_table, preferred_element_type=jnp.float32
     ).astype(jnp.bfloat16)
+    correction = correction.reshape(blocks, lon_local + 1, rows_here, 2 * levels)
+    correction = correction.transpose(0, 2, 1, 3)
     correction = correction.reshape(blocks, per_device * (lon_local + 1), levels)
     returned = lax.all_to_all(correction, "lon", split_axis=0, concat_axis=0, tiled=True)
     return returned.reshape(row_count, lon_local + 1, 2, levels)

time: 88.7 us -> 91.5 us (1.032)
  the two profiles are of different devices: /device:TPU:32 before, /device:TPU:38 now
where the time goes in v9:
time: 91.5 us; the launch traced here: 91 us
  starting transfers between devices  35.5 us (39%)
  other arithmetic  19.8 us (22%)
  waiting for transfers between devices  15.3 us (17%)
  local copies, waits for them, and re-layouts  14.5 us (16%)
  matrix products  5.49 us (6%)
    all_to_all x1, starting transfers between devices, filter_correction(): lax.all_to_all(outgoing, 'lon', split_axis=0, concat_axis=0, tiled=True)  13.4 us
    all_to_all x1, starting transfers between devices, filter_correction(): lax.all_to_all(correction, 'lon', split_axis=0, concat_axis=0, tiled=True)  8.97 us
    ppermute x2, waiting for transfers between devices, padded(): before = lax.ppermute(last, axis, up)  8.66 us
    another operation x2, other arithmetic  6.77 us
    transpose x1, other arithmetic, filter_correction(): forward_table = lax.optimization_barrier(forward_table.T)  5.84 us
    ppermute x2, starting transfers between devices, padded(): before = lax.ppermute(last, axis, up)  5.78 us
    ppermute x2, starting transfers between devices, padded(): after = lax.ppermute(leading, axis, down)  4.39 us
    neg x1, local copies, waits for them, and re-layouts, spectral_basis(): table = jnp.concatenate([cosine, -sine], axis=2)  4.28 us
  transfers between devices with their start and end apart: 7, of which 5 were waited for; matrix products, arithmetic and copies ran while one was open for 28% of the time, Pallas kernels for 0%

profile of v9, /device:TPU:38, one launch (start us, length us, event | category | flops | bytes accessed | tf_op | source)
XLA Modules:
  0.0 91.0 jit_solution(10223756735647998417)
XLA Ops:
  0.0 1.6 %copy.46 = bf16[32,2,45,128]{3,0,1,2:T(8,128)(2,1)S(1)} copy(f32[32,2,45,128]{3,1,2,0:T(2,128)} %param.6) | data formatting | bytes 2211840 | tf_op args[1]
  1.6 1.2 %copy.33 = bf16[32,90,128]{2,1,0:T(8,128)(2,1)} copy(bf16[32,90,128]{2,0,1:T(8,128)(2,1)S(1)} %bitcast.43) | data formatting | bytes 1474560 | tf_op jit(solution)/shard_map/reshape | solution.py:96
  2.8 13.4 %all-to-all-start = ((bf16[32,90,128]{2,1,0:T(8,128)(2,1)}), bf16[32,90,128]{2,1,0:T(8,128)(2,1)S(1)}, u32[]{:S(2)}, u32[]{:S(2)}) async-start(bf16[32,90,128]{2,1,0:T(8,128)(2,1)} %copy.33), calls=%async_computation | async-start | bytes 1572864 | tf_op jit(solution)/shard_map/all_to_all | solution.py:99
  16.2 0.6 fusion.53
  16.8 0.5 fusion.66
  17.3 3.0 %subtract_convert_fusion = (bf16[32,45,721]{2,1,0:T(8,128)(2,1)S(1)}, bf16[32,45,721]{2,1,0:T(8,128)(2,1)}) fusion(f32[45,721]{1,0:T(8,128)S(1)} %get-tuple-element.23, f32[32,721]{1,0:T(8,128)S(1)} %get-tuple-element.20, f32[45,721]{1,0:T(8,128)S(1)} %get-tuple-element.24, f32[32,721]{1,0:T(8,128)S(1)} %get-tuple-element.19), kind=kLoop, calls=%fused_computation.5 | loop fusion | flops 9344160 | bytes 4597096 | tf_op jit(solution)/shard_map/convert.4
  20.3 4.3 %neg.12 = bf16[1440,721]{1,0:T(8,128)(2,1)} reshape(bf16[32,45,721]{2,1,0:T(8,128)(2,1)} %get-tuple-element.14) | data formatting | bytes 4152960 | tf_op jit(solution)/shard_map/neg | solution.py:77
  24.6 2.4 %sub.119 = bf16[1440,721]{1,0:T(8,128)(2,1)} reshape(bf16[32,45,721]{2,1,0:T(8,128)(2,1)S(1)} %get-tuple-element.13) | data formatting | bytes 4152960 | tf_op jit(solution)/shard_map/sub | solution.py:75
  27.0 0.0 copy-start.6
  27.0 0.0 copy-start.7
  27.0 5.8 %maximum_bitcast_fusion = bf16[1442,1440]{0,1:T(8,128)(2,1)} fusion(bf16[1440,721]{1,0:T(8,128)(2,1)} %neg.12, bf16[1440,721]{1,0:T(8,128)(2,1)} %sub.119), kind=kLoop, calls=%fused_computation.8 | loop fusion | flops 8305920 | bytes 8305920 | tf_op jit(solution)/shard_map/transpose | solution.py:93
  32.9 0.0 copy-done.6
  32.9 0.0 copy-done.7
  32.9 0.0 copy-done.5
  32.9 0.1 select_subtract_fusion
  33.0 0.1 broadcast_in_dim.20
  33.1 0.1 reshape.352
  33.2 0.1 pad_maximum_fusion.7
  33.3 0.1 multiply_bitcast_fusion
  33.4 0.6 fusion.57
  34.1 3.8 %subtract_convert_fusion.1 = (bf16[32,46,721]{2,1,0:T(8,128)(2,1)}, bf16[32,46,721]{2,1,0:T(8,128)(2,1)}) fusion(f32[46,721]{1,0:T(8,128)S(1)} %get-tuple-element.21, f32[32,721]{1,0:T(8,128)S(1)} %get-tuple-element.20, f32[46,721]{1,0:T(8,128)S(1)} %get-tuple-element.22, f32[32,721]{1,0:T(8,128)S(1)} %get-tuple-element.19), kind=kLoop, calls=%fused_computation.7 | loop fusion | flops 9551808 | bytes 4695152 | tf_op jit(solution)/shard_map/convert.5
  37.8 0.8 all-to-all-done
  38.6 0.3 reshape_transpose_reshape.6
  39.0 0.0 copy-start.2
  39.0 0.0 copy-start.3
  39.0 3.9 %fusion.4 = bf16[1442,256]{1,0:T(8,128)(2,1)S(1)} fusion(bf16[1442,1440]{0,1:T(8,128)(2,1)} %maximum_bitcast_fusion, bf16[1440,256]{1,0:T(8,128)(2,1)S(1)} %reshape_transpose_reshape.6, f32[1442]{0:T(1024)S(1)} %slice_reduce_fusion), kind=kOutput, calls=%fused_computation.10 | convolution fusion | flops 1063896064 | bytes 5634312 | tf_op jit(solution)/shard_map/dot_general | solution.py:105
  42.9 0.0 copy-done.2
  42.9 0.0 copy-done.3
  42.9 0.0 copy-start.4
  42.9 0.0 copy-start
  42.9 1.6 %fusion.5 = bf16[32,46,256]{2,1,0:T(8,128)(2,1)S(1)} fusion(bf16[32,46,721]{2,1,0:T(8,128)(2,1)S(1)} %copy-done.3, bf16[32,46,721]{2,1,0:T(8,128)(2,1)S(1)} %copy-done.2, bf16[1442,256]{1,0:T(8,128)(2,1)S(1)} %fusion.4), kind=kOutput, calls=%fused_computation.17 | convolution fusion | flops 1095650816 | bytes 5737216 | tf_op jit(solution)/shard_map/mk,djm->djk/dot_general | solution.py:109
  44.5 1.1 %reshape_transpose_reshape.7 = bf16[32,92,128]{2,1,0:T(8,128)(2,1)} reshape(bf16[32,46,256]{2,1,0:T(8,128)(2,1)S(1)} %fusion.5) | data formatting | bytes 1507328 | tf_op jit(solution)/shard_map/reshape;transpose;reshape | solution.py:114
  45.7 9.0 %all-to-all-start.1 = ((bf16[32,92,128]{2,1,0:T(8,128)(2,1)}), bf16[32,92,128]{2,1,0:T(8,128)(2,1)S(1)}, u32[]{:S(2)}, u32[]{:S(2)}) async-start(bf16[32,92,128]{2,1,0:T(8,128)(2,1)} %reshape_transpose_reshape.7), calls=%async_computation.1 | async-start | bytes 1572864 | tf_op jit(solution)/shard_map/all_to_all | solution.py:115
  54.6 0.0 copy-done.4
  54.7 3.4 %collective-permute-start.1 = (bf16[1,32,3,128]{3,1,2,0:T(8,128)(2,1)S(1)}, bf16[1,32,3,128]{3,1,2,0:T(8,128)(2,1)S(1)}, u32[]{:S(2)}, u32[]{:S(2)}) collective-permute-start(bf16[1,32,3,128]{3,1,2,0:T(8,128)(2,1)S(1)} %get-tuple-element.17), channel_id=1, source_target_pairs={{0,1},{1,2},{2,3},{3,4},{4,5},{5,6},{6,7},{7,8},{8,9},{9,10},{10,1... | collective-permute-start | bytes 73736 | tf_op jit(solution)/shard_map/ppermute | solution.py:16
  58.0 2.5 %collective-permute-start.2 = (bf16[1,32,3,128]{3,1,2,0:T(8,128)(2,1)S(1)}, bf16[1,32,3,128]{3,1,2,0:T(8,128)(2,1)S(1)}, u32[]{:S(2)}, u32[]{:S(2)}) collective-permute-start(bf16[1,32,3,128]{3,1,2,0:T(8,128)(2,1)S(1)} %get-tuple-element.18), channel_id=1, source_target_pairs={{1,0},{2,1},{3,2},{4,3},{5,4},{6,5},{7,6},{8,7},{9,8},{10,9},{11,1... | collective-permute-start | bytes 73736 | tf_op jit(solution)/shard_map/ppermute | solution.py:17
  60.5 0.0 copy-done
  60.6 2.9 %collective-permute-start = (f32[32,1,128]{2,0,1:T(8,128)S(1)}, f32[32,1,128]{2,0,1:T(8,128)S(1)}, u32[]{:S(2)}, u32[]{:S(2)}) collective-permute-start(f32[32,1,128]{2,0,1:T(8,128)S(1)} %bitcast.45), channel_id=1, source_target_pairs={{0,31},{1,0},{2,1},{3,2},{4,3},{5,4},{6,5},{7,6},{8,7},{9,8},{10,9... | collective-permute-start | bytes 49160 | tf_op jit(solution)/shard_map/ppermute | solution.py:129
  63.5 2.0 %fusion.73 = (f32[32,1,45,128]{3,1,2,0:T(1,128)S(1)}, f32[32,1,45,128]{3,1,2,0:T(1,128)}) fusion(f32[32,2,45,128]{3,1,2,0:T(2,128)S(1)} %copy-done), kind=kLoop, calls=%fused_computation.128 | loop fusion | bytes 2949120 | tf_op jit(solution)/shard_map/slice | solution.py:133
  65.5 1.0 %copy.47 = f32[32,1,45,128]{3,0,2,1:T(8,128)} copy(f32[32,1,45,128]{3,1,2,0:T(1,128)S(1)} %get-tuple-element.5) | data formatting | bytes 1474560
  66.5 4.0 %collective-permute-done.1 = bf16[1,32,3,128]{3,1,2,0:T(8,128)(2,1)S(1)} collective-permute-done((bf16[1,32,3,128]{3,1,2,0:T(8,128)(2,1)S(1)}, bf16[1,32,3,128]{3,1,2,0:T(8,128)(2,1)S(1)}, u32[]{:S(2)}, u32[]{:S(2)}) %collective-permute-start.1) | collective-permute-done | bytes 24608 | tf_op jit(solution)/shard_map/ppermute | solution.py:16
  70.5 2.7 %collective-permute-done.2 = bf16[1,32,3,128]{3,1,2,0:T(8,128)(2,1)S(1)} collective-permute-done((bf16[1,32,3,128]{3,1,2,0:T(8,128)(2,1)S(1)}, bf16[1,32,3,128]{3,1,2,0:T(8,128)(2,1)S(1)}, u32[]{:S(2)}, u32[]{:S(2)}) %collective-permute-start.2) | collective-permute-done | bytes 24608 | tf_op jit(solution)/shard_map/ppermute | solution.py:17
  73.2 0.1 maximum_convert_fusion
  73.3 0.1 fusion.27
  73.5 0.2 slice_subtract_fusion.5
  73.7 3.1 %all-to-all-done.1 = bf16[32,92,128]{2,1,0:T(8,128)(2,1)S(1)} async-done(((bf16[32,92,128]{2,1,0:T(8,128)(2,1)}), bf16[32,92,128]{2,1,0:T(8,128)(2,1)S(1)}, u32[]{:S(2)}, u32[]{:S(2)}) %all-to-all-start.1) | async-done | bytes 753696 | tf_op jit(solution)/shard_map/all_to_all | solution.py:115
  76.8 0.3 copy.34
  77.1 0.2 convert.19
  77.3 0.0 copy-start.1
  77.3 0.0 collective-permute-done
  77.3 1.7 %fusion.36 = f32[1,32,46,128]{3,1,2,0:T(8,128)S(1)} fusion(f32[1,32,47,128]{3,1,2,0:T(8,128)S(1)} %get-tuple-element.10, f32[1,32,47,128]{3,1,2,0:T(8,128)S(1)} %get-tuple-element.9, f32[1,32,48,128]{3,1,2,0:T(8,128)S(1)} %fusion.27, f32[32,46,2,128]{3,0,2,1:T(8,128)S(1)} %convert.19, f32[1,32,1,128]{3,1,2,0:T(8,128)S(1)} %bitcast.44, ...), kind=kLoop, calls=%fused_computation.56 | loop fusion | flops 3768320 | bytes 6029312 | tf_op jit(solution)/shard_map/jit(_where)/select_n | solution.py:59
  79.0 0.1 fusion.45
  79.1 0.0 copy-done.1
  79.1 0.1 fusion.43
  79.2 0.1 pad_maximum_fusion.5
  79.3 1.9 %collective-permute-start.3 = (bf16[2,3,45,128]{3,1,2,0:T(4,128)(2,1)S(1)}, bf16[2,3,45,128]{3,1,2,0:T(4,128)(2,1)S(1)}, u32[]{:S(2)}, u32[]{:S(2)}) collective-permute-start(bf16[2,3,45,128]{3,1,2,0:T(4,128)(2,1)S(1)} %get-tuple-element.12), channel_id=1, source_target_pairs={{32,0},{64,32},{96,64},{128,96},{160,128},{192,160},{224,192},{256... | collective-permute-start | bytes 207368 | tf_op jit(solution)/shard_map/ppermute | solution.py:17
  81.3 2.4 %collective-permute-start.4 = (bf16[2,3,45,128]{3,1,2,0:T(4,128)(2,1)S(1)}, bf16[2,3,45,128]{3,1,2,0:T(4,128)(2,1)S(1)}, u32[]{:S(2)}, u32[]{:S(2)}) collective-permute-start(bf16[2,3,45,128]{3,1,2,0:T(4,128)(2,1)S(1)} %get-tuple-element.11), channel_id=1, source_target_pairs={{0,32},{32,64},{64,96},{96,128},{128,160},{160,192},{192,224},{224... | collective-permute-start | bytes 207368 | tf_op jit(solution)/shard_map/ppermute | solution.py:16
  83.7 0.0 collective-permute-done.3
  83.7 4.6 %collective-permute-done.4 = bf16[2,3,45,128]{3,1,2,0:T(4,128)(2,1)S(1)} collective-permute-done((bf16[2,3,45,128]{3,1,2,0:T(4,128)(2,1)S(1)}, bf16[2,3,45,128]{3,1,2,0:T(4,128)(2,1)S(1)}, u32[]{:S(2)}, u32[]{:S(2)}) %collective-permute-start.4) | collective-permute-done | bytes 69152 | tf_op jit(solution)/shard_map/ppermute | solution.py:16
  88.3 0.2 fusion.46
  88.5 0.3 fusion.19
  88.9 0.3 slice_subtract_fusion.1
  89.2 0.9 fusion.12
  90.1 0.9 %fusion.41 = bf16[1,32,45,128]{3,1,2,0:T(8,128)(2,1)} fusion(f32[1,33,45,128]{3,1,2,0:T(8,128)S(1)} %fusion.12, bf16[1,32,45,128]{3,1,2,0:T(8,128)(2,1)S(1)} %fusion.45), kind=kLoop, calls=%fused_computation.63 | loop fusion | flops 737280 | bytes 2211840 | tf_op jit(solution)/shard_map/convert_element_type | solution.py:148
  (9 shorter events, 0.1 us)
Async XLA Ops:
  2.8 35.9 %all-to-all-start = ((bf16[32,90,128]{2,1,0:T(8,128)(2,1)}), bf16[32,90,128]{2,1,0:T(8,128)(2,1)S(1)}, u32[]{:S(2)}, u32[]{:S(2)}) async-start(bf16[32,90,128]{2,1,0:T(8,128)(2,1)} %copy.33), calls=%async_computation | async-start | bytes 1572864 | tf_op jit(solution)/shard_map/all_to_all | solution.py:99
  27.0 5.8 %copy-start.6 = (s32[32]{0:T(128)S(1)}, s32[32]{0:T(128)}, u32[]{:S(2)}) copy-start(s32[32]{0:T(128)} %param.7) | copy-start | bytes 388
  27.0 5.9 %copy-start.7 = (s32[32]{0:T(128)S(1)}, s32[32]{0:T(128)}, u32[]{:S(2)}) copy-start(s32[32]{0:T(128)} %param.8) | copy-start | bytes 388
  27.0 5.9 %copy-start.5 = (f32[32,721]{1,0:T(8,128)S(1)}, f32[32,721]{1,0:T(8,128)}, u32[]{:S(2)}) copy-start(f32[32,721]{1,0:T(8,128)} %param.9) | copy-start | bytes 276868
  39.0 3.9 %copy-start.2 = (bf16[32,46,721]{2,1,0:T(8,128)(2,1)S(1)}, bf16[32,46,721]{2,1,0:T(8,128)(2,1)}, u32[]{:S(2)}) copy-start(bf16[32,46,721]{2,1,0:T(8,128)(2,1)} %get-tuple-element.15) | copy-start | bytes 6367876
  39.0 3.9 %copy-start.3 = (bf16[32,46,721]{2,1,0:T(8,128)(2,1)S(1)}, bf16[32,46,721]{2,1,0:T(8,128)(2,1)}, u32[]{:S(2)}) copy-start(bf16[32,46,721]{2,1,0:T(8,128)(2,1)} %get-tuple-element.16) | copy-start | bytes 6367876
  42.9 11.7 %copy-start.4 = (bf16[1,32,45,128]{3,1,2,0:T(8,128)(2,1)S(1)}, bf16[1,32,45,128]{3,1,2,0:T(8,128)(2,1)}, u32[]{:S(2)}) copy-start(bf16[1,32,45,128]{3,1,2,0:T(8,128)(2,1)} %param.5) | copy-start | bytes 1105924
  42.9 17.6 %copy-start = (f32[32,2,45,128]{3,1,2,0:T(2,128)S(1)}, f32[32,2,45,128]{3,1,2,0:T(2,128)}, u32[]{:S(2)}) copy-start(f32[32,2,45,128]{3,1,2,0:T(2,128)} %param.6) | copy-start | bytes 4423684
  45.7 31.1 %all-to-all-start.1 = ((bf16[32,92,128]{2,1,0:T(8,128)(2,1)}), bf16[32,92,128]{2,1,0:T(8,128)(2,1)S(1)}, u32[]{:S(2)}, u32[]{:S(2)}) async-start(bf16[32,92,128]{2,1,0:T(8,128)(2,1)} %reshape_transpose_reshape.7), calls=%async_computation.1 | async-start | bytes 1572864 | tf_op jit(solution)/shard_map/all_to_all | solution.py:115
  54.7 15.9 %collective-permute-start.1 = (bf16[1,32,3,128]{3,1,2,0:T(8,128)(2,1)S(1)}, bf16[1,32,3,128]{3,1,2,0:T(8,128)(2,1)S(1)}, u32[]{:S(2)}, u32[]{:S(2)}) collective-permute-start(bf16[1,32,3,128]{3,1,2,0:T(8,128)(2,1)S(1)} %get-tuple-element.17), channel_id=1, source_target_pairs={{0,1},{1,2},{2,3},{3,4},{4,5},{5,6},{6,7},{7,8},{8,9},{9,10},{10,1... | collective-permute-start | bytes 73736 | tf_op jit(solution)/shard_map/ppermute | solution.py:16
  58.0 15.2 %collective-permute-start.2 = (bf16[1,32,3,128]{3,1,2,0:T(8,128)(2,1)S(1)}, bf16[1,32,3,128]{3,1,2,0:T(8,128)(2,1)S(1)}, u32[]{:S(2)}, u32[]{:S(2)}) collective-permute-start(bf16[1,32,3,128]{3,1,2,0:T(8,128)(2,1)S(1)} %get-tuple-element.18), channel_id=1, source_target_pairs={{1,0},{2,1},{3,2},{4,3},{5,4},{6,5},{7,6},{8,7},{9,8},{10,9},{11,1... | collective-permute-start | bytes 73736 | tf_op jit(solution)/shard_map/ppermute | solution.py:17
  60.6 16.8 %collective-permute-start = (f32[32,1,128]{2,0,1:T(8,128)S(1)}, f32[32,1,128]{2,0,1:T(8,128)S(1)}, u32[]{:S(2)}, u32[]{:S(2)}) collective-permute-start(f32[32,1,128]{2,0,1:T(8,128)S(1)} %bitcast.45), channel_id=1, source_target_pairs={{0,31},{1,0},{2,1},{3,2},{4,3},{5,4},{6,5},{7,6},{8,7},{9,8},{10,9... | collective-permute-start | bytes 49160 | tf_op jit(solution)/shard_map/ppermute | solution.py:129
  77.3 1.8 %copy-start.1 = (f32[32,1,45,128]{3,1,2,0:T(1,128)S(1)}, f32[32,1,45,128]{3,1,2,0:T(1,128)}, u32[]{:S(2)}) copy-start(f32[32,1,45,128]{3,1,2,0:T(1,128)} %get-tuple-element.6) | copy-start | bytes 2211844
  79.3 4.4 %collective-permute-start.3 = (bf16[2,3,45,128]{3,1,2,0:T(4,128)(2,1)S(1)}, bf16[2,3,45,128]{3,1,2,0:T(4,128)(2,1)S(1)}, u32[]{:S(2)}, u32[]{:S(2)}) collective-permute-start(bf16[2,3,45,128]{3,1,2,0:T(4,128)(2,1)S(1)} %get-tuple-element.12), channel_id=1, source_target_pairs={{32,0},{64,32},{96,64},{128,96},{160,128},{192,160},{224,192},{256... | collective-permute-start | bytes 207368 | tf_op jit(solution)/shard_map/ppermute | solution.py:17
  81.3 7.1 %collective-permute-start.4 = (bf16[2,3,45,128]{3,1,2,0:T(4,128)(2,1)S(1)}, bf16[2,3,45,128]{3,1,2,0:T(4,128)(2,1)S(1)}, u32[]{:S(2)}, u32[]{:S(2)}) collective-permute-start(bf16[2,3,45,128]{3,1,2,0:T(4,128)(2,1)S(1)} %get-tuple-element.11), channel_id=1, source_target_pairs={{0,32},{32,64},{64,96},{96,128},{128,160},{160,192},{192,224},{224... | collective-permute-start | bytes 207368 | tf_op jit(solution)/shard_map/ppermute | solution.py:16

commit v10 on v0

--- a/solution.py
+++ b/solution.py
@@ -95,8 +95,16 @@
     level_block = lax.all_to_all(flattened, "lon", split_axis=0, concat_axis=1, tiled=True)
     first_row = lax.axis_index("lon") * per_device
     local_removal = lax.dynamic_slice_in_dim(removal, first_row, per_device, 0)
-    spectrum = jnp.einsum(
-        "cnl,nm->cml", level_block, forward_table, preferred_element_type=jnp.float32
+    spectrum = jnp.stack(
+        [
+            lax.dot_general(
+                forward_table,
+                level_block[c],
+                (((0,), (0,)), ((), ())),
+                preferred_element_type=jnp.float32,
+            )
+            for c in range(per_device)
+        ]
     )
     weighted = (spectrum * local_removal[:, :, None]).astype(jnp.bfloat16)
     correction = jnp.einsum(

time: 87.9 us -> 89.7 us (1.020)
  local copies, waits for them, and re-layouts: 6.87 us -> 13.3 us
  waiting for transfers between devices: 24.9 us -> 18.9 us
  matrix products: 5.61 us -> 6.96 us
    all_to_all x1, waiting for transfers between devices: 15.7 us -> 9.68 us  [filter_correction(): lax.all_to_all(flattened, 'lon', split_axis=0, concat_axis=1, tiled=True)]
    convert_element_type x0 -> x1, local copies, waits for them, and re-layouts: none -> 6.04 us  [filter_correction(): table[:, :lon_local].reshape(blocks * lon_local, 2 * mode_count)]
    dot_general x1 -> x2, matrix products: 4.17 us -> 5.38 us  [filter_correction(): lax.dot_general(forward_table, level_block[c], (((0,), (0,)), ((), ())),...]
  transfers between devices with their start and end apart: 7 -> 7, of which waited for: 4 -> 4; matrix products, arithmetic and copies ran while one was open for 12% -> 19% of each run, Pallas kernels for 0% -> 0%
where the time goes in v10:
time: 89.7 us; the launch traced here: 89.2 us
  starting transfers between devices  35.7 us (40%)
  waiting for transfers between devices  18.9 us (21%)
  other arithmetic  14 us (16%)
  local copies, waits for them, and re-layouts  13.3 us (15%)
  matrix products  6.96 us (8%)
    all_to_all x1, starting transfers between devices, filter_correction(): lax.all_to_all(flattened, 'lon', split_axis=0, concat_axis=1, tiled=True)  13.2 us
    all_to_all x1, waiting for transfers between devices, filter_correction(): lax.all_to_all(flattened, 'lon', split_axis=0, concat_axis=1, tiled=True)  9.68 us
    ppermute x2, waiting for transfers between devices, padded(): before = lax.ppermute(last, axis, up)  7.86 us
    ppermute x2, starting transfers between devices, padded(): after = lax.ppermute(leading, axis, down)  7.39 us
    ppermute x2, starting transfers between devices, padded(): before = lax.ppermute(last, axis, up)  6.1 us
    convert_element_type x1, local copies, waits for them, and re-layouts, filter_correction(): table[:, :lon_local].reshape(blocks * lon_local, 2 * mode_count)  6.04 us
    dot_general x2, matrix products, filter_correction(): lax.dot_general(forward_table, level_block[c], (((0,), (0,)), ((), ())),...  5.38 us
    all_to_all x1, starting transfers between devices, filter_correction(): lax.all_to_all(correction, 'lon', split_axis=0, concat_axis=0, tiled=True)  5.12 us
  transfers between devices with their start and end apart: 7, of which 4 were waited for; matrix products, arithmetic and copies ran while one was open for 19% of the time, Pallas kernels for 0%

profile of v10, /device:TPU:32, one launch (start us, length us, event | category | flops | bytes accessed | tf_op | source)
XLA Modules:
  0.0 89.2 jit_solution(3908405606068590993)
XLA Ops:
  0.0 1.9 %convert_element_type.154 = bf16[32,2,45,128]{3,1,2,0:T(2,128)(2,1)S(1)} convert(f32[32,2,45,128]{3,1,2,0:T(2,128)} %param.6) | non-fusion elementwise | flops 368640 | bytes 2211840 | tf_op jit(solution)/shard_map/convert_element_type | solution.py:91
  1.9 0.8 copy.40
  2.7 1.4 %copy.41 = bf16[64,45,128]{2,1,0:T(8,128)(2,1)} copy(bf16[64,45,128]{2,0,1:T(8,128)(2,1)S(1)} %bitcast.49) | data formatting | bytes 1474560 | tf_op jit(solution)/shard_map/convert_element_type | solution.py:91
  4.0 13.2 %all-to-all-start = ((bf16[64,45,128]{2,1,0:T(8,128)(2,1)}), bf16[64,45,128]{2,1,0:T(8,128)(2,1)S(1)}, u32[]{:S(2)}, u32[]{:S(2)}) async-start(bf16[64,45,128]{2,1,0:T(8,128)(2,1)} %copy.41), calls=%async_computation | async-start | bytes 1572864 | tf_op jit(solution)/shard_map/all_to_all | solution.py:95
  17.2 0.6 fusion.54
  17.9 0.5 fusion.62
  18.3 1.6 %multiply_subtract_fusion = (bf16[32,46,721]{2,1,0:T(8,128)(2,1)S(1)}, bf16[32,46,721]{2,1,0:T(8,128)(2,1)S(1)}) fusion(f32[46,721]{1,0:T(8,128)S(1)} %get-tuple-element.21, f32[32,721]{1,0:T(8,128)S(1)} %get-tuple-element.20, f32[46,721]{1,0:T(8,128)S(1)} %get-tuple-element.22, f32[32,721]{1,0:T(8,128)S(1)} %get-tuple-element.19), kind=kLoop, calls=%fused_computation.4 | loop fusion | flops 9551808 | bytes 4695152 | tf_op jit(solution)/shard_map/sub | solution.py:75
  20.0 3.9 %maximum_convert_fusion = bf16[32,46,1442]{2,1,0:T(8,128)(2,1)} fusion(bf16[32,46,721]{2,1,0:T(8,128)(2,1)S(1)} %get-tuple-element.16, bf16[32,46,721]{2,1,0:T(8,128)(2,1)S(1)} %get-tuple-element.15), kind=kLoop, calls=%fused_computation | loop fusion | flops 8490496 | bytes 8490496 | tf_op jit(solution)/shard_map/convert_element_type | solution.py:90
  23.8 0.0 copy-start.6
  23.8 6.0 %convert_element_type.153 = bf16[1440,1442]{1,0:T(8,128)(2,1)} reshape(bf16[32,45,1442]{2,1,0:T(8,128)(2,1)} %bitcast.45) | data formatting | bytes 8305920 | tf_op jit(solution)/shard_map/convert_element_type | solution.py:89
  29.9 0.0 copy-done.6
  29.9 0.0 copy-done.7
  29.9 0.0 copy-done.5
  29.9 0.1 select_subtract_fusion
  30.0 0.1 broadcast_in_dim.20
  30.1 0.1 reshape.296
  30.3 0.1 pad_maximum_fusion.7
  30.3 0.1 fusion.66
  30.4 9.7 %all-to-all-done = bf16[64,45,128]{2,1,0:T(8,128)(2,1)S(1)} async-done(((bf16[64,45,128]{2,1,0:T(8,128)(2,1)}), bf16[64,45,128]{2,1,0:T(8,128)(2,1)S(1)}, u32[]{:S(2)}, u32[]{:S(2)}) %all-to-all-start) | async-done | bytes 737312 | tf_op jit(solution)/shard_map/all_to_all | solution.py:95
  40.1 0.1 copy.56
  40.2 0.1 fusion.71
  40.2 0.1 squeeze.18
  40.3 0.1 squeeze.17
  40.5 0.0 copy-start
  40.5 0.0 copy-start.1
  40.5 3.9 %convolution_bitcast_fusion = f32[1,1442,128]{2,1,0:T(8,128)S(1)} fusion(bf16[1440,1442]{1,0:T(8,128)(2,1)} %convert_element_type.153, bf16[1440,128]{1,0:T(8,128)(2,1)S(1)} %squeeze.18), kind=kOutput, calls=%fused_computation.5 | convolution fusion | flops 531578880 | bytes 5259904 | tf_op jit(solution)/shard_map/dot_general | solution.py:100
  44.4 0.0 copy-done
  44.4 1.5 %convolution_bitcast_fusion.1 = f32[1,1442,128]{2,1,0:T(8,128)S(1)} fusion(bf16[1440,1442]{1,0:T(8,128)(2,1)S(1)} %copy-done, bf16[1440,128]{1,0:T(8,128)(2,1)S(1)} %squeeze.17), kind=kOutput, calls=%fused_computation.6 | convolution fusion | flops 531578880 | bytes 5259904 | tf_op jit(solution)/shard_map/dot_general | solution.py:100
  45.9 0.0 copy-done.1
  45.9 0.0 copy-start.4
  45.9 0.0 copy-start.2
  45.9 1.6 %fusion.6 = bf16[32,2,46,128]{3,2,1,0:T(8,128)(2,1)S(1)} fusion(bf16[32,46,1442]{2,1,0:T(8,128)(2,1)S(1)} %copy-done.1, f32[1,1442,128]{2,1,0:T(8,128)S(1)} %convolution_bitcast_fusion, f32[1,1442,128]{2,1,0:T(8,128)S(1)} %convolution_bitcast_fusion.1, f32[2,1442]{1,0:T(2,128)S(1)} %fusion.66), kind=kOutput, calls=%fused_computation.15 | convolution fusion | flops 1088267776 | bytes 6487056 | tf_op jit(solution)/shard_map/cml,djm->dcjl/dot_general | solution.py:110
  47.5 1.5 %copy.43 = bf16[32,2,46,128]{3,1,2,0:T(2,128)(2,1)} copy(bf16[32,2,46,128]{3,2,1,0:T(8,128)(2,1)S(1)} %fusion.6) | data formatting | bytes 1507328 | tf_op jit(solution)/shard_map/convert_element_type | solution.py:112
  49.0 5.1 %all-to-all-start.1 = ((bf16[32,2,46,128]{3,1,2,0:T(2,128)(2,1)}), bf16[32,2,46,128]{3,1,2,0:T(2,128)(2,1)S(1)}, u32[]{:S(2)}, u32[]{:S(2)}) async-start(bf16[32,2,46,128]{3,1,2,0:T(2,128)(2,1)} %copy.43), calls=%async_computation.1 | async-start | bytes 1507328 | tf_op jit(solution)/shard_map/all_to_all | solution.py:113
  54.1 0.0 copy-done.4
  54.1 3.7 %collective-permute-start.1 = (bf16[1,32,3,128]{3,1,2,0:T(8,128)(2,1)S(1)}, bf16[1,32,3,128]{3,1,2,0:T(8,128)(2,1)S(1)}, u32[]{:S(2)}, u32[]{:S(2)}) collective-permute-start(bf16[1,32,3,128]{3,1,2,0:T(8,128)(2,1)S(1)} %get-tuple-element.17), channel_id=1, source_target_pairs={{0,1},{1,2},{2,3},{3,4},{4,5},{5,6},{6,7},{7,8},{8,9},{9,10},{10,1... | collective-permute-start | bytes 73736 | tf_op jit(solution)/shard_map/ppermute | solution.py:16
  57.8 5.5 %collective-permute-start.2 = (bf16[1,32,3,128]{3,1,2,0:T(8,128)(2,1)S(1)}, bf16[1,32,3,128]{3,1,2,0:T(8,128)(2,1)S(1)}, u32[]{:S(2)}, u32[]{:S(2)}) collective-permute-start(bf16[1,32,3,128]{3,1,2,0:T(8,128)(2,1)S(1)} %get-tuple-element.18), channel_id=1, source_target_pairs={{1,0},{2,1},{3,2},{4,3},{5,4},{6,5},{7,6},{8,7},{9,8},{10,9},{11,1... | collective-permute-start | bytes 73736 | tf_op jit(solution)/shard_map/ppermute | solution.py:17
  63.3 0.0 copy-done.2
  63.3 4.0 %collective-permute-start = (f32[32,1,128]{2,0,1:T(8,128)S(1)}, f32[32,1,128]{2,0,1:T(8,128)S(1)}, u32[]{:S(2)}, u32[]{:S(2)}) collective-permute-start(f32[32,1,128]{2,0,1:T(8,128)S(1)} %bitcast.51), channel_id=1, source_target_pairs={{0,31},{1,0},{2,1},{3,2},{4,3},{5,4},{6,5},{7,6},{8,7},{9,8},{10,9... | collective-permute-start | bytes 49160 | tf_op jit(solution)/shard_map/ppermute | solution.py:127
  67.3 2.0 %fusion.70 = (f32[32,1,45,128]{3,1,2,0:T(1,128)S(1)}, f32[32,1,45,128]{3,1,2,0:T(1,128)}) fusion(f32[32,2,45,128]{3,1,2,0:T(2,128)S(1)} %copy-done.2), kind=kLoop, calls=%fused_computation.118 | loop fusion | bytes 2949120 | tf_op jit(solution)/shard_map/slice | solution.py:131
  69.4 1.0 %copy.57 = f32[32,1,45,128]{3,0,2,1:T(8,128)} copy(f32[32,1,45,128]{3,1,2,0:T(1,128)S(1)} %get-tuple-element.5) | data formatting | bytes 1474560
  70.3 3.2 %collective-permute-done.1 = bf16[1,32,3,128]{3,1,2,0:T(8,128)(2,1)S(1)} collective-permute-done((bf16[1,32,3,128]{3,1,2,0:T(8,128)(2,1)S(1)}, bf16[1,32,3,128]{3,1,2,0:T(8,128)(2,1)S(1)}, u32[]{:S(2)}, u32[]{:S(2)}) %collective-permute-start.1) | collective-permute-done | bytes 24608 | tf_op jit(solution)/shard_map/ppermute | solution.py:16
  73.5 0.0 collective-permute-done.2
  73.6 0.1 maximum_convert_fusion.1
  73.6 0.1 fusion.28
  73.8 0.2 slice_subtract_fusion.6
  74.0 1.3 %all-to-all-done.1 = bf16[32,2,46,128]{3,1,2,0:T(2,128)(2,1)S(1)} async-done(((bf16[32,2,46,128]{3,1,2,0:T(2,128)(2,1)}), bf16[32,2,46,128]{3,1,2,0:T(2,128)(2,1)S(1)}, u32[]{:S(2)}, u32[]{:S(2)}) %all-to-all-start.1) | async-done | bytes 753696 | tf_op jit(solution)/shard_map/all_to_all | solution.py:113
  75.3 0.2 copy_convert_fusion
  75.5 0.0 copy-start.3
  75.5 0.0 collective-permute-done
  75.5 1.7 %fusion.37 = f32[1,32,46,128]{3,1,2,0:T(8,128)S(1)} fusion(f32[1,32,47,128]{3,1,2,0:T(8,128)S(1)} %get-tuple-element.10, f32[1,32,47,128]{3,1,2,0:T(8,128)S(1)} %get-tuple-element.9, f32[1,32,48,128]{3,1,2,0:T(8,128)S(1)} %fusion.28, f32[32,2,46,128]{3,0,2,1:T(8,128)S(1)} %copy_convert_fusion, f32[1,32,1,128]{3,1,2,0:T(8,128)S(1)} %bitcast.50, ...), kind=kLoop, calls=%fused_computation.55 | loop fusion | flops 3768320 | bytes 6029312 | tf_op jit(solution)/shard_map/jit(_where)/select_n | solution.py:59
  77.2 0.1 fusion.47
  77.3 0.0 copy-done.3
  77.3 0.1 fusion.49
  77.5 0.1 pad_maximum_fusion.5
  77.5 1.9 %collective-permute-start.3 = (bf16[2,3,45,128]{3,1,2,0:T(4,128)(2,1)S(1)}, bf16[2,3,45,128]{3,1,2,0:T(4,128)(2,1)S(1)}, u32[]{:S(2)}, u32[]{:S(2)}) collective-permute-start(bf16[2,3,45,128]{3,1,2,0:T(4,128)(2,1)S(1)} %get-tuple-element.14), channel_id=1, source_target_pairs={{32,0},{64,32},{96,64},{128,96},{160,128},{192,160},{224,192},{256... | collective-permute-start | bytes 207368 | tf_op jit(solution)/shard_map/ppermute | solution.py:17
  79.5 2.4 %collective-permute-start.4 = (bf16[2,3,45,128]{3,1,2,0:T(4,128)(2,1)S(1)}, bf16[2,3,45,128]{3,1,2,0:T(4,128)(2,1)S(1)}, u32[]{:S(2)}, u32[]{:S(2)}) collective-permute-start(bf16[2,3,45,128]{3,1,2,0:T(4,128)(2,1)S(1)} %get-tuple-element.13), channel_id=1, source_target_pairs={{0,32},{32,64},{64,96},{96,128},{128,160},{160,192},{192,224},{224... | collective-permute-start | bytes 207368 | tf_op jit(solution)/shard_map/ppermute | solution.py:16
  81.9 0.0 collective-permute-done.3
  81.9 4.6 %collective-permute-done.4 = bf16[2,3,45,128]{3,1,2,0:T(4,128)(2,1)S(1)} collective-permute-done((bf16[2,3,45,128]{3,1,2,0:T(4,128)(2,1)S(1)}, bf16[2,3,45,128]{3,1,2,0:T(4,128)(2,1)S(1)}, u32[]{:S(2)}, u32[]{:S(2)}) %collective-permute-start.4) | collective-permute-done | bytes 69152 | tf_op jit(solution)/shard_map/ppermute | solution.py:16
  86.6 0.2 fusion.48
  86.7 0.3 fusion.20
  87.1 0.3 slice_subtract_fusion.1
  87.4 0.9 fusion.13
  88.3 0.9 %fusion.44 = bf16[1,32,45,128]{3,1,2,0:T(8,128)(2,1)} fusion(f32[1,33,45,128]{3,1,2,0:T(8,128)S(1)} %fusion.13, bf16[1,32,45,128]{3,1,2,0:T(8,128)(2,1)S(1)} %fusion.47), kind=kLoop, calls=%fused_computation.64 | loop fusion | flops 737280 | bytes 2211840 | tf_op jit(solution)/shard_map/convert_element_type | solution.py:146
  (9 shorter events, 0.1 us)
Async XLA Ops:
  4.0 36.1 %all-to-all-start = ((bf16[64,45,128]{2,1,0:T(8,128)(2,1)}), bf16[64,45,128]{2,1,0:T(8,128)(2,1)S(1)}, u32[]{:S(2)}, u32[]{:S(2)}) async-start(bf16[64,45,128]{2,1,0:T(8,128)(2,1)} %copy.41), calls=%async_computation | async-start | bytes 1572864 | tf_op jit(solution)/shard_map/all_to_all | solution.py:95
  23.8 6.0 %copy-start.6 = (s32[32]{0:T(128)S(1)}, s32[32]{0:T(128)}, u32[]{:S(2)}) copy-start(s32[32]{0:T(128)} %param.7) | copy-start | bytes 388
  23.8 6.1 %copy-start.7 = (s32[32]{0:T(128)S(1)}, s32[32]{0:T(128)}, u32[]{:S(2)}) copy-start(s32[32]{0:T(128)} %param.8) | copy-start | bytes 388
  23.8 6.1 %copy-start.5 = (f32[32,721]{1,0:T(8,128)S(1)}, f32[32,721]{1,0:T(8,128)}, u32[]{:S(2)}) copy-start(f32[32,721]{1,0:T(8,128)} %param.9) | copy-start | bytes 276868
  40.5 3.9 %copy-start = (bf16[1440,1442]{1,0:T(8,128)(2,1)S(1)}, bf16[1440,1442]{1,0:T(8,128)(2,1)}, u32[]{:S(2)}) copy-start(bf16[1440,1442]{1,0:T(8,128)(2,1)} %convert_element_type.153) | copy-start | bytes 12458884
  40.5 5.4 %copy-start.1 = (bf16[32,46,1442]{2,1,0:T(8,128)(2,1)S(1)}, bf16[32,46,1442]{2,1,0:T(8,128)(2,1)}, u32[]{:S(2)}) copy-start(bf16[32,46,1442]{2,1,0:T(8,128)(2,1)} %maximum_convert_fusion) | copy-start | bytes 12735748
  45.9 8.2 %copy-start.4 = (bf16[1,32,45,128]{3,1,2,0:T(8,128)(2,1)S(1)}, bf16[1,32,45,128]{3,1,2,0:T(8,128)(2,1)}, u32[]{:S(2)}) copy-start(bf16[1,32,45,128]{3,1,2,0:T(8,128)(2,1)} %param.5) | copy-start | bytes 1105924
  45.9 17.4 %copy-start.2 = (f32[32,2,45,128]{3,1,2,0:T(2,128)S(1)}, f32[32,2,45,128]{3,1,2,0:T(2,128)}, u32[]{:S(2)}) copy-start(f32[32,2,45,128]{3,1,2,0:T(2,128)} %param.6) | copy-start | bytes 4423684
  49.0 26.3 %all-to-all-start.1 = ((bf16[32,2,46,128]{3,1,2,0:T(2,128)(2,1)}), bf16[32,2,46,128]{3,1,2,0:T(2,128)(2,1)S(1)}, u32[]{:S(2)}, u32[]{:S(2)}) async-start(bf16[32,2,46,128]{3,1,2,0:T(2,128)(2,1)} %copy.43), calls=%async_computation.1 | async-start | bytes 1507328 | tf_op jit(solution)/shard_map/all_to_all | solution.py:113
  54.1 19.4 %collective-permute-start.1 = (bf16[1,32,3,128]{3,1,2,0:T(8,128)(2,1)S(1)}, bf16[1,32,3,128]{3,1,2,0:T(8,128)(2,1)S(1)}, u32[]{:S(2)}, u32[]{:S(2)}) collective-permute-start(bf16[1,32,3,128]{3,1,2,0:T(8,128)(2,1)S(1)} %get-tuple-element.17), channel_id=1, source_target_pairs={{0,1},{1,2},{2,3},{3,4},{4,5},{5,6},{6,7},{7,8},{8,9},{9,10},{10,1... | collective-permute-start | bytes 73736 | tf_op jit(solution)/shard_map/ppermute | solution.py:16
  57.8 15.7 %collective-permute-start.2 = (bf16[1,32,3,128]{3,1,2,0:T(8,128)(2,1)S(1)}, bf16[1,32,3,128]{3,1,2,0:T(8,128)(2,1)S(1)}, u32[]{:S(2)}, u32[]{:S(2)}) collective-permute-start(bf16[1,32,3,128]{3,1,2,0:T(8,128)(2,1)S(1)} %get-tuple-element.18), channel_id=1, source_target_pairs={{1,0},{2,1},{3,2},{4,3},{5,4},{6,5},{7,6},{8,7},{9,8},{10,9},{11,1... | collective-permute-start | bytes 73736 | tf_op jit(solution)/shard_map/ppermute | solution.py:17
  63.3 12.2 %collective-permute-start = (f32[32,1,128]{2,0,1:T(8,128)S(1)}, f32[32,1,128]{2,0,1:T(8,128)S(1)}, u32[]{:S(2)}, u32[]{:S(2)}) collective-permute-start(f32[32,1,128]{2,0,1:T(8,128)S(1)} %bitcast.51), channel_id=1, source_target_pairs={{0,31},{1,0},{2,1},{3,2},{4,3},{5,4},{6,5},{7,6},{8,7},{9,8},{10,9... | collective-permute-start | bytes 49160 | tf_op jit(solution)/shard_map/ppermute | solution.py:127
  75.5 1.8 %copy-start.3 = (f32[32,1,45,128]{3,1,2,0:T(1,128)S(1)}, f32[32,1,45,128]{3,1,2,0:T(1,128)}, u32[]{:S(2)}) copy-start(f32[32,1,45,128]{3,1,2,0:T(1,128)} %get-tuple-element.6) | copy-start | bytes 2211844
  77.5 4.4 %collective-permute-start.3 = (bf16[2,3,45,128]{3,1,2,0:T(4,128)(2,1)S(1)}, bf16[2,3,45,128]{3,1,2,0:T(4,128)(2,1)S(1)}, u32[]{:S(2)}, u32[]{:S(2)}) collective-permute-start(bf16[2,3,45,128]{3,1,2,0:T(4,128)(2,1)S(1)} %get-tuple-element.14), channel_id=1, source_target_pairs={{32,0},{64,32},{96,64},{128,96},{160,128},{192,160},{224,192},{256... | collective-permute-start | bytes 207368 | tf_op jit(solution)/shard_map/ppermute | solution.py:17
  79.5 7.1 %collective-permute-start.4 = (bf16[2,3,45,128]{3,1,2,0:T(4,128)(2,1)S(1)}, bf16[2,3,45,128]{3,1,2,0:T(4,128)(2,1)S(1)}, u32[]{:S(2)}, u32[]{:S(2)}) collective-permute-start(bf16[2,3,45,128]{3,1,2,0:T(4,128)(2,1)S(1)} %get-tuple-element.13), channel_id=1, source_target_pairs={{0,32},{32,64},{64,96},{96,128},{128,160},{160,192},{192,224},{224... | collective-permute-start | bytes 207368 | tf_op jit(solution)/shard_map/ppermute | solution.py:16

commit v11 on v0

--- a/solution.py
+++ b/solution.py
@@ -133,9 +133,20 @@
     meridional_faces = meridional_band[tracer_count, 3 : rows_local + 4].astype(jnp.float32)
     face_rows = lax.axis_index("lat") * rows_local + jnp.arange(rows_local + 1, dtype=jnp.int32)
     meridional_faces = jnp.where(face_rows[:, None, None] > 0, meridional_faces, 0.0)
-    return (
-        middle.astype(jnp.float32) + ppm_change(middle_wide, meridional_faces[None], 1, rows_local)
-    ).astype(jnp.bfloat16)
+    middle_f32 = middle.astype(jnp.float32)
+    faces = meridional_faces[None]
+
+    inner_faces = meridional_filtered[None].astype(jnp.float32)
+
+    def meridional_rows(low, high, wide, wide_low, row_faces, faces_low):
+        cells = wide[:, low - wide_low : high - wide_low + 6]
+        change = ppm_change(cells, row_faces[:, low - faces_low : high + 1 - faces_low], 1, high - low)
+        return (middle_f32[:, low:high] + change).astype(jnp.bfloat16)
+
+    inner = meridional_rows(3, rows_local - 3, middle_f32, 3, inner_faces, 0)
+    top = meridional_rows(0, 3, middle_wide, 0, faces, 0)
+    bottom = meridional_rows(rows_local - 3, rows_local, middle_wide, 0, faces, 0)
+    return jnp.concatenate([top, inner, bottom], axis=1)
 
 
 def solution(mesh):

time: 87.9 us -> 88.2 us (level)
    concatenate x0 -> x1, other arithmetic: none -> 0.94 us  [local(): return jnp.concatenate([top, inner, bottom], axis=1)]
    select_n x2 -> x3, other arithmetic: 2.49 us -> 2.5 us  [ppm_change(): face_flux = jnp.where(courant_faces > 0, upwind_plus, upwind_minus)]
  transfers between devices with their start and end apart: 7 -> 7, of which waited for: 4 -> 4; matrix products, arithmetic and copies ran while one was open for 12% -> 13% of each run, Pallas kernels for 0% -> 0%
where the time goes in v11:
time: 88.2 us; the launch traced here: 87.7 us
  starting transfers between devices  35.8 us (41%)
  waiting for transfers between devices  24.1 us (27%)
  other arithmetic  14.6 us (17%)
  local copies, waits for them, and re-layouts  7.32 us (8%)
  matrix products  5.62 us (6%)
    all_to_all x1, waiting for transfers between devices, filter_correction(): lax.all_to_all(flattened, 'lon', split_axis=0, concat_axis=1, tiled=True)  15.7 us
    all_to_all x1, starting transfers between devices, filter_correction(): lax.all_to_all(flattened, 'lon', split_axis=0, concat_axis=1, tiled=True)  13.2 us
    ppermute x2, starting transfers between devices, padded(): after = lax.ppermute(leading, axis, down)  7.39 us
    ppermute x2, waiting for transfers between devices, padded(): before = lax.ppermute(last, axis, up)  7.01 us
    ppermute x2, starting transfers between devices, padded(): before = lax.ppermute(last, axis, up)  6.1 us
    all_to_all x1, starting transfers between devices, filter_correction(): lax.all_to_all(correction, 'lon', split_axis=0, concat_axis=0, tiled=True)  5.13 us
    dot_general x1, matrix products, filter_correction(): jnp.einsum('cnl,nm->cml', level_block, forward_table, preferred_element_t...  4.17 us
    ppermute x1, starting transfers between devices, local(): lax.ppermute(courant[:, 0, 0:1], 'lon', [(i, (i - 1) % lon_size) for i in...  3.97 us
  transfers between devices with their start and end apart: 7, of which 4 were waited for; matrix products, arithmetic and copies ran while one was open for 13% of the time, Pallas kernels for 0%

profile of v11, /device:TPU:32, one launch (start us, length us, event | category | flops | bytes accessed | tf_op | source)
XLA Modules:
  0.0 87.7 jit_solution(5785881904785432261)
XLA Ops:
  0.0 0.0 copy-start.5
  0.0 0.0 copy-start.6
  0.0 0.0 copy-start.4
  0.0 1.9 %convert_element_type.165 = bf16[32,2,45,128]{3,1,2,0:T(2,128)(2,1)S(1)} convert(f32[32,2,45,128]{3,1,2,0:T(2,128)} %param.6) | non-fusion elementwise | flops 368640 | bytes 2211840 | tf_op jit(solution)/shard_map/convert_element_type | solution.py:91
  1.9 0.8 copy.38
  2.7 1.4 %copy.39 = bf16[64,45,128]{2,1,0:T(8,128)(2,1)} copy(bf16[64,45,128]{2,0,1:T(8,128)(2,1)S(1)} %bitcast.59) | data formatting | bytes 1474560 | tf_op jit(solution)/shard_map/convert_element_type | solution.py:91
  4.1 13.2 %all-to-all-start = ((bf16[64,45,128]{2,1,0:T(8,128)(2,1)}), bf16[64,45,128]{2,1,0:T(8,128)(2,1)S(1)}, u32[]{:S(2)}, u32[]{:S(2)}) async-start(bf16[64,45,128]{2,1,0:T(8,128)(2,1)} %copy.39), calls=%async_computation | async-start | bytes 1572864 | tf_op jit(solution)/shard_map/all_to_all | solution.py:95
  17.3 0.6 fusion.66
  18.0 0.0 copy-done.5
  18.0 0.0 copy-done.6
  18.0 0.1 pad_maximum_fusion.8
  18.1 0.0 copy-done.4
  18.1 0.1 select_subtract_fusion
  18.2 0.1 broadcast_in_dim.20
  18.3 0.1 reshape.298
  18.4 0.5 fusion.74
  18.9 1.6 %multiply_subtract_fusion = (bf16[32,46,721]{2,1,0:T(8,128)(2,1)S(1)}, bf16[32,46,721]{2,1,0:T(8,128)(2,1)S(1)}) fusion(f32[46,721]{1,0:T(8,128)S(1)} %get-tuple-element.31, f32[32,721]{1,0:T(8,128)S(1)} %get-tuple-element.30, f32[46,721]{1,0:T(8,128)S(1)} %get-tuple-element.32, f32[32,721]{1,0:T(8,128)S(1)} %get-tuple-element.29), kind=kLoop, calls=%fused_computation.6 | loop fusion | flops 9551808 | bytes 4695152 | tf_op jit(solution)/shard_map/sub | solution.py:75
  20.5 3.9 %maximum_convert_fusion = bf16[32,46,1442]{2,1,0:T(8,128)(2,1)} fusion(bf16[32,46,721]{2,1,0:T(8,128)(2,1)S(1)} %get-tuple-element.24, bf16[32,46,721]{2,1,0:T(8,128)(2,1)S(1)} %get-tuple-element.23), kind=kLoop, calls=%fused_computation | loop fusion | flops 8490496 | bytes 8490496 | tf_op jit(solution)/shard_map/convert_element_type | solution.py:90
  24.4 0.1 fusion.100
  24.5 15.7 %all-to-all-done = bf16[64,45,128]{2,1,0:T(8,128)(2,1)S(1)} async-done(((bf16[64,45,128]{2,1,0:T(8,128)(2,1)}), bf16[64,45,128]{2,1,0:T(8,128)(2,1)S(1)}, u32[]{:S(2)}, u32[]{:S(2)}) %all-to-all-start) | async-done | bytes 737312 | tf_op jit(solution)/shard_map/all_to_all | solution.py:95
  40.2 0.0 copy-start.1
  40.2 4.2 %fusion.6 = bf16[2,1442,128,1]{2,1,0,3:T(8,128)(2,1)S(1)} fusion(bf16[32,46,1442]{2,1,0:T(8,128)(2,1)} %maximum_convert_fusion, bf16[32,2,45,128]{3,2,1,0:T(8,128)(2,1)S(1)} %bitcast.60, f32[2,1442]{1,0:T(2,128)S(1)} %fusion.100), kind=kOutput, calls=%fused_computation.10 | convolution fusion | flops 1063896064 | bytes 5732368 | tf_op jit(solution)/shard_map/cnl,nm->cml/dot_general | solution.py:98
  44.4 0.0 copy-done.1
  44.4 0.0 copy-start.3
  44.4 0.0 copy-start
  44.4 1.4 %fusion.10 = bf16[32,2,46,128]{3,2,1,0:T(8,128)(2,1)S(1)} fusion(bf16[2,1442,128,1]{2,1,0,3:T(8,128)(2,1)S(1)} %fusion.6, bf16[32,46,1442]{2,1,0:T(8,128)(2,1)S(1)} %copy-done.1), kind=kOutput, calls=%fused_computation.22 | convolution fusion | flops 1087160320 | bytes 5737216 | tf_op jit(solution)/shard_map/cml,djm->dcjl/dot_general | solution.py:102
  45.9 1.5 %copy.42 = bf16[32,2,46,128]{3,1,2,0:T(2,128)(2,1)} copy(bf16[32,2,46,128]{3,2,1,0:T(8,128)(2,1)S(1)} %fusion.10) | data formatting | bytes 1507328 | tf_op jit(solution)/shard_map/convert_element_type | solution.py:104
  47.3 5.1 %all-to-all-start.1 = ((bf16[32,2,46,128]{3,1,2,0:T(2,128)(2,1)}), bf16[32,2,46,128]{3,1,2,0:T(2,128)(2,1)S(1)}, u32[]{:S(2)}, u32[]{:S(2)}) async-start(bf16[32,2,46,128]{3,1,2,0:T(2,128)(2,1)} %copy.42), calls=%async_computation.1 | async-start | bytes 1507328 | tf_op jit(solution)/shard_map/all_to_all | solution.py:105
  52.5 0.0 copy-done.3
  52.5 3.7 %collective-permute-start.1 = (bf16[1,32,3,128]{3,1,2,0:T(8,128)(2,1)S(1)}, bf16[1,32,3,128]{3,1,2,0:T(8,128)(2,1)S(1)}, u32[]{:S(2)}, u32[]{:S(2)}) collective-permute-start(bf16[1,32,3,128]{3,1,2,0:T(8,128)(2,1)S(1)} %get-tuple-element.25), channel_id=1, source_target_pairs={{0,1},{1,2},{2,3},{3,4},{4,5},{5,6},{6,7},{7,8},{8,9},{9,10},{10,1... | collective-permute-start | bytes 73736 | tf_op jit(solution)/shard_map/ppermute | solution.py:16
  56.2 5.5 %collective-permute-start.2 = (bf16[1,32,3,128]{3,1,2,0:T(8,128)(2,1)S(1)}, bf16[1,32,3,128]{3,1,2,0:T(8,128)(2,1)S(1)}, u32[]{:S(2)}, u32[]{:S(2)}) collective-permute-start(bf16[1,32,3,128]{3,1,2,0:T(8,128)(2,1)S(1)} %get-tuple-element.26), channel_id=1, source_target_pairs={{1,0},{2,1},{3,2},{4,3},{5,4},{6,5},{7,6},{8,7},{9,8},{10,9},{11,1... | collective-permute-start | bytes 73736 | tf_op jit(solution)/shard_map/ppermute | solution.py:17
  61.7 0.0 copy-done
  61.7 4.0 %collective-permute-start = (f32[32,1,128]{2,0,1:T(8,128)S(1)}, f32[32,1,128]{2,0,1:T(8,128)S(1)}, u32[]{:S(2)}, u32[]{:S(2)}) collective-permute-start(f32[32,1,128]{2,0,1:T(8,128)S(1)} %bitcast.62), channel_id=1, source_target_pairs={{0,31},{1,0},{2,1},{3,2},{4,3},{5,4},{6,5},{7,6},{8,7},{9,8},{10,9... | collective-permute-start | bytes 49160 | tf_op jit(solution)/shard_map/ppermute | solution.py:119
  65.7 2.0 %fusion.105 = (f32[32,1,45,128]{3,1,2,0:T(1,128)S(1)}, f32[32,1,45,128]{3,1,2,0:T(1,128)}) fusion(f32[32,2,45,128]{3,1,2,0:T(2,128)S(1)} %copy-done), kind=kLoop, calls=%fused_computation.168 | loop fusion | bytes 2949120 | tf_op jit(solution)/shard_map/slice | solution.py:123
  67.7 1.0 %copy.61 = f32[32,1,45,128]{3,0,2,1:T(8,128)} copy(f32[32,1,45,128]{3,1,2,0:T(1,128)S(1)} %get-tuple-element.7) | data formatting | bytes 1474560
  68.7 3.2 %collective-permute-done.1 = bf16[1,32,3,128]{3,1,2,0:T(8,128)(2,1)S(1)} collective-permute-done((bf16[1,32,3,128]{3,1,2,0:T(8,128)(2,1)S(1)}, bf16[1,32,3,128]{3,1,2,0:T(8,128)(2,1)S(1)}, u32[]{:S(2)}, u32[]{:S(2)}) %collective-permute-start.1) | collective-permute-done | bytes 24608 | tf_op jit(solution)/shard_map/ppermute | solution.py:16
  71.9 0.0 collective-permute-done.2
  71.9 0.1 maximum_convert_fusion.1
  72.0 0.1 fusion.22
  72.1 0.2 slice_subtract_fusion.5
  72.3 1.3 %all-to-all-done.1 = bf16[32,2,46,128]{3,1,2,0:T(2,128)(2,1)S(1)} async-done(((bf16[32,2,46,128]{3,1,2,0:T(2,128)(2,1)}), bf16[32,2,46,128]{3,1,2,0:T(2,128)(2,1)S(1)}, u32[]{:S(2)}, u32[]{:S(2)}) %all-to-all-start.1) | async-done | bytes 753696 | tf_op jit(solution)/shard_map/all_to_all | solution.py:105
  73.7 0.2 copy_convert_fusion
  73.9 0.0 collective-permute-done
  73.9 1.6 %fusion.33 = f32[1,32,46,128]{3,1,2,0:T(8,128)S(1)} fusion(f32[1,32,47,128]{3,1,2,0:T(8,128)S(1)} %get-tuple-element.16, f32[1,32,47,128]{3,1,2,0:T(8,128)S(1)} %get-tuple-element.15, f32[1,32,48,128]{3,1,2,0:T(8,128)S(1)} %fusion.22, f32[32,2,46,128]{3,0,2,1:T(8,128)S(1)} %copy_convert_fusion, f32[1,32,1,128]{3,1,2,0:T(8,128)S(1)} %bitcast.61, ...), kind=kLoop, calls=%fused_computation.47 | loop fusion | flops 3768320 | bytes 6029312 | tf_op jit(solution)/shard_map/jit(_where)/select_n | solution.py:59
  75.5 0.0 copy-start.2
  75.5 0.1 fusion.103
  75.6 0.3 fusion.47
  75.9 0.3 slice_subtract_fusion.6
  76.2 0.4 copy-done.2
  76.6 0.1 fusion.53
  76.7 0.1 pad_maximum_fusion.6
  76.8 1.9 %collective-permute-start.3 = (bf16[2,3,45,128]{3,1,2,0:T(4,128)(2,1)S(1)}, bf16[2,3,45,128]{3,1,2,0:T(4,128)(2,1)S(1)}, u32[]{:S(2)}, u32[]{:S(2)}) collective-permute-start(bf16[2,3,45,128]{3,1,2,0:T(4,128)(2,1)S(1)} %get-tuple-element.22), channel_id=1, source_target_pairs={{32,0},{64,32},{96,64},{128,96},{160,128},{192,160},{224,192},{256... | collective-permute-start | bytes 207368 | tf_op jit(solution)/shard_map/ppermute | solution.py:17
  78.7 2.4 %collective-permute-start.4 = (bf16[2,3,45,128]{3,1,2,0:T(4,128)(2,1)S(1)}, bf16[2,3,45,128]{3,1,2,0:T(4,128)(2,1)S(1)}, u32[]{:S(2)}, u32[]{:S(2)}) collective-permute-start(bf16[2,3,45,128]{3,1,2,0:T(4,128)(2,1)S(1)} %get-tuple-element.21), channel_id=1, source_target_pairs={{0,32},{32,64},{64,96},{96,128},{128,160},{160,192},{192,224},{224... | collective-permute-start | bytes 207368 | tf_op jit(solution)/shard_map/ppermute | solution.py:16
  81.1 0.6 fusion.42
  81.8 0.2 fusion.44
  82.0 0.0 collective-permute-done.3
  82.0 3.8 %collective-permute-done.4 = bf16[2,3,45,128]{3,1,2,0:T(4,128)(2,1)S(1)} collective-permute-done((bf16[2,3,45,128]{3,1,2,0:T(4,128)(2,1)S(1)}, bf16[2,3,45,128]{3,1,2,0:T(4,128)(2,1)S(1)}, u32[]{:S(2)}, u32[]{:S(2)}) %collective-permute-start.4) | collective-permute-done | bytes 69152 | tf_op jit(solution)/shard_map/ppermute | solution.py:16
  85.8 0.2 fusion.52
  86.0 0.1 fusion.60
  86.1 0.1 fusion.58
  86.3 0.1 convert_select_fusion
  86.4 0.3 fusion.94
  86.7 0.1 fusion.89
  86.8 0.9 %pad_maximum_fusion.5 = bf16[1,32,45,128]{3,1,2,0:T(8,128)(2,1)} fusion(bf16[1,3,45,128]{3,1,2,0:T(4,128)(2,1)S(1)} %get-tuple-element.18, bf16[1,26,45,128]{3,1,2,0:T(8,128)(2,1)S(1)} %fusion.44, bf16[1,3,45,128]{3,1,2,0:T(4,128)(2,1)S(1)} %get-tuple-element.17), kind=kLoop, calls=%fused_computation.87 | loop fusion | flops 1105920 | bytes 737280 | tf_op jit(solution)/shard_map/concatenate | solution.py:149
  (7 shorter events, 0.0 us)
Async XLA Ops:
  0.0 18.0 %copy-start.5 = (s32[32]{0:T(128)S(1)}, s32[32]{0:T(128)}, u32[]{:S(2)}) copy-start(s32[32]{0:T(128)} %param.7) | copy-start | bytes 388
  0.0 18.0 %copy-start.6 = (s32[32]{0:T(128)S(1)}, s32[32]{0:T(128)}, u32[]{:S(2)}) copy-start(s32[32]{0:T(128)} %param.8) | copy-start | bytes 388
  0.0 18.1 %copy-start.4 = (f32[32,721]{1,0:T(8,128)S(1)}, f32[32,721]{1,0:T(8,128)}, u32[]{:S(2)}) copy-start(f32[32,721]{1,0:T(8,128)} %param.9) | copy-start | bytes 276868
  4.1 36.1 %all-to-all-start = ((bf16[64,45,128]{2,1,0:T(8,128)(2,1)}), bf16[64,45,128]{2,1,0:T(8,128)(2,1)S(1)}, u32[]{:S(2)}, u32[]{:S(2)}) async-start(bf16[64,45,128]{2,1,0:T(8,128)(2,1)} %copy.39), calls=%async_computation | async-start | bytes 1572864 | tf_op jit(solution)/shard_map/all_to_all | solution.py:95
  40.2 4.2 %copy-start.1 = (bf16[32,46,1442]{2,1,0:T(8,128)(2,1)S(1)}, bf16[32,46,1442]{2,1,0:T(8,128)(2,1)}, u32[]{:S(2)}) copy-start(bf16[32,46,1442]{2,1,0:T(8,128)(2,1)} %maximum_convert_fusion) | copy-start | bytes 12735748
  44.4 8.1 %copy-start.3 = (bf16[1,32,45,128]{3,1,2,0:T(8,128)(2,1)S(1)}, bf16[1,32,45,128]{3,1,2,0:T(8,128)(2,1)}, u32[]{:S(2)}) copy-start(bf16[1,32,45,128]{3,1,2,0:T(8,128)(2,1)} %param.5) | copy-start | bytes 1105924
  44.4 17.3 %copy-start = (f32[32,2,45,128]{3,1,2,0:T(2,128)S(1)}, f32[32,2,45,128]{3,1,2,0:T(2,128)}, u32[]{:S(2)}) copy-start(f32[32,2,45,128]{3,1,2,0:T(2,128)} %param.6) | copy-start | bytes 4423684
  47.3 26.3 %all-to-all-start.1 = ((bf16[32,2,46,128]{3,1,2,0:T(2,128)(2,1)}), bf16[32,2,46,128]{3,1,2,0:T(2,128)(2,1)S(1)}, u32[]{:S(2)}, u32[]{:S(2)}) async-start(bf16[32,2,46,128]{3,1,2,0:T(2,128)(2,1)} %copy.42), calls=%async_computation.1 | async-start | bytes 1507328 | tf_op jit(solution)/shard_map/all_to_all | solution.py:105
  52.5 19.4 %collective-permute-start.1 = (bf16[1,32,3,128]{3,1,2,0:T(8,128)(2,1)S(1)}, bf16[1,32,3,128]{3,1,2,0:T(8,128)(2,1)S(1)}, u32[]{:S(2)}, u32[]{:S(2)}) collective-permute-start(bf16[1,32,3,128]{3,1,2,0:T(8,128)(2,1)S(1)} %get-tuple-element.25), channel_id=1, source_target_pairs={{0,1},{1,2},{2,3},{3,4},{4,5},{5,6},{6,7},{7,8},{8,9},{9,10},{10,1... | collective-permute-start | bytes 73736 | tf_op jit(solution)/shard_map/ppermute | solution.py:16
  56.2 15.7 %collective-permute-start.2 = (bf16[1,32,3,128]{3,1,2,0:T(8,128)(2,1)S(1)}, bf16[1,32,3,128]{3,1,2,0:T(8,128)(2,1)S(1)}, u32[]{:S(2)}, u32[]{:S(2)}) collective-permute-start(bf16[1,32,3,128]{3,1,2,0:T(8,128)(2,1)S(1)} %get-tuple-element.26), channel_id=1, source_target_pairs={{1,0},{2,1},{3,2},{4,3},{5,4},{6,5},{7,6},{8,7},{9,8},{10,9},{11,1... | collective-permute-start | bytes 73736 | tf_op jit(solution)/shard_map/ppermute | solution.py:17
  61.7 12.2 %collective-permute-start = (f32[32,1,128]{2,0,1:T(8,128)S(1)}, f32[32,1,128]{2,0,1:T(8,128)S(1)}, u32[]{:S(2)}, u32[]{:S(2)}) collective-permute-start(f32[32,1,128]{2,0,1:T(8,128)S(1)} %bitcast.62), channel_id=1, source_target_pairs={{0,31},{1,0},{2,1},{3,2},{4,3},{5,4},{6,5},{7,6},{8,7},{9,8},{10,9... | collective-permute-start | bytes 49160 | tf_op jit(solution)/shard_map/ppermute | solution.py:119
  75.5 1.1 %copy-start.2 = (f32[32,1,45,128]{3,1,2,0:T(1,128)S(1)}, f32[32,1,45,128]{3,1,2,0:T(1,128)}, u32[]{:S(2)}) copy-start(f32[32,1,45,128]{3,1,2,0:T(1,128)} %get-tuple-element.8) | copy-start | bytes 2211844
  76.8 5.2 %collective-permute-start.3 = (bf16[2,3,45,128]{3,1,2,0:T(4,128)(2,1)S(1)}, bf16[2,3,45,128]{3,1,2,0:T(4,128)(2,1)S(1)}, u32[]{:S(2)}, u32[]{:S(2)}) collective-permute-start(bf16[2,3,45,128]{3,1,2,0:T(4,128)(2,1)S(1)} %get-tuple-element.22), channel_id=1, source_target_pairs={{32,0},{64,32},{96,64},{128,96},{160,128},{192,160},{224,192},{256... | collective-permute-start | bytes 207368 | tf_op jit(solution)/shard_map/ppermute | solution.py:17
  78.7 7.1 %collective-permute-start.4 = (bf16[2,3,45,128]{3,1,2,0:T(4,128)(2,1)S(1)}, bf16[2,3,45,128]{3,1,2,0:T(4,128)(2,1)S(1)}, u32[]{:S(2)}, u32[]{:S(2)}) collective-permute-start(bf16[2,3,45,128]{3,1,2,0:T(4,128)(2,1)S(1)} %get-tuple-element.21), channel_id=1, source_target_pairs={{0,32},{32,64},{64,96},{96,128},{128,160},{160,192},{192,224},{224... | collective-permute-start | bytes 207368 | tf_op jit(solution)/shard_map/ppermute | solution.py:16

commit v12 on v0

--- a/solution.py
+++ b/solution.py
@@ -115,10 +115,16 @@
     mode_index = jnp.arange(mode_count, dtype=jnp.int32)
     damped = (row_mask[:, None] == 1) & (mode_index[None, :] >= mode_count - damped_modes[:, None])
     factor = jnp.where(damped, damping, 1.0)
-    tracer_wide = padded(tracers, (("lon", 2),), 3, True).astype(jnp.float32)
-    east_column = lax.ppermute(
-        courant[:, 0, 0:1], "lon", [(i, (i - 1) % lon_size) for i in range(lon_size)]
-    )
+    column = courant[None, :, 0, 0:1]
+    column_high = column.astype(jnp.bfloat16)
+    column_low = (column - column_high.astype(jnp.float32)).astype(jnp.bfloat16)
+    westward = jnp.concatenate([tracers[:, :, 0:3], column_high, column_low], axis=2)
+    eastward = tracers[:, :, lon_local - 3 :]
+    from_east = lax.ppermute(westward, "lon", [(i, (i - 1) % lon_size) for i in range(lon_size)])
+    from_west = lax.ppermute(eastward, "lon", [(i, (i + 1) % lon_size) for i in range(lon_size)])
+    tracer_wide = jnp.concatenate([from_west, tracers, from_east[:, :, 0:3]], axis=2)
+    tracer_wide = tracer_wide.astype(jnp.float32)
+    east_column = from_east[0, :, 3:4].astype(jnp.float32) + from_east[0, :, 4:5].astype(jnp.float32)
     correction = filter_correction(courant, factor).astype(jnp.float32)
     zonal_courant = jnp.concatenate([courant[:, 0], east_column], axis=1)
     zonal_faces = (zonal_courant - correction[:, 0]).astype(jnp.bfloat16)

time: 87.9 us -> 89.3 us (1.016)
  waiting for transfers between devices: 24.9 us -> 28.9 us
  starting transfers between devices: 35.8 us -> 31.9 us
  other arithmetic: 14 us -> 15.2 us
    ppermute x1 -> x2, waiting for transfers between devices: 0.01 us -> 7.15 us  [the longest x1 5.41 us: local(): lax.ppermute(eastward, 'lon', [(i, (i + 1) % lon_size) for i in range(lon...]
    ppermute x2 -> x1, starting transfers between devices: 7.39 us -> 1.92 us  [padded(): after = lax.ppermute(leading, axis, down)]
    ppermute x1 -> x2, starting transfers between devices: 3.97 us -> 9.15 us  [the longest x1 7.05 us: local(): lax.ppermute(westward, 'lon', [(i, (i - 1) % lon_size) for i in range(lon...]
    ppermute x2 -> x1, starting transfers between devices: 6.1 us -> 2.41 us  [padded(): before = lax.ppermute(last, axis, up)]
    ppermute x2 -> x1, waiting for transfers between devices: 7.87 us -> 4.64 us  [padded(): before = lax.ppermute(last, axis, up)]
    convert_element_type x1, other arithmetic: 0.19 us -> 1.38 us  [local(): correction = filter_correction(courant, factor).astype(jnp.float32)]
  transfers between devices with their start and end apart: 7 -> 6, of which waited for: 4 -> 5; matrix products, arithmetic and copies ran while one was open for 12% -> 12% of each run, Pallas kernels for 0% -> 0%
where the time goes in v12:
time: 89.3 us; the launch traced here: 88.8 us
  starting transfers between devices  31.9 us (36%)
  waiting for transfers between devices  28.9 us (32%)
  other arithmetic  15.2 us (17%)
  local copies, waits for them, and re-layouts  6.88 us (8%)
  matrix products  5.62 us (6%)
    all_to_all x1, waiting for transfers between devices, filter_correction(): lax.all_to_all(flattened, 'lon', split_axis=0, concat_axis=1, tiled=True)  15.7 us
    all_to_all x1, starting transfers between devices, filter_correction(): lax.all_to_all(flattened, 'lon', split_axis=0, concat_axis=1, tiled=True)  13.2 us
    ppermute x1, starting transfers between devices, local(): lax.ppermute(westward, 'lon', [(i, (i - 1) % lon_size) for i in range(lon...  7.05 us
    ppermute x1, waiting for transfers between devices, local(): lax.ppermute(eastward, 'lon', [(i, (i + 1) % lon_size) for i in range(lon...  5.41 us
    all_to_all x1, starting transfers between devices, filter_correction(): lax.all_to_all(correction, 'lon', split_axis=0, concat_axis=0, tiled=True)  5.24 us
    ppermute x1, waiting for transfers between devices, padded(): before = lax.ppermute(last, axis, up)  4.64 us
    dot_general x1, matrix products, filter_correction(): jnp.einsum('cnl,nm->cml', level_block, forward_table, preferred_element_t...  4.17 us
    convert_element_type x1, other arithmetic, filter_correction(): inverse_table = table.astype(jnp.bfloat16)  3.86 us
  transfers between devices with their start and end apart: 6, of which 5 were waited for; matrix products, arithmetic and copies ran while one was open for 12% of the time, Pallas kernels for 0%

profile of v12, /device:TPU:32, one launch (start us, length us, event | category | flops | bytes accessed | tf_op | source)
XLA Modules:
  0.0 88.8 jit_solution(18275773734781125254)
XLA Ops:
  0.0 0.0 copy-start
  0.0 0.0 copy-start.5
  0.0 0.0 copy-start.6
  0.0 0.0 copy-start.3
  0.0 0.0 copy-start.4
  0.0 2.0 %convert_element_type.208 = bf16[32,2,45,128]{3,1,2,0:T(2,128)(2,1)S(1)} convert(f32[32,2,45,128]{3,1,2,0:T(2,128)} %param.6) | non-fusion elementwise | flops 368640 | bytes 2211840 | tf_op jit(solution)/shard_map/convert_element_type | solution.py:91
  2.0 0.8 copy.38
  2.8 1.4 %copy.39 = bf16[64,45,128]{2,1,0:T(8,128)(2,1)} copy(bf16[64,45,128]{2,0,1:T(8,128)(2,1)S(1)} %bitcast.58) | data formatting | bytes 1474560 | tf_op jit(solution)/shard_map/convert_element_type | solution.py:91
  4.2 13.2 %all-to-all-start = ((bf16[64,45,128]{2,1,0:T(8,128)(2,1)}), bf16[64,45,128]{2,1,0:T(8,128)(2,1)S(1)}, u32[]{:S(2)}, u32[]{:S(2)}) async-start(bf16[64,45,128]{2,1,0:T(8,128)(2,1)} %copy.39), calls=%async_computation | async-start | bytes 1572864 | tf_op jit(solution)/shard_map/all_to_all | solution.py:95
  17.4 0.6 fusion.57
  18.0 0.0 copy-done.5
  18.1 0.0 copy-done.6
  18.1 0.1 pad_maximum_fusion.8
  18.2 0.0 copy-done.3
  18.2 0.0 copy-done.4
  18.2 0.1 select_subtract_fusion
  18.3 0.0 copy-done
  18.3 0.1 broadcast_in_dim.20
  18.4 0.1 reshape.350
  18.5 0.5 fusion.65
  19.0 1.6 %multiply_subtract_fusion = (bf16[32,46,721]{2,1,0:T(8,128)(2,1)S(1)}, bf16[32,46,721]{2,1,0:T(8,128)(2,1)S(1)}) fusion(f32[46,721]{1,0:T(8,128)S(1)} %get-tuple-element.21, f32[32,721]{1,0:T(8,128)S(1)} %get-tuple-element.20, f32[46,721]{1,0:T(8,128)S(1)} %get-tuple-element.22, f32[32,721]{1,0:T(8,128)S(1)} %get-tuple-element.19), kind=kLoop, calls=%fused_computation.6 | loop fusion | flops 9551808 | bytes 4695152 | tf_op jit(solution)/shard_map/sub | solution.py:75
  20.7 3.9 %maximum_convert_fusion = bf16[32,46,1442]{2,1,0:T(8,128)(2,1)} fusion(bf16[32,46,721]{2,1,0:T(8,128)(2,1)S(1)} %get-tuple-element.16, bf16[32,46,721]{2,1,0:T(8,128)(2,1)S(1)} %get-tuple-element.15), kind=kLoop, calls=%fused_computation | loop fusion | flops 8490496 | bytes 8490496 | tf_op jit(solution)/shard_map/convert_element_type | solution.py:90
  24.5 0.1 fusion.69
  24.6 15.7 %all-to-all-done = bf16[64,45,128]{2,1,0:T(8,128)(2,1)S(1)} async-done(((bf16[64,45,128]{2,1,0:T(8,128)(2,1)}), bf16[64,45,128]{2,1,0:T(8,128)(2,1)S(1)}, u32[]{:S(2)}, u32[]{:S(2)}) %all-to-all-start) | async-done | bytes 737312 | tf_op jit(solution)/shard_map/all_to_all | solution.py:95
  40.3 0.0 copy-start.1
  40.3 4.2 %fusion.6 = bf16[2,1442,128,1]{2,1,0,3:T(8,128)(2,1)S(1)} fusion(bf16[32,46,1442]{2,1,0:T(8,128)(2,1)} %maximum_convert_fusion, bf16[32,2,45,128]{3,2,1,0:T(8,128)(2,1)S(1)} %bitcast.59, f32[2,1442]{1,0:T(2,128)S(1)} %fusion.69), kind=kOutput, calls=%fused_computation.10 | convolution fusion | flops 1063896064 | bytes 5732368 | tf_op jit(solution)/shard_map/cnl,nm->cml/dot_general | solution.py:98
  44.5 0.0 copy-done.1
  44.5 1.4 %fusion.10 = bf16[32,2,46,128]{3,2,1,0:T(8,128)(2,1)S(1)} fusion(bf16[2,1442,128,1]{2,1,0,3:T(8,128)(2,1)S(1)} %fusion.6, bf16[32,46,1442]{2,1,0:T(8,128)(2,1)S(1)} %copy-done.1), kind=kOutput, calls=%fused_computation.17 | convolution fusion | flops 1087160320 | bytes 5737216 | tf_op jit(solution)/shard_map/cml,djm->dcjl/dot_general | solution.py:102
  45.9 1.5 %copy.42 = bf16[32,2,46,128]{3,1,2,0:T(2,128)(2,1)} copy(bf16[32,2,46,128]{3,2,1,0:T(8,128)(2,1)S(1)} %fusion.10) | data formatting | bytes 1507328 | tf_op jit(solution)/shard_map/convert_element_type | solution.py:104
  47.4 5.2 %all-to-all-start.1 = ((bf16[32,2,46,128]{3,1,2,0:T(2,128)(2,1)}), bf16[32,2,46,128]{3,1,2,0:T(2,128)(2,1)}, u32[]{:S(2)}, u32[]{:S(2)}) async-start(bf16[32,2,46,128]{3,1,2,0:T(2,128)(2,1)} %copy.42), calls=%async_computation.1 | async-start | bytes 1507328 | tf_op jit(solution)/shard_map/all_to_all | solution.py:105
  52.7 7.0 %collective-permute-start = (bf16[1,32,5,128]{3,1,2,0:T(8,128)(2,1)S(1)}, bf16[1,32,5,128]{3,1,2,0:T(8,128)(2,1)S(1)}, u32[]{:S(2)}, u32[]{:S(2)}) collective-permute-start(bf16[1,32,5,128]{3,1,2,0:T(8,128)(2,1)S(1)} %pad_maximum_fusion.7), channel_id=1, source_target_pairs={{0,31},{1,0},{2,1},{3,2},{4,3},{5,4},{6,5},{7,6},{8,7},{9,8},{10,9... | collective-permute-start | bytes 122888 | tf_op jit(solution)/shard_map/ppermute | solution.py:123
  59.7 2.1 %collective-permute-start.1 = (bf16[1,32,3,128]{3,1,2,0:T(8,128)(2,1)S(1)}, bf16[1,32,3,128]{3,1,2,0:T(8,128)(2,1)S(1)}, u32[]{:S(2)}, u32[]{:S(2)}) collective-permute-start(bf16[1,32,3,128]{3,1,2,0:T(8,128)(2,1)S(1)} %get-tuple-element.17), channel_id=1, source_target_pairs={{0,1},{1,2},{2,3},{3,4},{4,5},{5,6},{6,7},{7,8},{8,9},{9,10},{10,1... | collective-permute-start | bytes 73736 | tf_op jit(solution)/shard_map/ppermute | solution.py:124
  61.8 2.0 %fusion.72 = (f32[32,1,45,128]{3,1,2,0:T(1,128)S(1)}, f32[32,1,45,128]{3,1,2,0:T(1,128)}) fusion(f32[32,2,45,128]{3,1,2,0:T(2,128)S(1)} %copy-done), kind=kLoop, calls=%fused_computation.121 | loop fusion | bytes 2949120 | tf_op jit(solution)/shard_map/slice | solution.py:129
  63.9 1.0 %copy.61 = f32[32,1,45,128]{3,0,2,1:T(8,128)} copy(f32[32,1,45,128]{3,1,2,0:T(1,128)S(1)} %get-tuple-element.7) | data formatting | bytes 1474560
  64.8 1.7 %collective-permute-done = bf16[1,32,5,128]{3,1,2,0:T(8,128)(2,1)S(1)} collective-permute-done((bf16[1,32,5,128]{3,1,2,0:T(8,128)(2,1)S(1)}, bf16[1,32,5,128]{3,1,2,0:T(8,128)(2,1)S(1)}, u32[]{:S(2)}, u32[]{:S(2)}) %collective-permute-start) | collective-permute-done | bytes 40992 | tf_op jit(solution)/shard_map/ppermute | solution.py:123
  66.6 5.4 %collective-permute-done.1 = bf16[1,32,3,128]{3,1,2,0:T(8,128)(2,1)S(1)} collective-permute-done((bf16[1,32,3,128]{3,1,2,0:T(8,128)(2,1)S(1)}, bf16[1,32,3,128]{3,1,2,0:T(8,128)(2,1)S(1)}, u32[]{:S(2)}, u32[]{:S(2)}) %collective-permute-start.1) | collective-permute-done | bytes 24608 | tf_op jit(solution)/shard_map/ppermute | solution.py:124
  72.0 0.1 maximum_convert_fusion.1
  72.1 0.1 fusion.32
  72.2 0.2 slice_subtract_fusion.6
  72.4 1.4 %all-to-all-done.1 = bf16[32,2,46,128]{3,1,2,0:T(2,128)(2,1)} async-done(((bf16[32,2,46,128]{3,1,2,0:T(2,128)(2,1)}), bf16[32,2,46,128]{3,1,2,0:T(2,128)(2,1)}, u32[]{:S(2)}, u32[]{:S(2)}) %all-to-all-start.1) | async-done | bytes 753696 | tf_op jit(solution)/shard_map/all_to_all | solution.py:105
  73.9 0.0 copy-start.2
  73.9 1.4 %copy_convert_fusion = f32[32,2,46,128]{3,0,2,1:T(8,128)S(1)} fusion(bf16[32,2,46,128]{3,1,2,0:T(2,128)(2,1)} %all-to-all-done.1), kind=kLoop, calls=%fused_computation.62 | loop fusion | flops 376832 | bytes 2260992 | tf_op jit(solution)/shard_map/convert_element_type | solution.py:128
  75.2 1.6 %fusion.43 = f32[1,32,46,128]{3,1,2,0:T(8,128)S(1)} fusion(f32[1,32,47,128]{3,1,2,0:T(8,128)S(1)} %get-tuple-element.12, f32[1,32,47,128]{3,1,2,0:T(8,128)S(1)} %get-tuple-element.11, f32[1,32,48,128]{3,1,2,0:T(8,128)S(1)} %fusion.32, f32[32,2,46,128]{3,0,2,1:T(8,128)S(1)} %copy_convert_fusion, f32[1,32,1,128]{3,1,2,0:T(8,128)S(1)} %convert_add_fusion, ...), kind=kLoop, calls=%fused_computation.58 | loop fusion | flops 3768320 | bytes 6029312 | tf_op jit(solution)/shard_map/jit(_where)/select_n | solution.py:59
  76.8 0.1 fusion.50
  77.0 0.0 copy-done.2
  77.0 0.1 fusion.52
  77.1 0.1 pad_maximum_fusion.5
  77.2 1.9 %collective-permute-start.2 = (bf16[2,3,45,128]{3,1,2,0:T(4,128)(2,1)S(1)}, bf16[2,3,45,128]{3,1,2,0:T(4,128)(2,1)S(1)}, u32[]{:S(2)}, u32[]{:S(2)}) collective-permute-start(bf16[2,3,45,128]{3,1,2,0:T(4,128)(2,1)S(1)} %get-tuple-element.14), channel_id=1, source_target_pairs={{32,0},{64,32},{96,64},{128,96},{160,128},{192,160},{224,192},{256... | collective-permute-start | bytes 207368 | tf_op jit(solution)/shard_map/ppermute | solution.py:17
  79.1 2.4 %collective-permute-start.3 = (bf16[2,3,45,128]{3,1,2,0:T(4,128)(2,1)S(1)}, bf16[2,3,45,128]{3,1,2,0:T(4,128)(2,1)S(1)}, u32[]{:S(2)}, u32[]{:S(2)}) collective-permute-start(bf16[2,3,45,128]{3,1,2,0:T(4,128)(2,1)S(1)} %get-tuple-element.13), channel_id=1, source_target_pairs={{0,32},{32,64},{64,96},{96,128},{128,160},{160,192},{192,224},{224... | collective-permute-start | bytes 207368 | tf_op jit(solution)/shard_map/ppermute | solution.py:16
  81.5 0.0 collective-permute-done.2
  81.6 4.6 %collective-permute-done.3 = bf16[2,3,45,128]{3,1,2,0:T(4,128)(2,1)S(1)} collective-permute-done((bf16[2,3,45,128]{3,1,2,0:T(4,128)(2,1)S(1)}, bf16[2,3,45,128]{3,1,2,0:T(4,128)(2,1)S(1)}, u32[]{:S(2)}, u32[]{:S(2)}) %collective-permute-start.3) | collective-permute-done | bytes 69152 | tf_op jit(solution)/shard_map/ppermute | solution.py:16
  86.2 0.2 fusion.51
  86.4 0.3 fusion.24
  86.7 0.3 slice_subtract_fusion.1
  87.0 0.9 fusion.17
  87.9 0.9 %fusion.47 = bf16[1,32,45,128]{3,1,2,0:T(8,128)(2,1)} fusion(f32[1,33,45,128]{3,1,2,0:T(8,128)S(1)} %fusion.17, bf16[1,32,45,128]{3,1,2,0:T(8,128)(2,1)S(1)} %fusion.50), kind=kLoop, calls=%fused_computation.65 | loop fusion | flops 737280 | bytes 2211840 | tf_op jit(solution)/shard_map/convert_element_type | solution.py:144
  (11 shorter events, 0.1 us)
Async XLA Ops:
  0.0 18.3 %copy-start = (f32[32,2,45,128]{3,1,2,0:T(2,128)S(1)}, f32[32,2,45,128]{3,1,2,0:T(2,128)}, u32[]{:S(2)}) copy-start(f32[32,2,45,128]{3,1,2,0:T(2,128)} %param.6) | copy-start | bytes 4423684
  0.0 18.0 %copy-start.5 = (s32[32]{0:T(128)S(1)}, s32[32]{0:T(128)}, u32[]{:S(2)}) copy-start(s32[32]{0:T(128)} %param.7) | copy-start | bytes 388
  0.0 18.1 %copy-start.6 = (s32[32]{0:T(128)S(1)}, s32[32]{0:T(128)}, u32[]{:S(2)}) copy-start(s32[32]{0:T(128)} %param.8) | copy-start | bytes 388
  0.0 18.2 %copy-start.3 = (bf16[1,32,45,128]{3,1,2,0:T(8,128)(2,1)S(1)}, bf16[1,32,45,128]{3,1,2,0:T(8,128)(2,1)}, u32[]{:S(2)}) copy-start(bf16[1,32,45,128]{3,1,2,0:T(8,128)(2,1)} %param.5) | copy-start | bytes 1105924
  0.0 18.2 %copy-start.4 = (f32[32,721]{1,0:T(8,128)S(1)}, f32[32,721]{1,0:T(8,128)}, u32[]{:S(2)}) copy-start(f32[32,721]{1,0:T(8,128)} %param.9) | copy-start | bytes 276868
  4.2 36.1 %all-to-all-start = ((bf16[64,45,128]{2,1,0:T(8,128)(2,1)}), bf16[64,45,128]{2,1,0:T(8,128)(2,1)S(1)}, u32[]{:S(2)}, u32[]{:S(2)}) async-start(bf16[64,45,128]{2,1,0:T(8,128)(2,1)} %copy.39), calls=%async_computation | async-start | bytes 1572864 | tf_op jit(solution)/shard_map/all_to_all | solution.py:95
  40.3 4.2 %copy-start.1 = (bf16[32,46,1442]{2,1,0:T(8,128)(2,1)S(1)}, bf16[32,46,1442]{2,1,0:T(8,128)(2,1)}, u32[]{:S(2)}) copy-start(bf16[32,46,1442]{2,1,0:T(8,128)(2,1)} %maximum_convert_fusion) | copy-start | bytes 12735748
  47.4 26.4 %all-to-all-start.1 = ((bf16[32,2,46,128]{3,1,2,0:T(2,128)(2,1)}), bf16[32,2,46,128]{3,1,2,0:T(2,128)(2,1)}, u32[]{:S(2)}, u32[]{:S(2)}) async-start(bf16[32,2,46,128]{3,1,2,0:T(2,128)(2,1)} %copy.42), calls=%async_computation.1 | async-start | bytes 1507328 | tf_op jit(solution)/shard_map/all_to_all | solution.py:105
  52.7 13.9 %collective-permute-start = (bf16[1,32,5,128]{3,1,2,0:T(8,128)(2,1)S(1)}, bf16[1,32,5,128]{3,1,2,0:T(8,128)(2,1)S(1)}, u32[]{:S(2)}, u32[]{:S(2)}) collective-permute-start(bf16[1,32,5,128]{3,1,2,0:T(8,128)(2,1)S(1)} %pad_maximum_fusion.7), channel_id=1, source_target_pairs={{0,31},{1,0},{2,1},{3,2},{4,3},{5,4},{6,5},{7,6},{8,7},{9,8},{10,9... | collective-permute-start | bytes 122888 | tf_op jit(solution)/shard_map/ppermute | solution.py:123
  59.7 12.2 %collective-permute-start.1 = (bf16[1,32,3,128]{3,1,2,0:T(8,128)(2,1)S(1)}, bf16[1,32,3,128]{3,1,2,0:T(8,128)(2,1)S(1)}, u32[]{:S(2)}, u32[]{:S(2)}) collective-permute-start(bf16[1,32,3,128]{3,1,2,0:T(8,128)(2,1)S(1)} %get-tuple-element.17), channel_id=1, source_target_pairs={{0,1},{1,2},{2,3},{3,4},{4,5},{5,6},{6,7},{7,8},{8,9},{9,10},{10,1... | collective-permute-start | bytes 73736 | tf_op jit(solution)/shard_map/ppermute | solution.py:124
  73.9 3.1 %copy-start.2 = (f32[32,1,45,128]{3,1,2,0:T(1,128)S(1)}, f32[32,1,45,128]{3,1,2,0:T(1,128)}, u32[]{:S(2)}) copy-start(f32[32,1,45,128]{3,1,2,0:T(1,128)} %get-tuple-element.8) | copy-start | bytes 2211844
  77.2 4.4 %collective-permute-start.2 = (bf16[2,3,45,128]{3,1,2,0:T(4,128)(2,1)S(1)}, bf16[2,3,45,128]{3,1,2,0:T(4,128)(2,1)S(1)}, u32[]{:S(2)}, u32[]{:S(2)}) collective-permute-start(bf16[2,3,45,128]{3,1,2,0:T(4,128)(2,1)S(1)} %get-tuple-element.14), channel_id=1, source_target_pairs={{32,0},{64,32},{96,64},{128,96},{160,128},{192,160},{224,192},{256... | collective-permute-start | bytes 207368 | tf_op jit(solution)/shard_map/ppermute | solution.py:17
  79.1 7.1 %collective-permute-start.3 = (bf16[2,3,45,128]{3,1,2,0:T(4,128)(2,1)S(1)}, bf16[2,3,45,128]{3,1,2,0:T(4,128)(2,1)S(1)}, u32[]{:S(2)}, u32[]{:S(2)}) collective-permute-start(bf16[2,3,45,128]{3,1,2,0:T(4,128)(2,1)S(1)} %get-tuple-element.13), channel_id=1, source_target_pairs={{0,32},{32,64},{64,96},{96,128},{128,160},{160,192},{192,224},{224... | collective-permute-start | bytes 207368 | tf_op jit(solution)/shard_map/ppermute | solution.py:16
